TPU v7x, 512 devices: a whole 4x8x8 slice. The times are simulated.
512 devices in a mesh: seq: 128 (over y, z, core), kvh: 4 (over x).
Axes of the slice: x: 4, y: 8, z: 8, core: 2. Of those that a mesh axis runs over, the one named last changes fastest.
Arguments:
- queries: bfloat16 [8192, 64, 128], P('seq', 'kvh'), may hold values from -15 to 15
- stretch_kv: bfloat16 [2, 8192, 8, 128], P(None, 'seq', 'kvh'), may hold values from -15 to 15
- cache_kv: bfloat16 [2, 128, 2048, 8, 128], P(None, 'seq', None, 'kvh'), may hold values from -15 to 15
- selection: int32 [8, 8192, 3], P('kvh', 'seq'), may hold values from 0 to 127, all different within a row; in each aligned block of 64 rows (0 to 63, 64 to 127, ..., all dimensions but the last counted through in order) at most 2 rows name the same one
- block_owner: int32 [128], replicated, may hold values from 0 to 127, each once
Outputs:
- attended: bfloat16 [8192, 8192], P(('seq', 'kvh'))
Inputs may be any that keep to these rules, and one draw needn't show every extreme that they name: `selection`: each KV head and token names 3 different blocks. Among the 64 tokens of one index of seq, for one KV head, no block is named more than 2 times, and some block is named exactly 2 times. `block_owner`: A permutation: each storage position holds exactly one block.
All inputs are finite; a program needn't handle non-finite values.
Results may differ from a plain program's by a relative error of at most 0.0051.
Values may be sent and summed in bfloat16 or wider, within the bound.
No kernel may reach another device: no remote copies, remote signals or barrier semaphores. Data moves between devices by JAX's collectives and lax.ppermute only.
A program may use at most 128 MiB of HBM per device.

v0:
```python
import functools
import math

import jax
import jax.numpy as jnp
from jax import lax
from jax.experimental import pallas as pl
from jax.sharding import PartitionSpec as P

BLOCK_TOKENS = 2048
BLOCK_PICK_LIMIT = 2
WINDOW_SHIFTS = (8, 4, 16, 2, 1)


def shifted(value, axis, steps):
    count = lax.axis_size(axis)
    initial, last = (max(0, -steps), min(count, count - steps))
    return lax.ppermute(value, axis, [(source, source + steps) for source in range(initial, last)])


def gather_window(stretch_kv, span_devices):
    stack = stretch_kv[None]
    offsets = [0]
    for step in WINDOW_SHIFTS:
        if len(offsets) >= span_devices:
            break
        stack = jnp.concatenate([stack, shifted(stack, "seq", step)], axis=0)
        offsets = offsets + [o + step for o in offsets]
    return stack, offsets


def attend_kernel(masked, scaling, group_size, *refs):
    if masked:
        thr_ref, q_ref, k_ref, v_ref, o_ref, lse_ref = refs
    else:
        q_ref, k_ref, v_ref, o_ref, lse_ref = refs
    q = q_ref[...]
    q = q.reshape(-1, q.shape[-1])
    scores = (
        lax.dot_general(
            q, k_ref[...], (((1,), (1,)), ((), ())), preferred_element_type=jnp.float32
        )
        * scaling
    )
    if masked:
        token = lax.broadcasted_iota(jnp.int32, (scores.shape[0], 1), 0) // group_size
        scores = jnp.where(token >= thr_ref[...], scores, -jnp.inf)
    highest = jnp.max(scores, axis=1, keepdims=True)
    raw_weights = jnp.exp(scores - highest)
    weight_sum = jnp.sum(raw_weights, axis=1, keepdims=True)
    blended = (
        jnp.dot(raw_weights.astype(jnp.bfloat16), v_ref[...], preferred_element_type=jnp.float32)
        / weight_sum
    )
    o_ref[...] = blended.astype(o_ref.dtype).reshape(o_ref.shape)
    lse_ref[...] = highest + jnp.log(weight_sum)


def attend(q, q_block, q_map, heads, tiles, keys, values, out_dtype, scaling, group_size, thr=None):
    rows = q_block[0] * q_block[-2] if len(q_block) == 4 else q_block[-2]
    total_rows = rows * tiles
    key_count, head_dim = keys.shape[1], keys.shape[2]
    kv_spec = pl.BlockSpec((None, key_count, head_dim), lambda h, i: (h, 0, 0))
    in_specs = [pl.BlockSpec(q_block, q_map), kv_spec, kv_spec]
    operands = [q, keys, values]
    if thr is not None:
        in_specs = [pl.BlockSpec((1, key_count), lambda h, i: (0, 0))] + in_specs
        operands = [thr] + operands
    cost = pl.CostEstimate(
        flops=4 * heads * total_rows * key_count * head_dim,
        transcendentals=heads * total_rows * key_count,
        bytes_accessed=2 * (2 * heads * total_rows * head_dim + 2 * heads * key_count * head_dim),
    )
    return pl.pallas_call(
        functools.partial(attend_kernel, thr is not None, scaling, group_size),
        grid=(heads, tiles),
        in_specs=in_specs,
        out_specs=[
            pl.BlockSpec(q_block, q_map),
            pl.BlockSpec((None, rows, 1), lambda h, i: (h, i, 0)),
        ],
        out_shape=[
            jax.ShapeDtypeStruct(q.shape, out_dtype),
            jax.ShapeDtypeStruct((heads, total_rows, 1), jnp.float32),
        ],
        cost_estimate=cost,
    )(*operands)


def per_device(queries, stretch_kv, cache_kv, selection, block_owner):
    rows_local, query_heads, head_dim = queries.shape
    kv_heads = stretch_kv.shape[2]
    group_size = query_heads // kv_heads
    top_count = selection.shape[2]
    scaling = 1.0 / math.sqrt(head_dim)
    seq_count = lax.axis_size("seq")
    capacity = BLOCK_PICK_LIMIT
    span_devices = min(BLOCK_TOKENS // rows_local, seq_count)
    seq_place = lax.axis_index("seq")
    grouped = queries.reshape(rows_local, kv_heads, group_size, head_dim)
    requests = rows_local * top_count
    targets = block_owner[selection].reshape(kv_heads, requests)
    matches = (targets[:, :, None] == jnp.arange(seq_count, dtype=jnp.int32)[None, None, :]).astype(
        jnp.int32
    )
    places = jnp.sum((jnp.cumsum(matches, axis=1) - 1) * matches, axis=2)
    slots = targets * capacity + places
    one_hot = (
        (slots[:, None, :] == jnp.arange(seq_count * capacity, dtype=jnp.int32)[None, :, None])
        .astype(jnp.bfloat16)
        .reshape(kv_heads, seq_count, capacity, requests)
    )
    requested = jnp.repeat(jnp.swapaxes(grouped, 0, 1), top_count, axis=1).reshape(
        kv_heads, requests, group_size * head_dim
    )
    outgoing = jnp.einsum(
        "htcr,hrx->thcx", one_hot, requested, preferred_element_type=jnp.float32
    ).astype(jnp.bfloat16)
    slab = capacity * group_size
    outgoing = outgoing.reshape(seq_count, kv_heads, slab, head_dim)
    arrived = lax.all_to_all(outgoing, "seq", split_axis=0, concat_axis=0, tiled=True)
    cache_keys = jnp.swapaxes(cache_kv[0, 0], 0, 1)
    cache_values = jnp.swapaxes(cache_kv[1, 0], 0, 1)
    sources_per_tile = 32
    served, served_lse = attend(
        arrived,
        (sources_per_tile, None, slab, head_dim),
        lambda h, i: (i, h, 0, 0),
        kv_heads,
        seq_count // sources_per_tile,
        cache_keys,
        cache_values,
        jnp.bfloat16,
        scaling,
        group_size,
    )
    served_lse = jnp.swapaxes(served_lse.reshape(kv_heads, seq_count, slab), 0, 1)
    answers = lax.all_to_all(served, "seq", split_axis=0, concat_axis=0, tiled=True)
    answer_lse = lax.all_to_all(served_lse, "seq", split_axis=0, concat_axis=0, tiled=True)
    answers = answers.reshape(seq_count, kv_heads, capacity, group_size * head_dim)
    answer_lse = answer_lse.reshape(seq_count, kv_heads, capacity, group_size)
    window, offsets = gather_window(stretch_kv, span_devices)
    blocks = window.shape[0]
    window_keys = jnp.transpose(window[:, 0], (2, 0, 1, 3)).reshape(kv_heads, blocks * rows_local, head_dim)
    window_values = jnp.transpose(window[:, 1], (2, 0, 1, 3)).reshape(kv_heads, blocks * rows_local, head_dim)
    key_index = jnp.arange(blocks * rows_local, dtype=jnp.int32)
    key_offset = jnp.asarray(offsets, jnp.int32)[key_index // rows_local]
    threshold = jnp.where(
        seq_place - key_offset >= 0,
        jnp.where(key_offset == 0, key_index % rows_local, 0),
        rows_local,
    )[None, :]
    window_queries = jnp.swapaxes(grouped, 0, 1).reshape(kv_heads, rows_local * group_size, head_dim)
    own_out, own_lse = attend(
        window_queries,
        (None, rows_local * group_size, head_dim),
        lambda h, i: (h, 0, 0),
        kv_heads,
        1,
        window_keys,
        window_values,
        jnp.float32,
        scaling,
        group_size,
        threshold,
    )
    own_out = own_out.reshape(kv_heads, rows_local, group_size, head_dim)
    own_lse = own_lse.reshape(kv_heads, rows_local, group_size)
    head_rows = jnp.arange(kv_heads, dtype=jnp.int32)[:, None]
    picked = (
        jnp.einsum(
            "htcr,thcx->hrx",
            one_hot,
            answers,
            preferred_element_type=jnp.float32,
        )
        .reshape(kv_heads, rows_local, top_count, group_size, head_dim)
    )
    picked_lse = answer_lse[targets, head_rows, places].reshape(
        kv_heads, rows_local, top_count, group_size
    )
    ceiling = jnp.maximum(own_lse, jnp.max(picked_lse, axis=2))
    own_weight = jnp.exp(own_lse - ceiling)
    far_weight = jnp.exp(picked_lse - ceiling[:, :, None])
    denominator = own_weight + jnp.sum(far_weight, axis=2)
    combined = (
        own_weight[..., None] * own_out + jnp.sum(far_weight[..., None] * picked, axis=2)
    ) / denominator[..., None]
    heads_out = (
        jnp.transpose(combined, (1, 0, 2, 3))
        .astype(jnp.bfloat16)
        .reshape(rows_local, query_heads * head_dim)
    )
    return lax.all_to_all(heads_out, "kvh", split_axis=0, concat_axis=1, tiled=True)


def solution(mesh):
    placed = (
        P("seq", "kvh", None),
        P(None, "seq", "kvh", None),
        P(None, "seq", None, "kvh", None),
        P("kvh", "seq", None),
        P(),
    )
    return jax.shard_map(
        per_device, mesh=mesh, in_specs=placed, out_specs=P(("seq", "kvh"), None), check_vma=False
    )
```

profile of v0, /device:TPU:8, one launch (start us, length us, event | category | flops | bytes accessed | tf_op | source)
XLA Modules:
  0.0 202.2 jit_solution(8228407319189755483)
XLA Ops:
  0.0 11.0 %collective-permute-start = (bf16[1,2,64,2,128]{4,3,2,1,0:T(2,128)(2,1)}, bf16[1,2,64,2,128]{4,3,2,1,0:T(2,128)(2,1)S(1)}, u32[]{:S(2)}, u32[]{:S(2)}) collective-permute-start(bf16[1,2,64,2,128]{4,3,2,1,0:T(2,128)(2,1)} %bitcast.80), channel_id=1, source_target_pairs={{0,32},{4,36},{8,40},{12,44},{16,48},{20,52},{24,56},{28,60},{32,6... | collective-permute-start | bytes 196616 | tf_op jit(solution)/shard_map/ppermute | solution.py:18
  11.1 0.8 copy_bitcast_fusion.2
  11.8 0.7 compare_select_fusion.7
  12.5 0.1 copy.49
  12.6 0.2 reshape.294
  12.9 2.7 %gather_fusion = s32[384]{0:T(512)S(1)} fusion(s32[128]{0:T(128)S(1)} %copy-done.1, s32[1024]{0:T(1024)S(1)} %pad_clamp_fusion), kind=kCustom, calls=%fused_computation | custom fusion | bytes 4608 | tf_op jit(solution)/shard_map/gather | solution.py:102
  15.6 0.1 reshape.241
  15.7 0.1 iota_compare_fusion
  15.8 0.2 fusion.9
  16.1 0.1 broadcast_add_fusion
  16.2 0.2 fusion.13
  16.5 0.1 broadcast_in_dim.13
  16.6 0.3 reshape.388
  16.9 0.6 fusion
  17.5 1.1 copy.52
  18.6 1.5 reshape.244
  20.1 12.1 %all-to-all-start = ((bf16[128,2,16,128]{3,2,1,0:T(8,128)(2,1)}), bf16[128,2,16,128]{3,2,1,0:T(8,128)(2,1)}, u32[]{:S(2)}, u32[]{:S(2)}) async-start(bf16[128,2,16,128]{3,2,1,0:T(8,128)(2,1)} %reshape.244), calls=%async_computation | async-start | bytes 2097152 | tf_op jit(solution)/shard_map/all_to_all | solution.py:121
  32.3 0.2 pad_maximum_fusion.2
  32.4 4.3 %collective-permute-start.1 = (bf16[2,2,64,2,128]{4,3,2,1,0:T(2,128)(2,1)S(1)}, bf16[2,2,64,2,128]{4,3,2,1,0:T(2,128)(2,1)S(1)}, u32[]{:S(2)}, u32[]{:S(2)}) collective-permute-start(bf16[2,2,64,2,128]{4,3,2,1,0:T(2,128)(2,1)S(1)} %pad_maximum_fusion.2), channel_id=1, source_target_pairs={{0,16},{4,20},{8,24},{12,28},{16,32},{20,36},{24,40},{28,44},{32,4... | collective-permute-start | bytes 393224 | tf_op jit(solution)/shard_map/ppermute | solution.py:18
  36.7 1.5 fusion.26
  38.2 26.0 %collective-permute-done.1 = bf16[2,2,64,2,128]{4,3,2,1,0:T(2,128)(2,1)S(1)} collective-permute-done((bf16[2,2,64,2,128]{4,3,2,1,0:T(2,128)(2,1)S(1)}, bf16[2,2,64,2,128]{4,3,2,1,0:T(2,128)(2,1)S(1)}, u32[]{:S(2)}, u32[]{:S(2)}) %collective-permute-start.1) | collective-permute-done | bytes 131104 | tf_op jit(solution)/shard_map/ppermute | solution.py:18
  64.3 0.4 pad_maximum_fusion.1
  64.6 3.7 %collective-permute-start.2 = (bf16[4,2,64,2,128]{4,3,2,1,0:T(2,128)(2,1)S(1)}, bf16[4,2,64,2,128]{4,3,2,1,0:T(2,128)(2,1)S(1)}, u32[]{:S(2)}, u32[]{:S(2)}) collective-permute-start(bf16[4,2,64,2,128]{4,3,2,1,0:T(2,128)(2,1)S(1)} %pad_maximum_fusion.1), channel_id=1, source_target_pairs={{0,64},{4,68},{8,72},{12,76},{16,80},{20,84},{24,88},{28,92},{32,9... | collective-permute-start | bytes 786440 | tf_op jit(solution)/shard_map/ppermute | solution.py:18
  68.4 1.6 copy_bitcast_fusion
  70.1 3.7 %collective-permute-done.2 = bf16[4,2,64,2,128]{4,3,2,1,0:T(2,128)(2,1)S(1)} collective-permute-done((bf16[4,2,64,2,128]{4,3,2,1,0:T(2,128)(2,1)S(1)}, bf16[4,2,64,2,128]{4,3,2,1,0:T(2,128)(2,1)S(1)}, u32[]{:S(2)}, u32[]{:S(2)}) %collective-permute-start.2) | collective-permute-done | bytes 262176 | tf_op jit(solution)/shard_map/ppermute | solution.py:18
  73.8 0.8 pad_maximum_fusion
  74.5 2.4 %collective-permute-start.3 = (bf16[8,2,64,2,128]{4,3,2,1,0:T(2,128)(2,1)S(1)}, bf16[8,2,64,2,128]{4,3,2,1,0:T(2,128)(2,1)S(1)}, u32[]{:S(2)}, u32[]{:S(2)}) collective-permute-start(bf16[8,2,64,2,128]{4,3,2,1,0:T(2,128)(2,1)S(1)} %pad_maximum_fusion), channel_id=1, source_target_pairs={{0,8},{4,12},{8,16},{12,20},{16,24},{20,28},{24,32},{28,36},{32,40... | collective-permute-start | bytes 1572872 | tf_op jit(solution)/shard_map/ppermute | solution.py:18
  76.9 0.7 constant_dynamic-update-slice_fusion.4
  77.6 0.7 constant_dynamic-update-slice_fusion.3
  78.4 0.8 constant_dynamic-update-slice_fusion.2
  79.2 1.2 constant_dynamic-update-slice_fusion.1
  80.4 10.6 %collective-permute-done.3 = bf16[8,2,64,2,128]{4,3,2,1,0:T(2,128)(2,1)S(1)} collective-permute-done((bf16[8,2,64,2,128]{4,3,2,1,0:T(2,128)(2,1)S(1)}, bf16[8,2,64,2,128]{4,3,2,1,0:T(2,128)(2,1)S(1)}, u32[]{:S(2)}, u32[]{:S(2)}) %collective-permute-start.3) | collective-permute-done | bytes 524320 | tf_op jit(solution)/shard_map/ppermute | solution.py:18
  91.0 2.0 constant_dynamic-update-slice_fusion
  92.9 2.1 %collective-permute-start.4 = (bf16[16,2,64,2,128]{4,3,2,1,0:T(2,128)(2,1)}, bf16[16,2,64,2,128]{4,3,2,1,0:T(2,128)(2,1)S(1)}, u32[]{:S(2)}, u32[]{:S(2)}) collective-permute-start(bf16[16,2,64,2,128]{4,3,2,1,0:T(2,128)(2,1)} %get-tuple-element.23), channel_id=1, source_target_pairs={{0,4},{4,8},{8,12},{12,16},{16,20},{20,24},{24,28},{28,32},{32,36}... | collective-permute-start | bytes 3145736 | tf_op jit(solution)/shard_map/ppermute | solution.py:18
  95.1 26.5 %shard_map.65 = (bf16[128,2,16,128]{3,2,1,0:T(8,128)(2,1)}, f32[2,2048,1]{2,1,0:T(8,128)}) custom-call(bf16[128,2,16,128]{3,2,1,0:T(8,128)(2,1)} %all-to-all-done.refs_0_, bf16[2,2048,128]{2,1,0:T(8,128)(2,1)} %get-tuple-element.36.refs_1_, bf16[2,2048,128]{2,1,0:T(8,128)(2,1)} %get-tuple-element.35.refs_2_), custom_call_target="tpu_custom_call" | custom-call | flops 4294967296 | bytes 4194304 | tf_op jit(solution)/shard_map/pallas_call | solution.py:74
  121.6 2.2 %reduce.26 = f32[2,2048]{1,0:T(2,128)S(1)} reduce(f32[2,2048,1]{2,1,0:T(8,128)} %get-tuple-element.10, f32[]{:T(128)} %constant.215), dimensions={2}, to_apply=%get-tuple-element.10.reduce_sub_computation | reduce | bytes 32772 | tf_op jit(solution)/shard_map/pallas_call | solution.py:74
  123.8 0.1 reshape.245
  123.9 0.7 copy.55
  124.7 13.5 %all-to-all-start.1 = ((f32[128,2,16]{2,1,0:T(2,128)}), f32[128,2,16]{2,1,0:T(2,128)S(1)}, u32[]{:S(2)}, u32[]{:S(2)}) async-start(f32[128,2,16]{2,1,0:T(2,128)} %copy.55), calls=%async_computation.1 | async-start | bytes 262144 | tf_op jit(solution)/shard_map/all_to_all | solution.py:139
  138.3 11.8 %all-to-all-done.1 = f32[128,2,16]{2,1,0:T(2,128)S(1)} async-done(((f32[128,2,16]{2,1,0:T(2,128)}), f32[128,2,16]{2,1,0:T(2,128)S(1)}, u32[]{:S(2)}, u32[]{:S(2)}) %all-to-all-start.1) | async-done | bytes 16416 | tf_op jit(solution)/shard_map/all_to_all | solution.py:139
  150.1 6.5 %all-to-all-start.2 = ((bf16[128,2,16,128]{3,2,1,0:T(8,128)(2,1)}), bf16[128,2,16,128]{3,2,1,0:T(8,128)(2,1)S(1)}, u32[]{:S(2)}, u32[]{:S(2)}) async-start(bf16[128,2,16,128]{3,2,1,0:T(8,128)(2,1)} %get-tuple-element.12), calls=%async_computation.2 | async-start | bytes 2097152 | tf_op jit(solution)/shard_map/all_to_all | solution.py:138
  157.8 0.3 compare_reduce_fusion.9
  158.1 0.6 reshape_select_fusion.1.refs_0_
  158.7 1.8 constant_dynamic-update-slice_fusion.5
  160.6 2.9 %slice_bitcast_fusion = (bf16[2,32,64,128]{3,0,2,1:T(2,128)(2,1)S(1)}, bf16[2,32,64,128]{3,0,2,1:T(2,128)(2,1)S(1)}) fusion(bf16[32,2,64,2,128]{4,3,2,1,0:T(2,128)(2,1)} %constant_dynamic-update-slice_fusion.5), kind=kLoop, calls=%fused_computation.5 | loop fusion | bytes 4194304 | tf_op jit(solution)/shard_map/transpose | solution.py:145
  163.5 1.3 copy.48
  164.8 1.3 copy.47
  166.1 8.1 %shard_map.64 = (f32[2,512,128]{2,1,0:T(8,128)}, f32[2,512,1]{2,1,0:T(8,128)}) custom-call(s32[1,2048]{1,0:T(1,128)} %reshape_select_fusion.1.refs_0_, bf16[2,512,128]{2,1,0:T(8,128)(2,1)} %get-tuple-element.27.refs_1_, bf16[2,2048,128]{2,1,0:T(8,128)(2,1)} %bitcast.77, bf16[2,2048,128]{2,1,0:T(8,128)(2,1)} %bitcast.76), custom_call_target="tpu_custom_call" | custom-call | flops 1073741824 | bytes 2621440 | tf_op jit(solution)/shard_map/pallas_call | solution.py:74
  174.2 1.2 reduce.25
  175.4 0.1 reshape.240
  175.6 0.2 copy.57
  175.8 4.5 %gather_fusion.1 = f32[384,8]{1,0:T(8,128)S(1)} fusion(f32[128,2,2,8]{3,2,1,0:T(2,128)S(1)} %copy.57, s32[384]{0:T(512)S(1)} %reshape.300), kind=kCustom, calls=%fused_computation.1 | custom fusion | bytes 29184 | tf_op jit(solution)/shard_map/gather | solution.py:179
  180.4 0.2 reduce_max.9
  180.6 0.3 fusion.25
  180.9 7.2 %all-to-all-done.2 = bf16[128,2,16,128]{3,2,1,0:T(8,128)(2,1)S(1)} async-done(((bf16[128,2,16,128]{3,2,1,0:T(8,128)(2,1)}), bf16[128,2,16,128]{3,2,1,0:T(8,128)(2,1)S(1)}, u32[]{:S(2)}, u32[]{:S(2)}) %all-to-all-start.2) | async-done | bytes 1048608 | tf_op jit(solution)/shard_map/all_to_all | solution.py:138
  188.1 0.3 reshape.250
  188.4 0.8 fusion.1
  189.2 0.3 copy.66
  189.5 0.5 multiply_reduce_fusion
  190.1 0.2 copy-done.4
  190.2 0.4 fusion.11
  190.6 0.1 all_to_all.26
  190.8 10.8 %all_to_all.34 = bf16[4,16,2048]{2,1,0:T(8,128)(2,1)S(1)} all-to-all(bf16[4,16,2048]{2,1,0:T(8,128)(2,1)S(1)} %all_to_all.26), channel_id=1, replica_groups=mesh['seq'=128,'kvh'=4] {'kvh'}, dimensions={0} | all-to-all | bytes 524288 | tf_op jit(solution)/shard_map/all_to_all | solution.py:194
  201.5 0.7 copy.65
  (55 shorter events, 1.7 us)
Async XLA Ops:
  0.0 11.1 %copy-start = (bf16[64,16,128]{2,1,0:T(8,128)(2,1)S(1)}, bf16[64,16,128]{2,1,0:T(8,128)(2,1)}, u32[]{:S(2)}) copy-start(bf16[64,16,128]{2,1,0:T(8,128)(2,1)} %param.6) | copy-start | bytes 786436
  0.0 12.9 %copy-start.1 = (s32[128]{0:T(128)S(1)}, s32[128]{0:T(128)}, u32[]{:S(2)}) copy-start(s32[128]{0:T(128)} %param.10) | copy-start | bytes 1540
  0.0 32.2 %collective-permute-start = (bf16[1,2,64,2,128]{4,3,2,1,0:T(2,128)(2,1)}, bf16[1,2,64,2,128]{4,3,2,1,0:T(2,128)(2,1)S(1)}, u32[]{:S(2)}, u32[]{:S(2)}) collective-permute-start(bf16[1,2,64,2,128]{4,3,2,1,0:T(2,128)(2,1)} %bitcast.80), channel_id=1, source_target_pairs={{0,32},{4,36},{8,40},{12,44},{16,48},{20,52},{24,56},{28,60},{32,6... | collective-permute-start | bytes 196616 | tf_op jit(solution)/shard_map/ppermute | solution.py:18
  18.6 13.6 %copy-start.3 = (bf16[2,64,2,128]{3,2,1,0:T(2,128)(2,1)S(1)}, bf16[2,64,2,128]{3,2,1,0:T(2,128)(2,1)}, u32[]{:S(2)}) copy-start(bf16[2,64,2,128]{3,2,1,0:T(2,128)(2,1)} %param.7) | copy-start | bytes 196612
  18.6 18.1 %copy-start.2 = (bf16[2,1,2048,2,128]{4,3,2,1,0:T(2,128)(2,1)S(1)}, bf16[2,1,2048,2,128]{4,3,2,1,0:T(2,128)(2,1)}, u32[]{:S(2)}) copy-start(bf16[2,1,2048,2,128]{4,3,2,1,0:T(2,128)(2,1)} %param.8) | copy-start | bytes 6291460
  20.1 74.9 %all-to-all-start = ((bf16[128,2,16,128]{3,2,1,0:T(8,128)(2,1)}), bf16[128,2,16,128]{3,2,1,0:T(8,128)(2,1)}, u32[]{:S(2)}, u32[]{:S(2)}) async-start(bf16[128,2,16,128]{3,2,1,0:T(8,128)(2,1)} %reshape.244), calls=%async_computation | async-start | bytes 2097152 | tf_op jit(solution)/shard_map/all_to_all | solution.py:121
  32.4 31.8 %collective-permute-start.1 = (bf16[2,2,64,2,128]{4,3,2,1,0:T(2,128)(2,1)S(1)}, bf16[2,2,64,2,128]{4,3,2,1,0:T(2,128)(2,1)S(1)}, u32[]{:S(2)}, u32[]{:S(2)}) collective-permute-start(bf16[2,2,64,2,128]{4,3,2,1,0:T(2,128)(2,1)S(1)} %pad_maximum_fusion.2), channel_id=1, source_target_pairs={{0,16},{4,20},{8,24},{12,28},{16,32},{20,36},{24,40},{28,44},{32,4... | collective-permute-start | bytes 393224 | tf_op jit(solution)/shard_map/ppermute | solution.py:18
  64.6 9.1 %collective-permute-start.2 = (bf16[4,2,64,2,128]{4,3,2,1,0:T(2,128)(2,1)S(1)}, bf16[4,2,64,2,128]{4,3,2,1,0:T(2,128)(2,1)S(1)}, u32[]{:S(2)}, u32[]{:S(2)}) collective-permute-start(bf16[4,2,64,2,128]{4,3,2,1,0:T(2,128)(2,1)S(1)} %pad_maximum_fusion.1), channel_id=1, source_target_pairs={{0,64},{4,68},{8,72},{12,76},{16,80},{20,84},{24,88},{28,92},{32,9... | collective-permute-start | bytes 786440 | tf_op jit(solution)/shard_map/ppermute | solution.py:18
  74.5 16.5 %collective-permute-start.3 = (bf16[8,2,64,2,128]{4,3,2,1,0:T(2,128)(2,1)S(1)}, bf16[8,2,64,2,128]{4,3,2,1,0:T(2,128)(2,1)S(1)}, u32[]{:S(2)}, u32[]{:S(2)}) collective-permute-start(bf16[8,2,64,2,128]{4,3,2,1,0:T(2,128)(2,1)S(1)} %pad_maximum_fusion), channel_id=1, source_target_pairs={{0,8},{4,12},{8,16},{12,20},{16,24},{20,28},{24,32},{28,36},{32,40... | collective-permute-start | bytes 1572872 | tf_op jit(solution)/shard_map/ppermute | solution.py:18
  92.9 65.8 %collective-permute-start.4 = (bf16[16,2,64,2,128]{4,3,2,1,0:T(2,128)(2,1)}, bf16[16,2,64,2,128]{4,3,2,1,0:T(2,128)(2,1)S(1)}, u32[]{:S(2)}, u32[]{:S(2)}) collective-permute-start(bf16[16,2,64,2,128]{4,3,2,1,0:T(2,128)(2,1)} %get-tuple-element.23), channel_id=1, source_target_pairs={{0,4},{4,8},{8,12},{12,16},{16,20},{20,24},{24,28},{28,32},{32,36}... | collective-permute-start | bytes 3145736 | tf_op jit(solution)/shard_map/ppermute | solution.py:18
  124.7 25.5 %all-to-all-start.1 = ((f32[128,2,16]{2,1,0:T(2,128)}), f32[128,2,16]{2,1,0:T(2,128)S(1)}, u32[]{:S(2)}, u32[]{:S(2)}) async-start(f32[128,2,16]{2,1,0:T(2,128)} %copy.55), calls=%async_computation.1 | async-start | bytes 262144 | tf_op jit(solution)/shard_map/all_to_all | solution.py:139
  150.1 38.0 %all-to-all-start.2 = ((bf16[128,2,16,128]{3,2,1,0:T(8,128)(2,1)}), bf16[128,2,16,128]{3,2,1,0:T(8,128)(2,1)S(1)}, u32[]{:S(2)}, u32[]{:S(2)}) async-start(bf16[128,2,16,128]{3,2,1,0:T(8,128)(2,1)} %get-tuple-element.12), calls=%async_computation.2 | async-start | bytes 2097152 | tf_op jit(solution)/shard_map/all_to_all | solution.py:138
  189.2 1.0 copy-start.4
where the time goes:
time: 203 us; the launch traced here: 202 us
  waiting for transfers between devices  59.3 us (29%)
  starting transfers between devices  55.6 us (27%)
  Pallas kernels  34.6 us (17%)
  local copies, waits for them, and re-layouts  30.5 us (15%)
  blocking collectives  10.8 us (5%)
  other arithmetic  9.6 us (5%)
    ppermute x5, waiting for transfers between devices, shifted(): lax.ppermute(value, axis, [(source, source + steps) for source in range(i...  40.3 us
    pallas_call x2, Pallas kernels, attend(): pl.pallas_call(functools.partial(attend_kernel, thr is not None, scaling,...  34.6 us
    ppermute x5, starting transfers between devices, shifted(): lax.ppermute(value, axis, [(source, source + steps) for source in range(i...  23.5 us
    all_to_all x1, starting transfers between devices, per_device(): lax.all_to_all(served_lse, 'seq', split_axis=0, concat_axis=0, tiled=True)  13.5 us
    all_to_all x1, starting transfers between devices, per_device(): lax.all_to_all(outgoing, 'seq', split_axis=0, concat_axis=0, tiled=True)  12.1 us
    all_to_all x1, waiting for transfers between devices, per_device(): lax.all_to_all(served_lse, 'seq', split_axis=0, concat_axis=0, tiled=True)  11.8 us
    all_to_all x1, blocking collectives, per_device(): lax.all_to_all(heads_out, 'kvh', split_axis=0, concat_axis=1, tiled=True)  10.8 us
    all_to_all x1, waiting for transfers between devices, per_device(): lax.all_to_all(served, 'seq', split_axis=0, concat_axis=0, tiled=True)  7.18 us
  transfers between devices with their start and end apart: 8, of which 5 were waited for; matrix products, arithmetic and copies ran while one was open for 19% of the time, Pallas kernels for 17%

commit v1 on v0

--- a/solution.py
+++ b/solution.py
@@ -10,6 +10,7 @@
 BLOCK_TOKENS = 2048
 BLOCK_PICK_LIMIT = 2
 WINDOW_SHIFTS = (8, 4, 16, 2, 1)
+LOG2_E = 1.4426950408889634
 
 
 def shifted(value, axis, steps):
@@ -18,15 +19,20 @@
     return lax.ppermute(value, axis, [(source, source + steps) for source in range(initial, last)])
 
 
-def gather_window(stretch_kv, span_devices):
+def gather_window(stretch_kv, span_devices, companions):
     stack = stretch_kv[None]
     offsets = [0]
-    for step in WINDOW_SHIFTS:
+    results = []
+    for index, step in enumerate(WINDOW_SHIFTS):
         if len(offsets) >= span_devices:
             break
-        stack = jnp.concatenate([stack, shifted(stack, "seq", step)], axis=0)
+        arrived = shifted(stack, "seq", step)
+        if index < len(companions) and companions[index] is not None:
+            arrived, done = lax.optimization_barrier((arrived, companions[index]()))
+            results.append(done)
+        stack = jnp.concatenate([stack, arrived], axis=0)
         offsets = offsets + [o + step for o in offsets]
-    return stack, offsets
+    return stack, offsets, results
 
 
 def attend_kernel(masked, scaling, group_size, *refs):
@@ -36,27 +42,24 @@
         q_ref, k_ref, v_ref, o_ref, lse_ref = refs
     q = q_ref[...]
     q = q.reshape(-1, q.shape[-1])
-    scores = (
-        lax.dot_general(
-            q, k_ref[...], (((1,), (1,)), ((), ())), preferred_element_type=jnp.float32
-        )
-        * scaling
+    scores = lax.dot_general(
+        q, k_ref[...], (((1,), (1,)), ((), ())), preferred_element_type=jnp.float32
     )
     if masked:
         token = lax.broadcasted_iota(jnp.int32, (scores.shape[0], 1), 0) // group_size
         scores = jnp.where(token >= thr_ref[...], scores, -jnp.inf)
     highest = jnp.max(scores, axis=1, keepdims=True)
-    raw_weights = jnp.exp(scores - highest)
+    raw_weights = jnp.exp2((scores - highest) * (scaling * LOG2_E))
     weight_sum = jnp.sum(raw_weights, axis=1, keepdims=True)
     blended = (
         jnp.dot(raw_weights.astype(jnp.bfloat16), v_ref[...], preferred_element_type=jnp.float32)
         / weight_sum
     )
     o_ref[...] = blended.astype(o_ref.dtype).reshape(o_ref.shape)
-    lse_ref[...] = highest + jnp.log(weight_sum)
-
-
-def attend(q, q_block, q_map, heads, tiles, keys, values, out_dtype, scaling, group_size, thr=None):
+    lse_ref[...] = highest * scaling + jnp.log(weight_sum)
+
+
+def attend(q, q_block, q_map, heads, tiles, keys, values, out_dtype, scaling, group_size, thr=None, out_rows=None, out_map=None):
     rows = q_block[0] * q_block[-2] if len(q_block) == 4 else q_block[-2]
     total_rows = rows * tiles
     key_count, head_dim = keys.shape[1], keys.shape[2]
@@ -76,11 +79,11 @@
         grid=(heads, tiles),
         in_specs=in_specs,
         out_specs=[
-            pl.BlockSpec(q_block, q_map),
+            pl.BlockSpec(q_block, out_map or q_map),
             pl.BlockSpec((None, rows, 1), lambda h, i: (h, i, 0)),
         ],
         out_shape=[
-            jax.ShapeDtypeStruct(q.shape, out_dtype),
+            jax.ShapeDtypeStruct(((out_rows or q.shape[0]),) + q.shape[1:], out_dtype),
             jax.ShapeDtypeStruct((heads, total_rows, 1), jnp.float32),
         ],
         cost_estimate=cost,
@@ -119,28 +122,62 @@
     slab = capacity * group_size
     outgoing = outgoing.reshape(seq_count, kv_heads, slab, head_dim)
     arrived = lax.all_to_all(outgoing, "seq", split_axis=0, concat_axis=0, tiled=True)
+    arrived, window_start = lax.optimization_barrier((arrived, stretch_kv))
     cache_keys = jnp.swapaxes(cache_kv[0, 0], 0, 1)
     cache_values = jnp.swapaxes(cache_kv[1, 0], 0, 1)
     sources_per_tile = 32
-    served, served_lse = attend(
-        arrived,
-        (sources_per_tile, None, slab, head_dim),
-        lambda h, i: (i, h, 0, 0),
-        kv_heads,
-        seq_count // sources_per_tile,
-        cache_keys,
-        cache_values,
-        jnp.bfloat16,
-        scaling,
-        group_size,
-    )
-    served_lse = jnp.swapaxes(served_lse.reshape(kv_heads, seq_count, slab), 0, 1)
-    answers = lax.all_to_all(served, "seq", split_axis=0, concat_axis=0, tiled=True)
-    answer_lse = lax.all_to_all(served_lse, "seq", split_axis=0, concat_axis=0, tiled=True)
-    answers = answers.reshape(seq_count, kv_heads, capacity, group_size * head_dim)
-    answer_lse = answer_lse.reshape(seq_count, kv_heads, capacity, group_size)
-    window, offsets = gather_window(stretch_kv, span_devices)
+    pieces = seq_count // sources_per_tile
+
+    def serve_piece(piece):
+        return attend(
+            arrived,
+            (sources_per_tile, None, slab, head_dim),
+            lambda h, i: (piece, h, 0, 0),
+            kv_heads,
+            1,
+            cache_keys,
+            cache_values,
+            jnp.bfloat16,
+            scaling,
+            group_size,
+            out_rows=sources_per_tile,
+            out_map=lambda h, i: (0, h, 0, 0),
+        )
+
+    window, offsets, served_pieces = gather_window(
+        window_start,
+        span_devices,
+        [None] + [functools.partial(serve_piece, piece) for piece in range(pieces)],
+    )
     blocks = window.shape[0]
+    served = jnp.concatenate([piece[0] for piece in served_pieces], axis=0)
+    served_lse = jnp.concatenate(
+        [piece[1].reshape(kv_heads, sources_per_tile, slab) for piece in served_pieces], axis=1
+    )
+    served_lse = jnp.swapaxes(served_lse, 0, 1)
+    served, served_lse, window = lax.optimization_barrier((served, served_lse, window))
+    lse_rounded = lax.reduce_precision(served_lse, exponent_bits=8, mantissa_bits=7)
+    lse_high = lse_rounded.astype(jnp.bfloat16)
+    lse_low = (served_lse - lse_rounded).astype(jnp.bfloat16)
+    payload_width = kv_heads * slab * head_dim
+    lse_width = 2 * kv_heads * slab
+    lse_lanes = -(-lse_width // 128) * 128
+    lse_pack = jnp.concatenate([lse_high, lse_low], axis=2).reshape(seq_count, lse_width)
+    payload = jnp.concatenate(
+        [
+            served.reshape(seq_count, payload_width),
+            jnp.pad(lse_pack, ((0, 0), (0, lse_lanes - lse_width))),
+        ],
+        axis=1,
+    )
+    returned = lax.all_to_all(payload, "seq", split_axis=0, concat_axis=0, tiled=True)
+    answers = returned[:, :payload_width].reshape(seq_count, kv_heads, capacity, group_size * head_dim)
+    lse_parts = returned[:, payload_width : payload_width + lse_width].reshape(
+        seq_count, kv_heads, 2 * slab
+    ).astype(jnp.float32)
+    answer_lse = (lse_parts[:, :, :slab] + lse_parts[:, :, slab:]).reshape(
+        seq_count, kv_heads, capacity, group_size
+    )
     window_keys = jnp.transpose(window[:, 0], (2, 0, 1, 3)).reshape(kv_heads, blocks * rows_local, head_dim)
     window_values = jnp.transpose(window[:, 1], (2, 0, 1, 3)).reshape(kv_heads, blocks * rows_local, head_dim)
     key_index = jnp.arange(blocks * rows_local, dtype=jnp.int32)

time: 203 us -> 202 us (level)
  blocking collectives: 10.8 us -> 59.5 us
  waiting for transfers between devices: 59.3 us -> 29 us
  starting transfers between devices: 55.6 us -> 25.8 us
  local copies, waits for them, and re-layouts: 30.5 us -> 36.8 us
  Pallas kernels: 34.6 us -> 38.6 us
    all_to_all x0 -> x1, blocking collectives: none -> 48.7 us  [per_device(): lax.all_to_all(outgoing, 'seq', split_axis=0, concat_axis=0, tiled=True)]
    ppermute x5, waiting for transfers between devices: 40.3 us -> 14.1 us  [shifted(): lax.ppermute(value, axis, [(source, source + steps) for source in range(i...]
    all_to_all x3 -> x1, starting transfers between devices: 32.1 us -> 11.5 us  [per_device(): lax.all_to_all(payload, 'seq', split_axis=0, concat_axis=0, tiled=True)]
    ppermute x5, starting transfers between devices: 23.5 us -> 14.3 us  [shifted(): lax.ppermute(value, axis, [(source, source + steps) for source in range(i...]
    unnamed x15 -> x38, local copies, waits for them, and re-layouts: 4.03 us -> 9.6 us
    all_to_all x3 -> x1, waiting for transfers between devices: 19 us -> 14.8 us  [per_device(): lax.all_to_all(payload, 'seq', split_axis=0, concat_axis=0, tiled=True)]
    pallas_call x2 -> x5, Pallas kernels: 34.6 us -> 38.6 us  [attend(): pl.pallas_call(functools.partial(attend_kernel, thr is not None, scaling,...]
    all_to_all x1 -> x2, local copies, waits for them, and re-layouts: 0.06 us -> 3.24 us  [per_device(): lax.all_to_all(payload, 'seq', split_axis=0, concat_axis=0, tiled=True)]
  transfers between devices with their start and end apart: 8 -> 6, of which waited for: 5 -> 4; matrix products, arithmetic and copies ran while one was open for 19% -> 9% of each run, Pallas kernels for 17% -> 19%
where the time goes in v1:
time: 202 us; the launch traced here: 201 us
  blocking collectives  59.5 us (29%)
  Pallas kernels  38.6 us (19%)
  local copies, waits for them, and re-layouts  36.8 us (18%)
  waiting for transfers between devices  29 us (14%)
  starting transfers between devices  25.8 us (13%)
  other arithmetic  10 us (5%)
    all_to_all x1, blocking collectives, per_device(): lax.all_to_all(outgoing, 'seq', split_axis=0, concat_axis=0, tiled=True)  48.7 us
    pallas_call x5, Pallas kernels, attend(): pl.pallas_call(functools.partial(attend_kernel, thr is not None, scaling,...  38.6 us
    all_to_all x1, waiting for transfers between devices, per_device(): lax.all_to_all(payload, 'seq', split_axis=0, concat_axis=0, tiled=True)  14.8 us
    ppermute x5, starting transfers between devices, shifted(): lax.ppermute(value, axis, [(source, source + steps) for source in range(i...  14.3 us
    ppermute x5, waiting for transfers between devices, shifted(): lax.ppermute(value, axis, [(source, source + steps) for source in range(i...  14.1 us
    all_to_all x1, starting transfers between devices, per_device(): lax.all_to_all(payload, 'seq', split_axis=0, concat_axis=0, tiled=True)  11.5 us
    all_to_all x1, blocking collectives, per_device(): lax.all_to_all(heads_out, 'kvh', split_axis=0, concat_axis=1, tiled=True)  10.8 us
    unnamed x38, local copies, waits for them, and re-layouts  9.6 us
  transfers between devices with their start and end apart: 6, of which 4 were waited for; matrix products, arithmetic and copies ran while one was open for 9% of the time, Pallas kernels for 19%

profile of v1, /device:TPU:8, one launch (start us, length us, event | category | flops | bytes accessed | tf_op | source)
XLA Modules:
  0.0 201.3 jit_solution(3900115504250548557)
XLA Ops:
  0.0 0.7 compare_select_fusion.7
  0.9 0.2 reshape.320
  1.1 2.7 %gather_fusion = s32[384]{0:T(512)S(1)} fusion(s32[128]{0:T(128)S(1)} %copy-done.1, s32[1024]{0:T(1024)S(1)} %pad_clamp_fusion), kind=kCustom, calls=%fused_computation | custom fusion | bytes 4608 | tf_op jit(solution)/shard_map/gather | solution.py:105
  4.0 0.2 fusion.11
  4.4 0.2 fusion.15
  4.7 0.8 copy_bitcast_fusion.3
  5.6 0.3 reshape.414
  5.9 0.6 fusion.1
  6.5 1.1 copy.69
  7.6 0.7 reshape.261
  8.3 48.7 %all_to_all.36.refs_0_ = bf16[128,2,16,128]{3,2,1,0:T(8,128)(2,1)} all-to-all(bf16[128,2,16,128]{3,2,1,0:T(8,128)(2,1)S(1)} %reshape.261), channel_id=1, replica_groups=mesh['seq'=128,'kvh'=4] {'seq'}, dimensions={0} | all-to-all | bytes 2097152 | tf_op jit(solution)/shard_map/all_to_all | solution.py:124
  57.1 3.3 %collective-permute-start = (bf16[1,2,64,2,128]{4,3,2,1,0:T(2,128)(2,1)S(1)}, bf16[1,2,64,2,128]{4,3,2,1,0:T(2,128)(2,1)S(1)}, u32[]{:S(2)}, u32[]{:S(2)}) collective-permute-start(bf16[1,2,64,2,128]{4,3,2,1,0:T(2,128)(2,1)S(1)} %bitcast.98), channel_id=1, source_target_pairs={{0,32},{4,36},{8,40},{12,44},{16,48},{20,52},{24,56},{28,60},{32,6... | collective-permute-start | bytes 196616 | tf_op jit(solution)/shard_map/ppermute | solution.py:19
  60.4 1.5 fusion.30
  61.9 6.2 %collective-permute-done = bf16[1,2,64,2,128]{4,3,2,1,0:T(2,128)(2,1)S(1)} collective-permute-done((bf16[1,2,64,2,128]{4,3,2,1,0:T(2,128)(2,1)S(1)}, bf16[1,2,64,2,128]{4,3,2,1,0:T(2,128)(2,1)S(1)}, u32[]{:S(2)}, u32[]{:S(2)}) %collective-permute-start) | collective-permute-done | bytes 65568 | tf_op jit(solution)/shard_map/ppermute | solution.py:19
  68.1 0.2 pad_maximum_fusion.3
  68.3 2.4 %collective-permute-start.1 = (bf16[2,2,64,2,128]{4,3,2,1,0:T(2,128)(2,1)S(1)}, bf16[2,2,64,2,128]{4,3,2,1,0:T(2,128)(2,1)S(1)}, u32[]{:S(2)}, u32[]{:S(2)}) collective-permute-start(bf16[2,2,64,2,128]{4,3,2,1,0:T(2,128)(2,1)S(1)} %pad_maximum_fusion.3), channel_id=1, source_target_pairs={{0,16},{4,20},{8,24},{12,28},{16,32},{20,36},{24,40},{28,44},{32,4... | collective-permute-start | bytes 393224 | tf_op jit(solution)/shard_map/ppermute | solution.py:19
  70.7 1.6 copy_bitcast_fusion.1
  72.3 7.6 %shard_map.64 = (bf16[32,2,16,128]{3,2,1,0:T(8,128)(2,1)}, f32[2,512,1]{2,1,0:T(8,128)}) custom-call(bf16[128,2,16,128]{3,2,1,0:T(8,128)(2,1)} %all_to_all.36.refs_0_, bf16[2,2048,128]{2,1,0:T(8,128)(2,1)} %get-tuple-element.84.refs_1_, bf16[2,2048,128]{2,1,0:T(8,128)(2,1)} %get-tuple-element.83.refs_2_), custom_call_target="tpu_custom_call" | custom-call | flops 1073741824 | bytes 2621440 | tf_op jit(solution)/shard_map/pallas_call | solution.py:77
  79.9 0.4 pad_maximum_fusion.2
  80.3 3.0 %collective-permute-start.2 = (bf16[4,2,64,2,128]{4,3,2,1,0:T(2,128)(2,1)S(1)}, bf16[4,2,64,2,128]{4,3,2,1,0:T(2,128)(2,1)S(1)}, u32[]{:S(2)}, u32[]{:S(2)}) collective-permute-start(bf16[4,2,64,2,128]{4,3,2,1,0:T(2,128)(2,1)S(1)} %pad_maximum_fusion.2), channel_id=1, source_target_pairs={{0,64},{4,68},{8,72},{12,76},{16,80},{20,84},{24,88},{28,92},{32,9... | collective-permute-start | bytes 786440 | tf_op jit(solution)/shard_map/ppermute | solution.py:19
  83.3 7.7 %shard_map.65 = (bf16[32,2,16,128]{3,2,1,0:T(8,128)(2,1)}, f32[2,512,1]{2,1,0:T(8,128)}) custom-call(bf16[128,2,16,128]{3,2,1,0:T(8,128)(2,1)} %all_to_all.36.refs_0_, bf16[2,2048,128]{2,1,0:T(8,128)(2,1)} %get-tuple-element.84.refs_1_, bf16[2,2048,128]{2,1,0:T(8,128)(2,1)} %get-tuple-element.83.refs_2_), custom_call_target="tpu_custom_call" | custom-call | flops 1073741824 | bytes 2621440 | tf_op jit(solution)/shard_map/pallas_call | solution.py:77
  90.9 0.7 pad_maximum_fusion.1
  91.7 3.4 %collective-permute-start.3 = (bf16[8,2,64,2,128]{4,3,2,1,0:T(2,128)(2,1)S(1)}, bf16[8,2,64,2,128]{4,3,2,1,0:T(2,128)(2,1)S(1)}, u32[]{:S(2)}, u32[]{:S(2)}) collective-permute-start(bf16[8,2,64,2,128]{4,3,2,1,0:T(2,128)(2,1)S(1)} %pad_maximum_fusion.1), channel_id=1, source_target_pairs={{0,8},{4,12},{8,16},{12,20},{16,24},{20,28},{24,32},{28,36},{32,40... | collective-permute-start | bytes 1572872 | tf_op jit(solution)/shard_map/ppermute | solution.py:19
  95.1 0.7 constant_dynamic-update-slice_fusion.10
  95.8 7.6 %shard_map.66 = (bf16[32,2,16,128]{3,2,1,0:T(8,128)(2,1)}, f32[2,512,1]{2,1,0:T(8,128)}) custom-call(bf16[128,2,16,128]{3,2,1,0:T(8,128)(2,1)} %all_to_all.36.refs_0_, bf16[2,2048,128]{2,1,0:T(8,128)(2,1)} %get-tuple-element.84.refs_1_, bf16[2,2048,128]{2,1,0:T(8,128)(2,1)} %get-tuple-element.83.refs_2_), custom_call_target="tpu_custom_call" | custom-call | flops 1073741824 | bytes 2621440 | tf_op jit(solution)/shard_map/pallas_call | solution.py:77
  103.4 0.7 constant_dynamic-update-slice_fusion.9
  104.1 0.8 constant_dynamic-update-slice_fusion.8
  105.0 1.3 constant_dynamic-update-slice_fusion.7
  106.3 0.5 collective-permute-done.3
  106.7 2.0 constant_dynamic-update-slice_fusion.6
  108.7 2.3 %collective-permute-start.4 = (bf16[16,2,64,2,128]{4,3,2,1,0:T(2,128)(2,1)}, bf16[16,2,64,2,128]{4,3,2,1,0:T(2,128)(2,1)S(1)}, u32[]{:S(2)}, u32[]{:S(2)}) collective-permute-start(bf16[16,2,64,2,128]{4,3,2,1,0:T(2,128)(2,1)} %get-tuple-element.70), channel_id=1, source_target_pairs={{0,4},{4,8},{8,12},{12,16},{16,20},{20,24},{24,28},{28,32},{32,36}... | collective-permute-start | bytes 3145736 | tf_op jit(solution)/shard_map/ppermute | solution.py:19
  111.0 7.7 %shard_map.67 = (bf16[32,2,16,128]{3,2,1,0:T(8,128)(2,1)}, f32[2,512,1]{2,1,0:T(8,128)}) custom-call(bf16[128,2,16,128]{3,2,1,0:T(8,128)(2,1)} %all_to_all.36.refs_0_, bf16[2,2048,128]{2,1,0:T(8,128)(2,1)} %get-tuple-element.84.refs_1_, bf16[2,2048,128]{2,1,0:T(8,128)(2,1)} %get-tuple-element.83.refs_2_), custom_call_target="tpu_custom_call" | custom-call | flops 1073741824 | bytes 2621440 | tf_op jit(solution)/shard_map/pallas_call | solution.py:77
  118.7 0.2 reduce.25
  119.0 0.2 reduce.26
  119.4 0.2 reduce.27
  119.8 7.5 %collective-permute-done.4 = bf16[16,2,64,2,128]{4,3,2,1,0:T(2,128)(2,1)S(1)} collective-permute-done((bf16[16,2,64,2,128]{4,3,2,1,0:T(2,128)(2,1)}, bf16[16,2,64,2,128]{4,3,2,1,0:T(2,128)(2,1)S(1)}, u32[]{:S(2)}, u32[]{:S(2)}) %collective-permute-start.4) | collective-permute-done | bytes 1048608 | tf_op jit(solution)/shard_map/ppermute | solution.py:19
  127.3 0.2 reduce.28
  127.6 1.9 constant_dynamic-update-slice_fusion.5
  129.8 0.5 copy.101
  130.5 0.5 broadcast.558
  131.0 1.4 reduce.55
  132.4 1.6 reshape.447
  134.0 11.5 %all-to-all-start.1 = ((bf16[128,2,2112]{2,1,0:T(2,128)(2,1)}), bf16[128,2,2112]{2,1,0:T(2,128)(2,1)S(1)}, u32[]{:S(2)}, u32[]{:S(2)}) async-start(bf16[128,2,2112]{2,1,0:T(2,128)(2,1)} %reshape.447), calls=%async_computation.1 | async-start | bytes 2228224 | tf_op jit(solution)/shard_map/all_to_all | solution.py:173
  146.8 0.3 compare_reduce_fusion
  147.2 0.6 reshape_select_fusion.1.refs_0_
  147.8 2.9 %slice_bitcast_fusion = (bf16[2,32,64,128]{3,0,2,1:T(2,128)(2,1)S(1)}, bf16[2,32,64,128]{3,0,2,1:T(2,128)(2,1)S(1)}) fusion(bf16[32,2,64,2,128]{4,3,2,1,0:T(2,128)(2,1)} %constant_dynamic-update-slice_fusion.5), kind=kLoop, calls=%fused_computation.13 | loop fusion | bytes 4194304 | tf_op jit(solution)/shard_map/transpose | solution.py:182
  150.7 1.3 copy.77
  152.0 1.3 copy.76
  153.3 8.1 %shard_map.68 = (f32[2,512,128]{2,1,0:T(8,128)}, f32[2,512,1]{2,1,0:T(8,128)}) custom-call(s32[1,2048]{1,0:T(1,128)} %reshape_select_fusion.1.refs_0_, bf16[2,512,128]{2,1,0:T(8,128)(2,1)} %get-tuple-element.71.refs_1_, bf16[2,2048,128]{2,1,0:T(8,128)(2,1)} %bitcast.95, bf16[2,2048,128]{2,1,0:T(8,128)(2,1)} %bitcast.94), custom_call_target="tpu_custom_call" | custom-call | flops 1073741824 | bytes 2621440 | tf_op jit(solution)/shard_map/pallas_call | solution.py:77
  161.4 1.2 reduce.29
  162.7 0.7 reshape.268
  163.4 14.8 %all-to-all-done.1 = bf16[128,2,2112]{2,1,0:T(2,128)(2,1)S(1)} async-done(((bf16[128,2,2112]{2,1,0:T(2,128)(2,1)}), bf16[128,2,2112]{2,1,0:T(2,128)(2,1)S(1)}, u32[]{:S(2)}, u32[]{:S(2)}) %all-to-all-start.1) | async-done | bytes 1081376 | tf_op jit(solution)/shard_map/all_to_all | solution.py:173
  178.2 1.2 reshape.448
  179.4 2.7 %copy.80 = bf16[128,1,4224]{0,2,1:T(8,128)(2,1)S(1)} copy(bf16[128,1,4224]{2,1,0:T(2,128)(2,1)S(1)} %reshape.448) | data formatting | bytes 2162688 | tf_op jit(solution)/shard_map/all_to_all | solution.py:173
  182.3 0.2 copy.81
  182.5 4.5 %gather_fusion.1 = f32[384,8]{1,0:T(8,128)S(1)} fusion(f32[128,2,2,8]{3,2,1,0:T(2,128)S(1)} %copy.81, s32[384]{0:T(512)S(1)} %reshape.326), kind=kCustom, calls=%fused_computation.1 | custom fusion | bytes 29184 | tf_op jit(solution)/shard_map/gather | solution.py:216
  187.1 0.5 fusion.8
  187.6 0.3 copy.93
  188.1 0.3 copy-done.4
  188.5 0.3 fusion.29
  188.8 0.5 multiply_reduce_fusion
  189.3 0.4 fusion.13
  189.8 10.8 %all_to_all.37 = bf16[4,16,2048]{2,1,0:T(8,128)(2,1)S(1)} all-to-all(bf16[4,16,2048]{2,1,0:T(8,128)(2,1)S(1)} %all_to_all.29), channel_id=1, replica_groups=mesh['seq'=128,'kvh'=4] {'kvh'}, dimensions={0} | all-to-all | bytes 524288 | tf_op jit(solution)/shard_map/all_to_all | solution.py:231
  200.6 0.7 copy.91
  (96 shorter events, 3.6 us)
Async XLA Ops:
  0.0 4.7 %copy-start = (bf16[64,16,128]{2,1,0:T(8,128)(2,1)S(1)}, bf16[64,16,128]{2,1,0:T(8,128)(2,1)}, u32[]{:S(2)}) copy-start(bf16[64,16,128]{2,1,0:T(8,128)(2,1)} %param.6) | copy-start | bytes 786436
  0.0 1.1 copy-start.1
  7.6 49.5 %copy-start.3 = (bf16[2,64,2,128]{3,2,1,0:T(2,128)(2,1)S(1)}, bf16[2,64,2,128]{3,2,1,0:T(2,128)(2,1)}, u32[]{:S(2)}) copy-start(bf16[2,64,2,128]{3,2,1,0:T(2,128)(2,1)} %param.7) | copy-start | bytes 196612
  8.3 52.1 %copy-start.2 = (bf16[2,1,2048,2,128]{4,3,2,1,0:T(2,128)(2,1)S(1)}, bf16[2,1,2048,2,128]{4,3,2,1,0:T(2,128)(2,1)}, u32[]{:S(2)}) copy-start(bf16[2,1,2048,2,128]{4,3,2,1,0:T(2,128)(2,1)} %param.8) | copy-start | bytes 6291460
  57.1 11.0 %collective-permute-start = (bf16[1,2,64,2,128]{4,3,2,1,0:T(2,128)(2,1)S(1)}, bf16[1,2,64,2,128]{4,3,2,1,0:T(2,128)(2,1)S(1)}, u32[]{:S(2)}, u32[]{:S(2)}) collective-permute-start(bf16[1,2,64,2,128]{4,3,2,1,0:T(2,128)(2,1)S(1)} %bitcast.98), channel_id=1, source_target_pairs={{0,32},{4,36},{8,40},{12,44},{16,48},{20,52},{24,56},{28,60},{32,6... | collective-permute-start | bytes 196616 | tf_op jit(solution)/shard_map/ppermute | solution.py:19
  68.3 11.6 %collective-permute-start.1 = (bf16[2,2,64,2,128]{4,3,2,1,0:T(2,128)(2,1)S(1)}, bf16[2,2,64,2,128]{4,3,2,1,0:T(2,128)(2,1)S(1)}, u32[]{:S(2)}, u32[]{:S(2)}) collective-permute-start(bf16[2,2,64,2,128]{4,3,2,1,0:T(2,128)(2,1)S(1)} %pad_maximum_fusion.3), channel_id=1, source_target_pairs={{0,16},{4,20},{8,24},{12,28},{16,32},{20,36},{24,40},{28,44},{32,4... | collective-permute-start | bytes 393224 | tf_op jit(solution)/shard_map/ppermute | solution.py:19
  80.3 10.6 %collective-permute-start.2 = (bf16[4,2,64,2,128]{4,3,2,1,0:T(2,128)(2,1)S(1)}, bf16[4,2,64,2,128]{4,3,2,1,0:T(2,128)(2,1)S(1)}, u32[]{:S(2)}, u32[]{:S(2)}) collective-permute-start(bf16[4,2,64,2,128]{4,3,2,1,0:T(2,128)(2,1)S(1)} %pad_maximum_fusion.2), channel_id=1, source_target_pairs={{0,64},{4,68},{8,72},{12,76},{16,80},{20,84},{24,88},{28,92},{32,9... | collective-permute-start | bytes 786440 | tf_op jit(solution)/shard_map/ppermute | solution.py:19
  91.7 15.0 %collective-permute-start.3 = (bf16[8,2,64,2,128]{4,3,2,1,0:T(2,128)(2,1)S(1)}, bf16[8,2,64,2,128]{4,3,2,1,0:T(2,128)(2,1)S(1)}, u32[]{:S(2)}, u32[]{:S(2)}) collective-permute-start(bf16[8,2,64,2,128]{4,3,2,1,0:T(2,128)(2,1)S(1)} %pad_maximum_fusion.1), channel_id=1, source_target_pairs={{0,8},{4,12},{8,16},{12,20},{16,24},{20,28},{24,32},{28,36},{32,40... | collective-permute-start | bytes 1572872 | tf_op jit(solution)/shard_map/ppermute | solution.py:19
  108.7 9.9 %copy-start.5 = (f32[2,512,1]{2,1,0:T(8,128)S(1)}, f32[2,512,1]{2,1,0:T(8,128)}, u32[]{:S(2)}) copy-start(f32[2,512,1]{2,1,0:T(8,128)} %get-tuple-element.49) | copy-start | bytes 12292
  108.7 10.3 %copy-start.6 = (f32[2,512,1]{2,1,0:T(8,128)S(1)}, f32[2,512,1]{2,1,0:T(8,128)}, u32[]{:S(2)}) copy-start(f32[2,512,1]{2,1,0:T(8,128)} %get-tuple-element.50) | copy-start | bytes 12292
  108.7 10.7 %copy-start.7 = (f32[2,512,1]{2,1,0:T(8,128)S(1)}, f32[2,512,1]{2,1,0:T(8,128)}, u32[]{:S(2)}) copy-start(f32[2,512,1]{2,1,0:T(8,128)} %get-tuple-element.51) | copy-start | bytes 12292
  108.7 18.6 %collective-permute-start.4 = (bf16[16,2,64,2,128]{4,3,2,1,0:T(2,128)(2,1)}, bf16[16,2,64,2,128]{4,3,2,1,0:T(2,128)(2,1)S(1)}, u32[]{:S(2)}, u32[]{:S(2)}) collective-permute-start(bf16[16,2,64,2,128]{4,3,2,1,0:T(2,128)(2,1)} %get-tuple-element.70), channel_id=1, source_target_pairs={{0,4},{4,8},{8,12},{12,16},{16,20},{20,24},{24,28},{28,32},{32,36}... | collective-permute-start | bytes 3145736 | tf_op jit(solution)/shard_map/ppermute | solution.py:19
  118.7 8.6 %copy-start.8 = (f32[2,512,1]{2,1,0:T(8,128)S(1)}, f32[2,512,1]{2,1,0:T(8,128)}, u32[]{:S(2)}) copy-start(f32[2,512,1]{2,1,0:T(8,128)} %get-tuple-element.52) | copy-start | bytes 12292
  118.9 10.7 %copy-start.10 = (bf16[32,2,16,128]{3,2,1,0:T(8,128)(2,1)S(1)}, bf16[32,2,16,128]{3,2,1,0:T(8,128)(2,1)}, u32[]{:S(2)}) copy-start(bf16[32,2,16,128]{3,2,1,0:T(8,128)(2,1)} %get-tuple-element.36) | copy-start | bytes 786436
  118.9 10.7 %copy-start.11 = (bf16[32,2,16,128]{3,2,1,0:T(8,128)(2,1)S(1)}, bf16[32,2,16,128]{3,2,1,0:T(8,128)(2,1)}, u32[]{:S(2)}) copy-start(bf16[32,2,16,128]{3,2,1,0:T(8,128)(2,1)} %get-tuple-element.40) | copy-start | bytes 786436
  119.3 10.3 %copy-start.12 = (bf16[32,2,16,128]{3,2,1,0:T(8,128)(2,1)S(1)}, bf16[32,2,16,128]{3,2,1,0:T(8,128)(2,1)}, u32[]{:S(2)}) copy-start(bf16[32,2,16,128]{3,2,1,0:T(8,128)(2,1)} %get-tuple-element.44) | copy-start | bytes 786436
  119.3 10.3 %copy-start.13 = (bf16[32,2,16,128]{3,2,1,0:T(8,128)(2,1)S(1)}, bf16[32,2,16,128]{3,2,1,0:T(8,128)(2,1)}, u32[]{:S(2)}) copy-start(bf16[32,2,16,128]{3,2,1,0:T(8,128)(2,1)} %get-tuple-element.48) | copy-start | bytes 786436
  134.0 44.2 %all-to-all-start.1 = ((bf16[128,2,2112]{2,1,0:T(2,128)(2,1)}), bf16[128,2,2112]{2,1,0:T(2,128)(2,1)S(1)}, u32[]{:S(2)}, u32[]{:S(2)}) async-start(bf16[128,2,2112]{2,1,0:T(2,128)(2,1)} %reshape.447), calls=%async_computation.1 | async-start | bytes 2228224 | tf_op jit(solution)/shard_map/all_to_all | solution.py:173
  187.6 0.8 copy-start.4
  188.0 1.3 copy-start.9

commit v2 on v1

--- a/solution.py
+++ b/solution.py
@@ -130,9 +130,9 @@
 
     def serve_piece(piece):
         return attend(
-            arrived,
+            arrived[piece * sources_per_tile : (piece + 1) * sources_per_tile],
             (sources_per_tile, None, slab, head_dim),
-            lambda h, i: (piece, h, 0, 0),
+            lambda h, i: (0, h, 0, 0),
             kv_heads,
             1,
             cache_keys,
@@ -140,8 +140,6 @@
             jnp.bfloat16,
             scaling,
             group_size,
-            out_rows=sources_per_tile,
-            out_map=lambda h, i: (0, h, 0, 0),
         )
 
     window, offsets, served_pieces = gather_window(
@@ -173,11 +171,9 @@
     returned = lax.all_to_all(payload, "seq", split_axis=0, concat_axis=0, tiled=True)
     answers = returned[:, :payload_width].reshape(seq_count, kv_heads, capacity, group_size * head_dim)
     lse_parts = returned[:, payload_width : payload_width + lse_width].reshape(
-        seq_count, kv_heads, 2 * slab
-    ).astype(jnp.float32)
-    answer_lse = (lse_parts[:, :, :slab] + lse_parts[:, :, slab:]).reshape(
-        seq_count, kv_heads, capacity, group_size
-    )
+        seq_count, kv_heads, 2, capacity, group_size
+    )
+    lse_parts = jnp.swapaxes(lse_parts, 2, 3).reshape(seq_count, kv_heads, capacity, 2 * group_size)
     window_keys = jnp.transpose(window[:, 0], (2, 0, 1, 3)).reshape(kv_heads, blocks * rows_local, head_dim)
     window_values = jnp.transpose(window[:, 1], (2, 0, 1, 3)).reshape(kv_heads, blocks * rows_local, head_dim)
     key_index = jnp.arange(blocks * rows_local, dtype=jnp.int32)
@@ -213,7 +209,10 @@
         )
         .reshape(kv_heads, rows_local, top_count, group_size, head_dim)
     )
-    picked_lse = answer_lse[targets, head_rows, places].reshape(
+    picked_parts = jnp.einsum(
+        "htcr,thcx->hrx", one_hot, lse_parts, preferred_element_type=jnp.float32
+    )
+    picked_lse = (picked_parts[..., :group_size] + picked_parts[..., group_size:]).reshape(
         kv_heads, rows_local, top_count, group_size
     )
     ceiling = jnp.maximum(own_lse, jnp.max(picked_lse, axis=2))

time: 202 us -> 198 us (0.980)
  blocking collectives: 59.5 us -> 10.8 us
  waiting for transfers between devices: 29 us -> 58.4 us
  starting transfers between devices: 25.8 us -> 43.7 us
  local copies, waits for them, and re-layouts: 36.8 us -> 34.4 us
    all_to_all x1 -> x0, blocking collectives: 48.7 us -> none  [per_device(): lax.all_to_all(outgoing, 'seq', split_axis=0, concat_axis=0, tiled=True)]
    all_to_all x0 -> x1, waiting for transfers between devices: none -> 28.6 us  [per_device(): lax.all_to_all(outgoing, 'seq', split_axis=0, concat_axis=0, tiled=True)]
    all_to_all x0 -> x1, starting transfers between devices: none -> 17.4 us  [per_device(): lax.all_to_all(outgoing, 'seq', split_axis=0, concat_axis=0, tiled=True)]
    gather x1 -> x0, local copies, waits for them, and re-layouts: 4.52 us -> none  [per_device(): answer_lse[targets, head_rows, places]]
    unnamed x38 -> x34, local copies, waits for them, and re-layouts: 9.6 us -> 9.18 us
  transfers between devices with their start and end apart: 6 -> 7, of which waited for: 4 -> 6; matrix products, arithmetic and copies ran while one was open for 9% -> 10% of each run, Pallas kernels for 19% -> 20%
where the time goes in v2:
time: 198 us
  waiting for transfers between devices  58.4 us (29%)
  starting transfers between devices  43.7 us (22%)
  Pallas kernels  38.7 us (20%)
  local copies, waits for them, and re-layouts  34.4 us (17%)
  blocking collectives  10.8 us (5%)
  other arithmetic  9.93 us (5%)
    pallas_call x5, Pallas kernels, attend(): pl.pallas_call(functools.partial(attend_kernel, thr is not None, scaling,...  38.7 us
    all_to_all x1, waiting for transfers between devices, per_device(): lax.all_to_all(outgoing, 'seq', split_axis=0, concat_axis=0, tiled=True)  28.6 us
    all_to_all x1, starting transfers between devices, per_device(): lax.all_to_all(outgoing, 'seq', split_axis=0, concat_axis=0, tiled=True)  17.4 us
    all_to_all x1, waiting for transfers between devices, per_device(): lax.all_to_all(payload, 'seq', split_axis=0, concat_axis=0, tiled=True)  15.5 us
    ppermute x5, waiting for transfers between devices, shifted(): lax.ppermute(value, axis, [(source, source + steps) for source in range(i...  14.2 us
    ppermute x5, starting transfers between devices, shifted(): lax.ppermute(value, axis, [(source, source + steps) for source in range(i...  14.2 us
    all_to_all x1, starting transfers between devices, per_device(): lax.all_to_all(payload, 'seq', split_axis=0, concat_axis=0, tiled=True)  12.1 us
    all_to_all x1, blocking collectives, per_device(): lax.all_to_all(heads_out, 'kvh', split_axis=0, concat_axis=1, tiled=True)  10.8 us
  transfers between devices with their start and end apart: 7, of which 6 were waited for; matrix products, arithmetic and copies ran while one was open for 10% of the time, Pallas kernels for 20%

profile of v2, /device:TPU:8, one launch (start us, length us, event | category | flops | bytes accessed | tf_op | source)
XLA Modules:
  0.0 197.7 jit_solution(9291460183314178218)
XLA Ops:
  0.0 0.7 compare_select_fusion.7
  0.9 0.2 reshape.274
  1.1 2.7 %gather_fusion = s32[384]{0:T(512)S(1)} fusion(s32[128]{0:T(128)S(1)} %copy-done.1, s32[1024]{0:T(1024)S(1)} %pad_clamp_fusion), kind=kCustom, calls=%fused_computation | custom fusion | bytes 4608 | tf_op jit(solution)/shard_map/gather | solution.py:105
  4.0 0.2 fusion.12
  4.4 0.2 fusion.16
  4.7 0.8 copy_bitcast_fusion.3
  5.6 0.3 reshape.360
  5.9 0.6 fusion.1
  6.5 1.1 copy.110
  7.6 1.5 reshape.216
  9.1 17.4 %all-to-all-start = ((bf16[128,2,16,128]{3,2,1,0:T(8,128)(2,1)}), bf16[128,2,16,128]{3,2,1,0:T(8,128)(2,1)S(1)}, u32[]{:S(2)}, u32[]{:S(2)}) async-start(bf16[128,2,16,128]{3,2,1,0:T(8,128)(2,1)} %reshape.216), calls=%async_computation | async-start | bytes 2097152 | tf_op jit(solution)/shard_map/all_to_all | solution.py:124
  26.5 2.7 %fusion.28 = (bf16[1,1,2048,2,128]{4,3,2,1,0:T(2,128)(2,1)S(1)}, bf16[1,1,2048,2,128]{4,3,2,1,0:T(2,128)(2,1)S(1)}) fusion(bf16[2,1,2048,2,128]{4,3,2,1,0:T(2,128)(2,1)} %param.8), kind=kLoop, calls=%fused_computation.115 | loop fusion | bytes 4194304 | tf_op jit(solution)/shard_map/slice | solution.py:127
  29.2 28.6 %all-to-all-done = bf16[128,2,16,128]{3,2,1,0:T(8,128)(2,1)S(1)} async-done(((bf16[128,2,16,128]{3,2,1,0:T(8,128)(2,1)}), bf16[128,2,16,128]{3,2,1,0:T(8,128)(2,1)S(1)}, u32[]{:S(2)}, u32[]{:S(2)}) %all-to-all-start) | async-done | bytes 1048608 | tf_op jit(solution)/shard_map/all_to_all | solution.py:124
  57.8 3.3 %collective-permute-start = (bf16[1,2,64,2,128]{4,3,2,1,0:T(2,128)(2,1)S(1)}, bf16[1,2,64,2,128]{4,3,2,1,0:T(2,128)(2,1)S(1)}, u32[]{:S(2)}, u32[]{:S(2)}) collective-permute-start(bf16[1,2,64,2,128]{4,3,2,1,0:T(2,128)(2,1)S(1)} %bitcast.102), channel_id=1, source_target_pairs={{0,32},{4,36},{8,40},{12,44},{16,48},{20,52},{24,56},{28,60},{32,6... | collective-permute-start | bytes 196616 | tf_op jit(solution)/shard_map/ppermute | solution.py:19
  61.1 1.6 copy_bitcast_fusion.1
  62.7 6.1 %collective-permute-done = bf16[1,2,64,2,128]{4,3,2,1,0:T(2,128)(2,1)S(1)} collective-permute-done((bf16[1,2,64,2,128]{4,3,2,1,0:T(2,128)(2,1)S(1)}, bf16[1,2,64,2,128]{4,3,2,1,0:T(2,128)(2,1)S(1)}, u32[]{:S(2)}, u32[]{:S(2)}) %collective-permute-start) | collective-permute-done | bytes 65568 | tf_op jit(solution)/shard_map/ppermute | solution.py:19
  68.9 0.2 pad_maximum_fusion.3
  69.0 2.4 %collective-permute-start.1 = (bf16[2,2,64,2,128]{4,3,2,1,0:T(2,128)(2,1)S(1)}, bf16[2,2,64,2,128]{4,3,2,1,0:T(2,128)(2,1)S(1)}, u32[]{:S(2)}, u32[]{:S(2)}) collective-permute-start(bf16[2,2,64,2,128]{4,3,2,1,0:T(2,128)(2,1)S(1)} %pad_maximum_fusion.3), channel_id=1, source_target_pairs={{0,16},{4,20},{8,24},{12,28},{16,32},{20,36},{24,40},{28,44},{32,4... | collective-permute-start | bytes 393224 | tf_op jit(solution)/shard_map/ppermute | solution.py:19
  71.4 1.0 fusion.29
  72.4 7.6 %shard_map.64 = (bf16[32,2,16,128]{3,2,1,0:T(8,128)(2,1)}, f32[2,512,1]{2,1,0:T(8,128)}) custom-call(bf16[32,2,16,128]{3,2,1,0:T(8,128)(2,1)} %get-tuple-element.72.refs_0_, bf16[2,2048,128]{2,1,0:T(8,128)(2,1)} %get-tuple-element.88.refs_1_, bf16[2,2048,128]{2,1,0:T(8,128)(2,1)} %get-tuple-element.87.refs_2_), custom_call_target="tpu_custom_call" | custom-call | flops 1073741824 | bytes 2621440 | tf_op jit(solution)/shard_map/pallas_call | solution.py:77
  80.2 0.4 pad_maximum_fusion.2
  80.6 2.8 %collective-permute-start.2 = (bf16[4,2,64,2,128]{4,3,2,1,0:T(2,128)(2,1)S(1)}, bf16[4,2,64,2,128]{4,3,2,1,0:T(2,128)(2,1)S(1)}, u32[]{:S(2)}, u32[]{:S(2)}) collective-permute-start(bf16[4,2,64,2,128]{4,3,2,1,0:T(2,128)(2,1)S(1)} %pad_maximum_fusion.2), channel_id=1, source_target_pairs={{0,64},{4,68},{8,72},{12,76},{16,80},{20,84},{24,88},{28,92},{32,9... | collective-permute-start | bytes 786440 | tf_op jit(solution)/shard_map/ppermute | solution.py:19
  83.4 7.6 %shard_map.65 = (bf16[32,2,16,128]{3,2,1,0:T(8,128)(2,1)}, f32[2,512,1]{2,1,0:T(8,128)}) custom-call(bf16[32,2,16,128]{3,2,1,0:T(8,128)(2,1)} %get-tuple-element.71.refs_0_, bf16[2,2048,128]{2,1,0:T(8,128)(2,1)} %get-tuple-element.88.refs_1_, bf16[2,2048,128]{2,1,0:T(8,128)(2,1)} %get-tuple-element.87.refs_2_), custom_call_target="tpu_custom_call" | custom-call | flops 1073741824 | bytes 2621440 | tf_op jit(solution)/shard_map/pallas_call | solution.py:77
  91.0 0.7 pad_maximum_fusion.1
  91.8 3.4 %collective-permute-start.3 = (bf16[8,2,64,2,128]{4,3,2,1,0:T(2,128)(2,1)S(1)}, bf16[8,2,64,2,128]{4,3,2,1,0:T(2,128)(2,1)S(1)}, u32[]{:S(2)}, u32[]{:S(2)}) collective-permute-start(bf16[8,2,64,2,128]{4,3,2,1,0:T(2,128)(2,1)S(1)} %pad_maximum_fusion.1), channel_id=1, source_target_pairs={{0,8},{4,12},{8,16},{12,20},{16,24},{20,28},{24,32},{28,36},{32,40... | collective-permute-start | bytes 1572872 | tf_op jit(solution)/shard_map/ppermute | solution.py:19
  95.2 0.7 constant_dynamic-update-slice_fusion.10
  95.9 7.6 %shard_map.66 = (bf16[32,2,16,128]{3,2,1,0:T(8,128)(2,1)}, f32[2,512,1]{2,1,0:T(8,128)}) custom-call(bf16[32,2,16,128]{3,2,1,0:T(8,128)(2,1)} %get-tuple-element.70.refs_0_, bf16[2,2048,128]{2,1,0:T(8,128)(2,1)} %get-tuple-element.88.refs_1_, bf16[2,2048,128]{2,1,0:T(8,128)(2,1)} %get-tuple-element.87.refs_2_), custom_call_target="tpu_custom_call" | custom-call | flops 1073741824 | bytes 2621440 | tf_op jit(solution)/shard_map/pallas_call | solution.py:77
  103.5 0.7 constant_dynamic-update-slice_fusion.9
  104.2 0.8 constant_dynamic-update-slice_fusion.8
  105.0 1.2 constant_dynamic-update-slice_fusion.7
  106.3 0.6 collective-permute-done.3
  106.8 2.0 constant_dynamic-update-slice_fusion.6
  108.8 2.3 %collective-permute-start.4 = (bf16[16,2,64,2,128]{4,3,2,1,0:T(2,128)(2,1)}, bf16[16,2,64,2,128]{4,3,2,1,0:T(2,128)(2,1)S(1)}, u32[]{:S(2)}, u32[]{:S(2)}) collective-permute-start(bf16[16,2,64,2,128]{4,3,2,1,0:T(2,128)(2,1)} %get-tuple-element.74), channel_id=1, source_target_pairs={{0,4},{4,8},{8,12},{12,16},{16,20},{20,24},{24,28},{28,32},{32,36}... | collective-permute-start | bytes 3145736 | tf_op jit(solution)/shard_map/ppermute | solution.py:19
  111.1 7.7 %shard_map.67 = (bf16[32,2,16,128]{3,2,1,0:T(8,128)(2,1)}, f32[2,512,1]{2,1,0:T(8,128)}) custom-call(bf16[32,2,16,128]{3,2,1,0:T(8,128)(2,1)} %get-tuple-element.69.refs_0_, bf16[2,2048,128]{2,1,0:T(8,128)(2,1)} %get-tuple-element.88.refs_1_, bf16[2,2048,128]{2,1,0:T(8,128)(2,1)} %get-tuple-element.87.refs_2_), custom_call_target="tpu_custom_call" | custom-call | flops 1073741824 | bytes 2621440 | tf_op jit(solution)/shard_map/pallas_call | solution.py:77
  118.8 0.2 reduce.25
  119.2 0.2 reduce.26
  119.6 0.2 reduce.27
  119.9 7.4 %collective-permute-done.4 = bf16[16,2,64,2,128]{4,3,2,1,0:T(2,128)(2,1)S(1)} collective-permute-done((bf16[16,2,64,2,128]{4,3,2,1,0:T(2,128)(2,1)}, bf16[16,2,64,2,128]{4,3,2,1,0:T(2,128)(2,1)S(1)}, u32[]{:S(2)}, u32[]{:S(2)}) %collective-permute-start.4) | collective-permute-done | bytes 1048608 | tf_op jit(solution)/shard_map/ppermute | solution.py:19
  127.3 0.2 reduce.28
  127.7 1.9 constant_dynamic-update-slice_fusion.5
  129.9 0.5 copy.156
  130.5 0.5 broadcast.489
  131.1 1.4 reduce.55
  132.4 1.6 reshape.394
  134.0 12.1 %all-to-all-start.1 = ((bf16[128,2,2112]{2,1,0:T(2,128)(2,1)}), bf16[128,2,2112]{2,1,0:T(2,128)(2,1)S(1)}, u32[]{:S(2)}, u32[]{:S(2)}) async-start(bf16[128,2,2112]{2,1,0:T(2,128)(2,1)} %reshape.394), calls=%async_computation.1 | async-start | bytes 2228224 | tf_op jit(solution)/shard_map/all_to_all | solution.py:171
  147.3 0.3 compare_reduce_fusion
  147.7 0.6 reshape_select_fusion.1.refs_0_
  148.3 2.9 %slice_bitcast_fusion = (bf16[2,32,64,128]{3,0,2,1:T(2,128)(2,1)S(1)}, bf16[2,32,64,128]{3,0,2,1:T(2,128)(2,1)S(1)}) fusion(bf16[32,2,64,2,128]{4,3,2,1,0:T(2,128)(2,1)} %constant_dynamic-update-slice_fusion.5), kind=kLoop, calls=%fused_computation.13 | loop fusion | bytes 4194304 | tf_op jit(solution)/shard_map/transpose | solution.py:178
  151.3 1.3 copy.118
  152.6 1.3 copy.117
  153.8 8.1 %shard_map.68 = (f32[2,512,128]{2,1,0:T(8,128)}, f32[2,512,1]{2,1,0:T(8,128)}) custom-call(s32[1,2048]{1,0:T(1,128)} %reshape_select_fusion.1.refs_0_, bf16[2,512,128]{2,1,0:T(8,128)(2,1)} %get-tuple-element.75.refs_1_, bf16[2,2048,128]{2,1,0:T(8,128)(2,1)} %bitcast.99, bf16[2,2048,128]{2,1,0:T(8,128)(2,1)} %bitcast.98), custom_call_target="tpu_custom_call" | custom-call | flops 1073741824 | bytes 2621440 | tf_op jit(solution)/shard_map/pallas_call | solution.py:77
  161.9 1.2 reduce.29
  163.4 15.5 %all-to-all-done.1 = bf16[128,2,2112]{2,1,0:T(2,128)(2,1)S(1)} async-done(((bf16[128,2,2112]{2,1,0:T(2,128)(2,1)}), bf16[128,2,2112]{2,1,0:T(2,128)(2,1)S(1)}, u32[]{:S(2)}, u32[]{:S(2)}) %all-to-all-start.1) | async-done | bytes 1081376 | tf_op jit(solution)/shard_map/all_to_all | solution.py:171
  178.9 1.2 reshape.395
  180.1 2.7 %copy.121 = bf16[128,1,4224]{0,2,1:T(8,128)(2,1)S(1)} copy(bf16[128,1,4224]{2,1,0:T(2,128)(2,1)S(1)} %reshape.395) | data formatting | bytes 2162688 | tf_op jit(solution)/shard_map/all_to_all | solution.py:171
  182.9 0.2 convolution_bitcast_fusion
  183.2 0.2 copy.123
  183.6 0.5 fusion.5
  184.1 0.3 copy.144
  184.5 0.2 fusion.27
  185.1 0.5 multiply_reduce_fusion
  185.7 0.4 fusion.14
  186.2 10.8 %all_to_all.36 = bf16[4,16,2048]{2,1,0:T(8,128)(2,1)S(1)} all-to-all(bf16[4,16,2048]{2,1,0:T(8,128)(2,1)S(1)} %all_to_all.29), channel_id=1, replica_groups=mesh['seq'=128,'kvh'=4] {'kvh'}, dimensions={0} | all-to-all | bytes 524288 | tf_op jit(solution)/shard_map/all_to_all | solution.py:230
  197.0 0.7 copy.142
  (96 shorter events, 4.1 us)
Async XLA Ops:
  0.0 4.7 %copy-start = (bf16[64,16,128]{2,1,0:T(8,128)(2,1)S(1)}, bf16[64,16,128]{2,1,0:T(8,128)(2,1)}, u32[]{:S(2)}) copy-start(bf16[64,16,128]{2,1,0:T(8,128)(2,1)} %param.6) | copy-start | bytes 786436
  0.0 1.1 copy-start.1
  9.1 48.7 %all-to-all-start = ((bf16[128,2,16,128]{3,2,1,0:T(8,128)(2,1)}), bf16[128,2,16,128]{3,2,1,0:T(8,128)(2,1)S(1)}, u32[]{:S(2)}, u32[]{:S(2)}) async-start(bf16[128,2,16,128]{3,2,1,0:T(8,128)(2,1)} %reshape.216), calls=%async_computation | async-start | bytes 2097152 | tf_op jit(solution)/shard_map/all_to_all | solution.py:124
  26.5 31.3 %copy-start.2 = (bf16[2,64,2,128]{3,2,1,0:T(2,128)(2,1)S(1)}, bf16[2,64,2,128]{3,2,1,0:T(2,128)(2,1)}, u32[]{:S(2)}) copy-start(bf16[2,64,2,128]{3,2,1,0:T(2,128)(2,1)} %param.7) | copy-start | bytes 196612
  57.8 11.0 %collective-permute-start = (bf16[1,2,64,2,128]{4,3,2,1,0:T(2,128)(2,1)S(1)}, bf16[1,2,64,2,128]{4,3,2,1,0:T(2,128)(2,1)S(1)}, u32[]{:S(2)}, u32[]{:S(2)}) collective-permute-start(bf16[1,2,64,2,128]{4,3,2,1,0:T(2,128)(2,1)S(1)} %bitcast.102), channel_id=1, source_target_pairs={{0,32},{4,36},{8,40},{12,44},{16,48},{20,52},{24,56},{28,60},{32,6... | collective-permute-start | bytes 196616 | tf_op jit(solution)/shard_map/ppermute | solution.py:19
  69.0 11.1 %collective-permute-start.1 = (bf16[2,2,64,2,128]{4,3,2,1,0:T(2,128)(2,1)S(1)}, bf16[2,2,64,2,128]{4,3,2,1,0:T(2,128)(2,1)S(1)}, u32[]{:S(2)}, u32[]{:S(2)}) collective-permute-start(bf16[2,2,64,2,128]{4,3,2,1,0:T(2,128)(2,1)S(1)} %pad_maximum_fusion.3), channel_id=1, source_target_pairs={{0,16},{4,20},{8,24},{12,28},{16,32},{20,36},{24,40},{28,44},{32,4... | collective-permute-start | bytes 393224 | tf_op jit(solution)/shard_map/ppermute | solution.py:19
  80.6 10.5 %collective-permute-start.2 = (bf16[4,2,64,2,128]{4,3,2,1,0:T(2,128)(2,1)S(1)}, bf16[4,2,64,2,128]{4,3,2,1,0:T(2,128)(2,1)S(1)}, u32[]{:S(2)}, u32[]{:S(2)}) collective-permute-start(bf16[4,2,64,2,128]{4,3,2,1,0:T(2,128)(2,1)S(1)} %pad_maximum_fusion.2), channel_id=1, source_target_pairs={{0,64},{4,68},{8,72},{12,76},{16,80},{20,84},{24,88},{28,92},{32,9... | collective-permute-start | bytes 786440 | tf_op jit(solution)/shard_map/ppermute | solution.py:19
  91.8 15.0 %collective-permute-start.3 = (bf16[8,2,64,2,128]{4,3,2,1,0:T(2,128)(2,1)S(1)}, bf16[8,2,64,2,128]{4,3,2,1,0:T(2,128)(2,1)S(1)}, u32[]{:S(2)}, u32[]{:S(2)}) collective-permute-start(bf16[8,2,64,2,128]{4,3,2,1,0:T(2,128)(2,1)S(1)} %pad_maximum_fusion.1), channel_id=1, source_target_pairs={{0,8},{4,12},{8,16},{12,20},{16,24},{20,28},{24,32},{28,36},{32,40... | collective-permute-start | bytes 1572872 | tf_op jit(solution)/shard_map/ppermute | solution.py:19
  108.8 10.0 %copy-start.3 = (f32[2,512,1]{2,1,0:T(8,128)S(1)}, f32[2,512,1]{2,1,0:T(8,128)}, u32[]{:S(2)}) copy-start(f32[2,512,1]{2,1,0:T(8,128)} %get-tuple-element.49) | copy-start | bytes 12292
  108.8 18.6 %collective-permute-start.4 = (bf16[16,2,64,2,128]{4,3,2,1,0:T(2,128)(2,1)}, bf16[16,2,64,2,128]{4,3,2,1,0:T(2,128)(2,1)S(1)}, u32[]{:S(2)}, u32[]{:S(2)}) collective-permute-start(bf16[16,2,64,2,128]{4,3,2,1,0:T(2,128)(2,1)} %get-tuple-element.74), channel_id=1, source_target_pairs={{0,4},{4,8},{8,12},{12,16},{16,20},{20,24},{24,28},{28,32},{32,36}... | collective-permute-start | bytes 3145736 | tf_op jit(solution)/shard_map/ppermute | solution.py:19
  111.0 8.1 %copy-start.4 = (f32[2,512,1]{2,1,0:T(8,128)S(1)}, f32[2,512,1]{2,1,0:T(8,128)}, u32[]{:S(2)}) copy-start(f32[2,512,1]{2,1,0:T(8,128)} %get-tuple-element.50) | copy-start | bytes 12292
  111.1 8.5 %copy-start.5 = (f32[2,512,1]{2,1,0:T(8,128)S(1)}, f32[2,512,1]{2,1,0:T(8,128)}, u32[]{:S(2)}) copy-start(f32[2,512,1]{2,1,0:T(8,128)} %get-tuple-element.51) | copy-start | bytes 12292
  118.8 8.6 %copy-start.6 = (f32[2,512,1]{2,1,0:T(8,128)S(1)}, f32[2,512,1]{2,1,0:T(8,128)}, u32[]{:S(2)}) copy-start(f32[2,512,1]{2,1,0:T(8,128)} %get-tuple-element.52) | copy-start | bytes 12292
  119.0 10.6 %copy-start.8 = (bf16[32,2,16,128]{3,2,1,0:T(8,128)(2,1)S(1)}, bf16[32,2,16,128]{3,2,1,0:T(8,128)(2,1)}, u32[]{:S(2)}) copy-start(bf16[32,2,16,128]{3,2,1,0:T(8,128)(2,1)} %get-tuple-element.36) | copy-start | bytes 786436
  119.0 10.6 %copy-start.9 = (bf16[32,2,16,128]{3,2,1,0:T(8,128)(2,1)S(1)}, bf16[32,2,16,128]{3,2,1,0:T(8,128)(2,1)}, u32[]{:S(2)}) copy-start(bf16[32,2,16,128]{3,2,1,0:T(8,128)(2,1)} %get-tuple-element.40) | copy-start | bytes 786436
  119.4 10.2 %copy-start.10 = (bf16[32,2,16,128]{3,2,1,0:T(8,128)(2,1)S(1)}, bf16[32,2,16,128]{3,2,1,0:T(8,128)(2,1)}, u32[]{:S(2)}) copy-start(bf16[32,2,16,128]{3,2,1,0:T(8,128)(2,1)} %get-tuple-element.44) | copy-start | bytes 786436
  119.4 10.2 %copy-start.11 = (bf16[32,2,16,128]{3,2,1,0:T(8,128)(2,1)S(1)}, bf16[32,2,16,128]{3,2,1,0:T(8,128)(2,1)}, u32[]{:S(2)}) copy-start(bf16[32,2,16,128]{3,2,1,0:T(8,128)(2,1)} %get-tuple-element.48) | copy-start | bytes 786436
  134.0 44.9 %all-to-all-start.1 = ((bf16[128,2,2112]{2,1,0:T(2,128)(2,1)}), bf16[128,2,2112]{2,1,0:T(2,128)(2,1)S(1)}, u32[]{:S(2)}, u32[]{:S(2)}) async-start(bf16[128,2,2112]{2,1,0:T(2,128)(2,1)} %reshape.394), calls=%async_computation.1 | async-start | bytes 2228224 | tf_op jit(solution)/shard_map/all_to_all | solution.py:171
  184.4 1.2 copy-start.7

commit v3 on v2

--- a/solution.py
+++ b/solution.py
@@ -5,34 +5,18 @@
 import jax.numpy as jnp
 from jax import lax
 from jax.experimental import pallas as pl
-from jax.sharding import PartitionSpec as P
+from jax.sharding import Mesh, PartitionSpec as P
 
 BLOCK_TOKENS = 2048
+STRETCH_TOKENS = 8192
+SEQ = ("seq_group", "seq_slot")
 BLOCK_PICK_LIMIT = 2
-WINDOW_SHIFTS = (8, 4, 16, 2, 1)
 LOG2_E = 1.4426950408889634
 
 
-def shifted(value, axis, steps):
-    count = lax.axis_size(axis)
+def shifted(value, axis, steps, count):
     initial, last = (max(0, -steps), min(count, count - steps))
     return lax.ppermute(value, axis, [(source, source + steps) for source in range(initial, last)])
-
-
-def gather_window(stretch_kv, span_devices, companions):
-    stack = stretch_kv[None]
-    offsets = [0]
-    results = []
-    for index, step in enumerate(WINDOW_SHIFTS):
-        if len(offsets) >= span_devices:
-            break
-        arrived = shifted(stack, "seq", step)
-        if index < len(companions) and companions[index] is not None:
-            arrived, done = lax.optimization_barrier((arrived, companions[index]()))
-            results.append(done)
-        stack = jnp.concatenate([stack, arrived], axis=0)
-        offsets = offsets + [o + step for o in offsets]
-    return stack, offsets, results
 
 
 def attend_kernel(masked, scaling, group_size, *refs):
@@ -96,10 +80,12 @@
     group_size = query_heads // kv_heads
     top_count = selection.shape[2]
     scaling = 1.0 / math.sqrt(head_dim)
-    seq_count = lax.axis_size("seq")
+    group_count, window_group = lax.axis_size("seq_group"), lax.axis_size("seq_slot")
+    seq_count = group_count * window_group
     capacity = BLOCK_PICK_LIMIT
     span_devices = min(BLOCK_TOKENS // rows_local, seq_count)
-    seq_place = lax.axis_index("seq")
+    slot_place = lax.axis_index("seq_slot")
+    seq_place = lax.axis_index("seq_group") * window_group + slot_place
     grouped = queries.reshape(rows_local, kv_heads, group_size, head_dim)
     requests = rows_local * top_count
     targets = block_owner[selection].reshape(kv_heads, requests)
@@ -121,39 +107,30 @@
     ).astype(jnp.bfloat16)
     slab = capacity * group_size
     outgoing = outgoing.reshape(seq_count, kv_heads, slab, head_dim)
-    arrived = lax.all_to_all(outgoing, "seq", split_axis=0, concat_axis=0, tiled=True)
-    arrived, window_start = lax.optimization_barrier((arrived, stretch_kv))
+    arrived = lax.all_to_all(outgoing, SEQ, split_axis=0, concat_axis=0, tiled=True)
+    earlier = shifted(stretch_kv, SEQ, window_group, seq_count)
+    gathered_earlier = lax.all_gather(earlier, "seq_slot", axis=0, tiled=False)
+    gathered_own = lax.all_gather(stretch_kv, "seq_slot", axis=0, tiled=False)
     cache_keys = jnp.swapaxes(cache_kv[0, 0], 0, 1)
     cache_values = jnp.swapaxes(cache_kv[1, 0], 0, 1)
     sources_per_tile = 32
-    pieces = seq_count // sources_per_tile
-
-    def serve_piece(piece):
-        return attend(
-            arrived[piece * sources_per_tile : (piece + 1) * sources_per_tile],
-            (sources_per_tile, None, slab, head_dim),
-            lambda h, i: (0, h, 0, 0),
-            kv_heads,
-            1,
-            cache_keys,
-            cache_values,
-            jnp.bfloat16,
-            scaling,
-            group_size,
-        )
-
-    window, offsets, served_pieces = gather_window(
-        window_start,
-        span_devices,
-        [None] + [functools.partial(serve_piece, piece) for piece in range(pieces)],
-    )
+    served, served_lse = attend(
+        arrived,
+        (sources_per_tile, None, slab, head_dim),
+        lambda h, i: (i, h, 0, 0),
+        kv_heads,
+        seq_count // sources_per_tile,
+        cache_keys,
+        cache_values,
+        jnp.bfloat16,
+        scaling,
+        group_size,
+    )
+    served_lse = jnp.swapaxes(served_lse.reshape(kv_heads, seq_count, slab), 0, 1)
+    both = jnp.concatenate([gathered_earlier, gathered_own], axis=0)
+    window = lax.dynamic_slice_in_dim(both, slot_place + window_group - span_devices + 1, span_devices, 0)
+    offsets = [span_devices - 1 - p for p in range(span_devices)]
     blocks = window.shape[0]
-    served = jnp.concatenate([piece[0] for piece in served_pieces], axis=0)
-    served_lse = jnp.concatenate(
-        [piece[1].reshape(kv_heads, sources_per_tile, slab) for piece in served_pieces], axis=1
-    )
-    served_lse = jnp.swapaxes(served_lse, 0, 1)
-    served, served_lse, window = lax.optimization_barrier((served, served_lse, window))
     lse_rounded = lax.reduce_precision(served_lse, exponent_bits=8, mantissa_bits=7)
     lse_high = lse_rounded.astype(jnp.bfloat16)
     lse_low = (served_lse - lse_rounded).astype(jnp.bfloat16)
@@ -168,7 +145,7 @@
         ],
         axis=1,
     )
-    returned = lax.all_to_all(payload, "seq", split_axis=0, concat_axis=0, tiled=True)
+    returned = lax.all_to_all(payload, SEQ, split_axis=0, concat_axis=0, tiled=True)
     answers = returned[:, :payload_width].reshape(seq_count, kv_heads, capacity, group_size * head_dim)
     lse_parts = returned[:, payload_width : payload_width + lse_width].reshape(
         seq_count, kv_heads, 2, capacity, group_size
@@ -231,13 +208,23 @@
 
 
 def solution(mesh):
+    seq_total, kvh_total = mesh.devices.shape
+    window_group = min(BLOCK_TOKENS // (STRETCH_TOKENS // seq_total), seq_total)
+    split_mesh = Mesh(
+        mesh.devices.reshape(seq_total // window_group, window_group, kvh_total),
+        ("seq_group", "seq_slot", "kvh"),
+    )
     placed = (
-        P("seq", "kvh", None),
-        P(None, "seq", "kvh", None),
-        P(None, "seq", None, "kvh", None),
-        P("kvh", "seq", None),
+        P(SEQ, "kvh", None),
+        P(None, SEQ, "kvh", None),
+        P(None, SEQ, None, "kvh", None),
+        P("kvh", SEQ, None),
         P(),
     )
     return jax.shard_map(
-        per_device, mesh=mesh, in_specs=placed, out_specs=P(("seq", "kvh"), None), check_vma=False
-    )
+        per_device,
+        mesh=split_mesh,
+        in_specs=placed,
+        out_specs=P(SEQ + ("kvh",), None),
+        check_vma=False,
+    )

time: 198 us -> 226 us (1.14)
  the two profiles are of different devices: /device:TPU:8 before, /device:TPU:48 now
where the time goes in v3:
time: 226 us
  waiting for transfers between devices  100 us (44%)
  Pallas kernels  32.7 us (14%)
  starting transfers between devices  28.7 us (13%)
  local copies, waits for them, and re-layouts  26.1 us (12%)
  between operations  13.8 us (6%)
  other arithmetic  11.8 us (5%)
  blocking collectives  11.3 us (5%)
    all_gather x1, waiting for transfers between devices, per_device(): gathered_earlier = lax.all_gather(earlier, 'seq_slot', axis=0, tiled=False)  71.6 us
    pallas_call x2, Pallas kernels, attend(): pl.pallas_call(functools.partial(attend_kernel, thr is not None, scaling,...  32.7 us
    ppermute x1, waiting for transfers between devices, shifted(): lax.ppermute(value, axis, [(source, source + steps) for source in range(i...  28.6 us
    all_to_all x1, starting transfers between devices, per_device(): lax.all_to_all(outgoing, SEQ, split_axis=0, concat_axis=0, tiled=True)  17.3 us
    all_to_all x1, blocking collectives, per_device(): lax.all_to_all(heads_out, 'kvh', split_axis=0, concat_axis=1, tiled=True)  11.3 us
    unnamed x22, local copies, waits for them, and re-layouts  10.5 us
    all_to_all x1, starting transfers between devices, per_device(): lax.all_to_all(payload, SEQ, split_axis=0, concat_axis=0, tiled=True)  10 us
  transfers between devices with their start and end apart: 5, of which 2 were waited for; matrix products, arithmetic and copies ran while one was open for 12% of the time, Pallas kernels for 14%

profile of v3, /device:TPU:48, one launch (start us, length us, event | category | flops | bytes accessed | tf_op | source)
XLA Modules:
  0.0 225.9 jit_solution(1493068113303976316)
XLA Ops:
  6.5 1.5 copy.107
  8.1 0.7 compare_select_fusion.7
  8.8 0.1 copy.111
  8.9 0.2 reshape.262
  9.1 2.7 %gather_fusion = s32[384]{0:T(512)S(1)} fusion(s32[128]{0:T(128)S(1)} %copy-done.1, s32[1024]{0:T(1024)S(1)} %pad_clamp_fusion), kind=kCustom, calls=%fused_computation | custom fusion | bytes 4608 | tf_op jit(solution)/shard_map/gather | solution.py:91
  11.8 0.1 reshape.207
  11.9 0.1 iota_compare_fusion.1
  12.1 0.2 fusion.13
  12.3 0.1 broadcast_add_fusion
  12.5 0.8 copy_bitcast_fusion.3
  13.2 0.1 broadcast_in_dim.8
  13.3 0.3 reshape.350
  13.7 0.2 fusion.17
  14.0 0.6 fusion.2
  14.6 1.1 copy.114
  15.7 1.5 reshape.210
  17.2 17.3 %all-to-all-start = ((bf16[128,2,16,128]{3,2,1,0:T(8,128)(2,1)}), bf16[128,2,16,128]{3,2,1,0:T(8,128)(2,1)S(1)}, u32[]{:S(2)}, u32[]{:S(2)}) async-start(bf16[128,2,16,128]{3,2,1,0:T(8,128)(2,1)} %reshape.210), calls=%async_computation | async-start | bytes 2097152 | tf_op jit(solution)/shard_map/all_to_all | solution.py:110
  34.6 1.3 collective-permute-start
  35.9 28.6 %collective-permute-done = bf16[2,64,2,128]{3,1,2,0:T(8,128)(2,1)S(1)} collective-permute-done((bf16[2,64,2,128]{3,1,2,0:T(8,128)(2,1)S(1)}, bf16[2,64,2,128]{3,1,2,0:T(8,128)(2,1)S(1)}, u32[]{:S(2)}, u32[]{:S(2)}) %collective-permute-start) | collective-permute-done | bytes 65568 | tf_op jit(solution)/shard_map/ppermute | solution.py:19
  64.5 0.6 copy-done.6
  65.2 1.5 fusion.30
  66.7 1.6 copy_bitcast_fusion.1
  68.3 1.1 copy-done.3
  69.3 24.6 %shard_map.65 = (bf16[128,2,16,128]{3,2,1,0:T(8,128)(2,1)}, f32[2,2048,1]{2,1,0:T(8,128)}) custom-call(bf16[128,2,16,128]{3,2,1,0:T(8,128)(2,1)} %copy-done.3, bf16[2,2048,128]{2,1,0:T(8,128)(2,1)} %get-tuple-element.28.refs_1_, bf16[2,2048,128]{2,1,0:T(8,128)(2,1)} %get-tuple-element.27.refs_2_), custom_call_target="tpu_custom_call" | custom-call | flops 4294967296 | bytes 4194304 | tf_op jit(solution)/shard_map/pallas_call | solution.py:61
  93.9 1.7 copy.159
  95.6 2.2 reduce.26
  97.8 0.1 reshape.212
  98.0 0.1 copy.144
  98.2 0.1 fusion.4
  98.3 0.5 broadcast.488
  98.8 1.4 reduce.52
  100.2 1.6 reshape.381
  101.8 10.0 %all-to-all-start.1 = ((bf16[128,2,2112]{2,1,0:T(2,128)(2,1)}), bf16[128,2,2112]{2,1,0:T(2,128)(2,1)S(1)}, u32[]{:S(2)}, u32[]{:S(2)}) async-start(bf16[128,2,2112]{2,1,0:T(2,128)(2,1)} %reshape.381), calls=%async_computation.1 | async-start | bytes 2228224 | tf_op jit(solution)/shard_map/all_to_all | solution.py:148
  113.1 0.6 reshape_select_fusion.1.refs_0_
  113.7 71.6 %all-gather.5.cloned.1.call-done = bf16[64,64,2,128]{3,1,2,0:T(8,128)(2,1)} async-done(((bf16[2,64,2,128]{3,1,2,0:T(8,128)(2,1)}), bf16[64,64,2,128]{3,1,2,0:T(8,128)(2,1)}) %all-gather.5.cloned.1.call-update) | async-done | bytes 2097168 | tf_op jit(solution)/shard_map/all_gather | solution.py:112
  185.3 2.3 %fusion.1 = bf16[32,2,64,2,128]{4,2,3,1,0:T(8,128)(2,1)S(1)} fusion(s32[]{:T(128)S(6)} %select_n.68, bf16[32,2,64,2,128]{4,2,3,1,0:T(8,128)(2,1)} %bitcast.96, bf16[32,2,64,2,128]{4,2,3,1,0:T(8,128)(2,1)} %bitcast.95), kind=kLoop, calls=%fused_computation.5 | loop fusion | flops 1048576 | bytes 6291460 | tf_op jit(solution)/shard_map/concatenate | solution.py:130
  187.6 0.3 fusion.29
  187.9 1.1 copy.141
  189.0 1.1 copy.140
  190.1 8.1 %shard_map.64 = (f32[2,512,128]{2,1,0:T(8,128)}, f32[2,512,1]{2,1,0:T(8,128)}) custom-call(s32[1,2048]{1,0:T(1,128)} %reshape_select_fusion.1.refs_0_, bf16[2,512,128]{2,1,0:T(8,128)(2,1)} %get-tuple-element.23.refs_1_, bf16[2,2048,128]{2,1,0:T(8,128)(2,1)} %bitcast.100, bf16[2,2048,128]{2,1,0:T(8,128)(2,1)} %bitcast.99), custom_call_target="tpu_custom_call" | custom-call | flops 1073741824 | bytes 2621440 | tf_op jit(solution)/shard_map/pallas_call | solution.py:61
  198.1 1.2 reduce.25
  199.4 0.1 reshape.206
  199.5 0.1 copy.125
  199.6 1.2 reshape.382
  200.8 2.7 %copy.120 = bf16[128,1,4224]{0,2,1:T(8,128)(2,1)S(1)} copy(bf16[128,1,4224]{2,1,0:T(2,128)(2,1)S(1)} %reshape.382) | data formatting | bytes 2162688 | tf_op jit(solution)/shard_map/all_to_all | solution.py:148
  203.5 0.1 slice.87
  203.6 0.2 convolution_bitcast_fusion
  203.8 0.2 copy.122
  204.0 0.1 reduce_max.9
  204.2 0.1 copy.124
  204.2 0.1 copy.127
  204.4 0.2 fusion.28
  204.6 0.1 copy.130
  204.7 0.1 copy.131
  204.8 0.1 copy.126
  204.9 0.1 copy.128
  205.0 0.5 fusion.6
  205.5 0.3 copy.147
  205.8 0.5 multiply_reduce_fusion
  206.3 0.2 copy-done.4
  206.5 0.4 fusion.15
  206.9 0.1 all_to_all.29
  207.0 11.3 %all_to_all.36 = bf16[4,16,2048]{2,1,0:T(8,128)(2,1)S(1)} all-to-all(bf16[4,16,2048]{2,1,0:T(8,128)(2,1)S(1)} %all_to_all.29), channel_id=1, replica_groups=mesh['seq_group'=4,'seq_slot'=32,'kvh'=4] {'kvh'}, dimensions={0} | all-to-all | bytes 524288 | tf_op jit(solution)/shard_map/all_to_all | solution.py:207
  218.3 0.7 copy.145
  (62 shorter events, 1.6 us)
Async XLA Ops:
  6.5 5.9 %copy-start = (bf16[64,16,128]{2,1,0:T(8,128)(2,1)S(1)}, bf16[64,16,128]{2,1,0:T(8,128)(2,1)}, u32[]{:S(2)}) copy-start(bf16[64,16,128]{2,1,0:T(8,128)(2,1)} %param.6) | copy-start | bytes 786436
  6.5 2.6 %copy-start.1 = (s32[128]{0:T(128)S(1)}, s32[128]{0:T(128)}, u32[]{:S(2)}) copy-start(s32[128]{0:T(128)} %param.10) | copy-start | bytes 1540
  6.5 107.1 %all-gather.7.cloned.1.call-start = ((), (), s32[]{:S(2)}) async-start(), calls=%async_computation.4 | async-start | bytes 2162688 | tf_op jit(solution)/shard_map/all_gather | solution.py:113
  15.7 18.9 %copy-start.5 = (bf16[2,64,2,128]{3,1,2,0:T(8,128)(2,1)S(1)}, bf16[2,64,2,128]{3,1,2,0:T(8,128)(2,1)}, u32[]{:S(2)}) copy-start(bf16[2,64,2,128]{3,1,2,0:T(8,128)(2,1)} %copy.107) | copy-start | bytes 196612
  15.7 49.5 %copy-start.2 = (bf16[2,1,2048,2,128]{4,3,2,1,0:T(2,128)(2,1)S(1)}, bf16[2,1,2048,2,128]{4,3,2,1,0:T(2,128)(2,1)}, u32[]{:S(2)}) copy-start(bf16[2,1,2048,2,128]{4,3,2,1,0:T(2,128)(2,1)} %param.8) | copy-start | bytes 6291460
  17.2 51.1 %all-to-all-start = ((bf16[128,2,16,128]{3,2,1,0:T(8,128)(2,1)}), bf16[128,2,16,128]{3,2,1,0:T(8,128)(2,1)S(1)}, u32[]{:S(2)}, u32[]{:S(2)}) async-start(bf16[128,2,16,128]{3,2,1,0:T(8,128)(2,1)} %reshape.210), calls=%async_computation | async-start | bytes 2097152 | tf_op jit(solution)/shard_map/all_to_all | solution.py:110
  34.5 150.7 %all-gather.5.cloned.1.call-start = ((), (), s32[]{:S(2)}) async-start(), calls=%async_computation.3 | async-start | bytes 2162688 | tf_op jit(solution)/shard_map/all_gather | solution.py:112
  34.6 29.9 %collective-permute-start = (bf16[2,64,2,128]{3,1,2,0:T(8,128)(2,1)S(1)}, bf16[2,64,2,128]{3,1,2,0:T(8,128)(2,1)S(1)}, u32[]{:S(2)}, u32[]{:S(2)}) collective-permute-start(bf16[2,64,2,128]{3,1,2,0:T(8,128)(2,1)S(1)} %copy-done.5), channel_id=1, source_target_pairs={{0,128},{4,132},{8,136},{12,140},{16,144},{20,148},{24,152},{28,15... | collective-permute-start | bytes 196616 | tf_op jit(solution)/shard_map/ppermute | solution.py:19
  64.5 0.6 copy-start.6
  68.3 1.1 copy-start.3
  101.8 97.8 %all-to-all-start.1 = ((bf16[128,2,2112]{2,1,0:T(2,128)(2,1)}), bf16[128,2,2112]{2,1,0:T(2,128)(2,1)S(1)}, u32[]{:S(2)}, u32[]{:S(2)}) async-start(bf16[128,2,2112]{2,1,0:T(2,128)(2,1)} %reshape.381), calls=%async_computation.1 | async-start | bytes 2228224 | tf_op jit(solution)/shard_map/all_to_all | solution.py:148
  205.5 1.0 copy-start.4
Sparse Core Ops, SparseCore 0:
  9.5 90.5 all-gather.6
  102.2 82.9 all-gather.4

commit v4 on v2

--- a/solution.py
+++ b/solution.py
@@ -19,7 +19,7 @@
     return lax.ppermute(value, axis, [(source, source + steps) for source in range(initial, last)])
 
 
-def gather_window(stretch_kv, span_devices, companions):
+def gather_window(stretch_kv, span_devices, partner, meet_step, companions):
     stack = stretch_kv[None]
     offsets = [0]
     results = []
@@ -27,9 +27,11 @@
         if len(offsets) >= span_devices:
             break
         arrived = shifted(stack, "seq", step)
-        if index < len(companions) and companions[index] is not None:
-            arrived, done = lax.optimization_barrier((arrived, companions[index]()))
-            results.append(done)
+        if index == meet_step:
+            arrived, partner = lax.optimization_barrier((arrived, partner))
+        if companions[index] is not None:
+            arrived, done = lax.optimization_barrier((arrived, companions[index](partner)))
+            results.extend(done)
         stack = jnp.concatenate([stack, arrived], axis=0)
         offsets = offsets + [o + step for o in offsets]
     return stack, offsets, results
@@ -122,13 +124,12 @@
     slab = capacity * group_size
     outgoing = outgoing.reshape(seq_count, kv_heads, slab, head_dim)
     arrived = lax.all_to_all(outgoing, "seq", split_axis=0, concat_axis=0, tiled=True)
-    arrived, window_start = lax.optimization_barrier((arrived, stretch_kv))
     cache_keys = jnp.swapaxes(cache_kv[0, 0], 0, 1)
     cache_values = jnp.swapaxes(cache_kv[1, 0], 0, 1)
     sources_per_tile = 32
     pieces = seq_count // sources_per_tile
 
-    def serve_piece(piece):
+    def serve_piece(piece, arrived):
         return attend(
             arrived[piece * sources_per_tile : (piece + 1) * sources_per_tile],
             (sources_per_tile, None, slab, head_dim),
@@ -142,10 +143,16 @@
             group_size,
         )
 
+    def serve_pieces(first, last, arrived):
+        return tuple(serve_piece(piece, arrived) for piece in range(first, last))
+
     window, offsets, served_pieces = gather_window(
-        window_start,
+        stretch_kv,
         span_devices,
-        [None] + [functools.partial(serve_piece, piece) for piece in range(pieces)],
+        arrived,
+        2,
+        [None, None, None, functools.partial(serve_pieces, 0, pieces // 2),
+         functools.partial(serve_pieces, pieces // 2, pieces)],
     )
     blocks = window.shape[0]
     served = jnp.concatenate([piece[0] for piece in served_pieces], axis=0)

time: 198 us -> 201 us (1.015)
  waiting for transfers between devices: 58.4 us -> 45.8 us
  starting transfers between devices: 43.7 us -> 51.8 us
  other arithmetic: 9.93 us -> 15.9 us
    all_to_all x1, waiting for transfers between devices: 28.6 us -> 0.01 us  [per_device(): lax.all_to_all(outgoing, 'seq', split_axis=0, concat_axis=0, tiled=True)]
    ppermute x5, waiting for transfers between devices: 14.2 us -> 30.3 us  [shifted(): lax.ppermute(value, axis, [(source, source + steps) for source in range(i...]
    ppermute x5, starting transfers between devices: 14.2 us -> 20.3 us  [shifted(): lax.ppermute(value, axis, [(source, source + steps) for source in range(i...]
    optimization_barrier x4, other arithmetic: 0.86 us -> 5.03 us  [gather_window(): lax.optimization_barrier((arrived, companions[index](partner)))]
    unnamed x34 -> x38, local copies, waits for them, and re-layouts: 9.18 us -> 11.8 us
    all_to_all x1, starting transfers between devices: 12.1 us -> 14.2 us  [per_device(): lax.all_to_all(payload, 'seq', split_axis=0, concat_axis=0, tiled=True)]
  transfers between devices with their start and end apart: 7 -> 7, of which waited for: 6 -> 4; matrix products, arithmetic and copies ran while one was open for 10% -> 10% of each run, Pallas kernels for 20% -> 19%
where the time goes in v4:
time: 201 us; the launch traced here: 200 us
  starting transfers between devices  51.8 us (26%)
  waiting for transfers between devices  45.8 us (23%)
  Pallas kernels  38.7 us (19%)
  local copies, waits for them, and re-layouts  34.9 us (17%)
  other arithmetic  15.9 us (8%)
  blocking collectives  10.8 us (5%)
    pallas_call x5, Pallas kernels, attend(): pl.pallas_call(functools.partial(attend_kernel, thr is not None, scaling,...  38.7 us
    ppermute x5, waiting for transfers between devices, shifted(): lax.ppermute(value, axis, [(source, source + steps) for source in range(i...  30.3 us
    ppermute x5, starting transfers between devices, shifted(): lax.ppermute(value, axis, [(source, source + steps) for source in range(i...  20.3 us
    all_to_all x1, starting transfers between devices, per_device(): lax.all_to_all(outgoing, 'seq', split_axis=0, concat_axis=0, tiled=True)  17.4 us
    all_to_all x1, waiting for transfers between devices, per_device(): lax.all_to_all(payload, 'seq', split_axis=0, concat_axis=0, tiled=True)  15.5 us
    all_to_all x1, starting transfers between devices, per_device(): lax.all_to_all(payload, 'seq', split_axis=0, concat_axis=0, tiled=True)  14.2 us
    unnamed x38, local copies, waits for them, and re-layouts  11.8 us
    all_to_all x1, blocking collectives, per_device(): lax.all_to_all(heads_out, 'kvh', split_axis=0, concat_axis=1, tiled=True)  10.8 us
  transfers between devices with their start and end apart: 7, of which 4 were waited for; matrix products, arithmetic and copies ran while one was open for 10% of the time, Pallas kernels for 19%

profile of v4, /device:TPU:8, one launch (start us, length us, event | category | flops | bytes accessed | tf_op | source)
XLA Modules:
  0.0 199.8 jit_solution(7070220271968858964)
XLA Ops:
  0.0 0.7 compare_select_fusion.7
  0.9 0.2 reshape.274
  1.1 2.7 %gather_fusion = s32[384]{0:T(512)S(1)} fusion(s32[128]{0:T(128)S(1)} %copy-done.1, s32[1024]{0:T(1024)S(1)} %pad_clamp_fusion), kind=kCustom, calls=%fused_computation | custom fusion | bytes 4608 | tf_op jit(solution)/shard_map/gather | solution.py:107
  4.0 0.2 fusion.12
  4.4 0.2 fusion.16
  4.7 0.8 copy_bitcast_fusion.3
  5.6 0.3 reshape.360
  5.9 0.6 fusion.1
  6.5 1.1 copy.110
  7.6 1.5 reshape.216
  9.1 17.4 %all-to-all-start = ((bf16[128,2,16,128]{3,2,1,0:T(8,128)(2,1)}), bf16[128,2,16,128]{3,2,1,0:T(8,128)(2,1)S(1)}, u32[]{:S(2)}, u32[]{:S(2)}) async-start(bf16[128,2,16,128]{3,2,1,0:T(8,128)(2,1)} %reshape.216), calls=%async_computation | async-start | bytes 2097152 | tf_op jit(solution)/shard_map/all_to_all | solution.py:126
  26.5 7.3 %collective-permute-start = (bf16[1,2,64,2,128]{4,3,2,1,0:T(2,128)(2,1)S(1)}, bf16[1,2,64,2,128]{4,3,2,1,0:T(2,128)(2,1)S(1)}, u32[]{:S(2)}, u32[]{:S(2)}) collective-permute-start(bf16[1,2,64,2,128]{4,3,2,1,0:T(2,128)(2,1)S(1)} %bitcast.103), channel_id=1, source_target_pairs={{0,32},{4,36},{8,40},{12,44},{16,48},{20,52},{24,56},{28,60},{32,6... | collective-permute-start | bytes 196616 | tf_op jit(solution)/shard_map/ppermute | solution.py:19
  33.9 1.5 fusion.28
  35.4 21.2 %collective-permute-done = bf16[1,2,64,2,128]{4,3,2,1,0:T(2,128)(2,1)S(1)} collective-permute-done((bf16[1,2,64,2,128]{4,3,2,1,0:T(2,128)(2,1)S(1)}, bf16[1,2,64,2,128]{4,3,2,1,0:T(2,128)(2,1)S(1)}, u32[]{:S(2)}, u32[]{:S(2)}) %collective-permute-start) | collective-permute-done | bytes 65568 | tf_op jit(solution)/shard_map/ppermute | solution.py:19
  56.5 0.2 pad_maximum_fusion.3
  56.7 2.3 %collective-permute-start.1 = (bf16[2,2,64,2,128]{4,3,2,1,0:T(2,128)(2,1)S(1)}, bf16[2,2,64,2,128]{4,3,2,1,0:T(2,128)(2,1)S(1)}, u32[]{:S(2)}, u32[]{:S(2)}) collective-permute-start(bf16[2,2,64,2,128]{4,3,2,1,0:T(2,128)(2,1)S(1)} %pad_maximum_fusion.3), channel_id=1, source_target_pairs={{0,16},{4,20},{8,24},{12,28},{16,32},{20,36},{24,40},{28,44},{32,4... | collective-permute-start | bytes 393224 | tf_op jit(solution)/shard_map/ppermute | solution.py:19
  59.0 1.6 copy_bitcast_fusion.1
  60.7 7.5 %collective-permute-done.1 = bf16[2,2,64,2,128]{4,3,2,1,0:T(2,128)(2,1)S(1)} collective-permute-done((bf16[2,2,64,2,128]{4,3,2,1,0:T(2,128)(2,1)S(1)}, bf16[2,2,64,2,128]{4,3,2,1,0:T(2,128)(2,1)S(1)}, u32[]{:S(2)}, u32[]{:S(2)}) %collective-permute-start.1) | collective-permute-done | bytes 131104 | tf_op jit(solution)/shard_map/ppermute | solution.py:19
  68.1 0.4 pad_maximum_fusion.2
  68.5 5.0 %collective-permute-start.2 = (bf16[4,2,64,2,128]{4,3,2,1,0:T(2,128)(2,1)S(1)}, bf16[4,2,64,2,128]{4,3,2,1,0:T(2,128)(2,1)}, u32[]{:S(2)}, u32[]{:S(2)}) collective-permute-start(bf16[4,2,64,2,128]{4,3,2,1,0:T(2,128)(2,1)S(1)} %pad_maximum_fusion.2), channel_id=1, source_target_pairs={{0,64},{4,68},{8,72},{12,76},{16,80},{20,84},{24,88},{28,92},{32,9... | collective-permute-start | bytes 786440 | tf_op jit(solution)/shard_map/ppermute | solution.py:19
  73.5 0.7 constant_dynamic-update-slice_fusion.10
  74.2 0.7 constant_dynamic-update-slice_fusion.9
  74.9 0.8 constant_dynamic-update-slice_fusion.8
  75.7 1.7 collective-permute-done.2
  77.4 2.5 %pad_maximum_fusion.1 = bf16[8,2,64,2,128]{4,3,2,1,0:T(2,128)(2,1)} fusion(bf16[4,2,64,2,128]{4,3,2,1,0:T(2,128)(2,1)} %collective-permute-done.2, bf16[2,2,64,2,128]{4,3,2,1,0:T(2,128)(2,1)S(1)} %collective-permute-done.1, bf16[1,2,64,2,128]{4,3,2,1,0:T(2,128)(2,1)} %copy-done.6, bf16[1,2,64,2,128]{4,3,2,1,0:T(2,128)(2,1)} %bitcast.102), kind=kLoop, calls=%fused_computation.20 | loop fusion | flops 786432 | bytes 1048576 | tf_op jit(solution)/shard_map/concatenate | solution.py:35
  79.9 3.5 %collective-permute-start.3 = (bf16[8,2,64,2,128]{4,3,2,1,0:T(2,128)(2,1)}, bf16[8,2,64,2,128]{4,3,2,1,0:T(2,128)(2,1)}, u32[]{:S(2)}, u32[]{:S(2)}) collective-permute-start(bf16[8,2,64,2,128]{4,3,2,1,0:T(2,128)(2,1)} %pad_maximum_fusion.1), channel_id=1, source_target_pairs={{0,8},{4,12},{8,16},{12,20},{16,24},{20,28},{24,32},{28,36},{32,40... | collective-permute-start | bytes 1572872 | tf_op jit(solution)/shard_map/ppermute | solution.py:19
  83.5 1.1 fusion.29
  84.5 7.6 %shard_map.65 = (bf16[32,2,16,128]{3,2,1,0:T(8,128)(2,1)}, f32[2,512,1]{2,1,0:T(8,128)}) custom-call(bf16[32,2,16,128]{3,2,1,0:T(8,128)(2,1)} %get-tuple-element.67.refs_0_, bf16[2,2048,128]{2,1,0:T(8,128)(2,1)} %get-tuple-element.84.refs_1_, bf16[2,2048,128]{2,1,0:T(8,128)(2,1)} %get-tuple-element.83.refs_2_), custom_call_target="tpu_custom_call" | custom-call | flops 1073741824 | bytes 2621440 | tf_op jit(solution)/shard_map/pallas_call | solution.py:79
  92.1 7.7 %shard_map.64 = (bf16[32,2,16,128]{3,2,1,0:T(8,128)(2,1)}, f32[2,512,1]{2,1,0:T(8,128)}) custom-call(bf16[32,2,16,128]{3,2,1,0:T(8,128)(2,1)} %get-tuple-element.68.refs_0_, bf16[2,2048,128]{2,1,0:T(8,128)(2,1)} %get-tuple-element.84.refs_1_, bf16[2,2048,128]{2,1,0:T(8,128)(2,1)} %get-tuple-element.83.refs_2_), custom_call_target="tpu_custom_call" | custom-call | flops 1073741824 | bytes 2621440 | tf_op jit(solution)/shard_map/pallas_call | solution.py:79
  99.8 1.4 constant_dynamic-update-slice_fusion.7
  101.2 2.1 %constant_dynamic-update-slice_fusion.6 = (bf16[32,2,64,2,128]{4,3,2,1,0:T(2,128)(2,1)S(1)}, bf16[16,2,64,2,128]{4,3,2,1,0:T(2,128)(2,1)S(1)}) fusion(bf16[32,2,64,2,128]{4,3,2,1,0:T(2,128)(2,1)S(1)} %get-tuple-element.73, bf16[8,2,64,2,128]{4,3,2,1,0:T(2,128)(2,1)} %collective-permute-done.3, bf16[16,2,64,2,128]{4,3,2,1,0:T(2,128)(2,1)S(1)} %get-tuple-element.74), kind=kLoop, calls=%fused_computation.90 | loop fusion | bytes 1572864
  103.4 1.0 copy-done.13
  104.3 2.1 %collective-permute-start.4 = (bf16[16,2,64,2,128]{4,3,2,1,0:T(2,128)(2,1)}, bf16[16,2,64,2,128]{4,3,2,1,0:T(2,128)(2,1)S(1)}, u32[]{:S(2)}, u32[]{:S(2)}) collective-permute-start(bf16[16,2,64,2,128]{4,3,2,1,0:T(2,128)(2,1)} %copy-done.13), channel_id=1, source_target_pairs={{0,4},{4,8},{8,12},{12,16},{16,20},{20,24},{24,28},{28,32},{32,36}... | collective-permute-start | bytes 3145736 | tf_op jit(solution)/shard_map/ppermute | solution.py:19
  106.5 7.7 %shard_map.67 = (bf16[32,2,16,128]{3,2,1,0:T(8,128)(2,1)}, f32[2,512,1]{2,1,0:T(8,128)}) custom-call(bf16[32,2,16,128]{3,2,1,0:T(8,128)(2,1)} %get-tuple-element.65.refs_0_, bf16[2,2048,128]{2,1,0:T(8,128)(2,1)} %get-tuple-element.84.refs_1_, bf16[2,2048,128]{2,1,0:T(8,128)(2,1)} %get-tuple-element.83.refs_2_), custom_call_target="tpu_custom_call" | custom-call | flops 1073741824 | bytes 2621440 | tf_op jit(solution)/shard_map/pallas_call | solution.py:79
  114.1 7.6 %shard_map.66 = (bf16[32,2,16,128]{3,2,1,0:T(8,128)(2,1)}, f32[2,512,1]{2,1,0:T(8,128)}) custom-call(bf16[32,2,16,128]{3,2,1,0:T(8,128)(2,1)} %get-tuple-element.66.refs_0_, bf16[2,2048,128]{2,1,0:T(8,128)(2,1)} %get-tuple-element.84.refs_1_, bf16[2,2048,128]{2,1,0:T(8,128)(2,1)} %get-tuple-element.83.refs_2_), custom_call_target="tpu_custom_call" | custom-call | flops 1073741824 | bytes 2621440 | tf_op jit(solution)/shard_map/pallas_call | solution.py:79
  121.8 1.2 reduce.25
  123.0 1.3 reduce.26
  124.6 1.3 reduce.27
  125.9 1.3 reduce.28
  127.5 0.9 constant_dynamic-update-slice_fusion.5
  128.8 1.1 copy-done.2
  130.0 0.5 copy.156
  130.7 0.5 broadcast.489
  131.2 1.4 reduce.55
  132.6 1.6 reshape.394
  134.2 14.2 %all-to-all-start.1 = ((bf16[128,2,2112]{2,1,0:T(2,128)(2,1)}), bf16[128,2,2112]{2,1,0:T(2,128)(2,1)S(1)}, u32[]{:S(2)}, u32[]{:S(2)}) async-start(bf16[128,2,2112]{2,1,0:T(2,128)(2,1)} %reshape.394), calls=%async_computation.1 | async-start | bytes 2228224 | tf_op jit(solution)/shard_map/all_to_all | solution.py:178
  149.5 0.3 compare_reduce_fusion
  149.8 0.6 reshape_select_fusion.1.refs_0_
  150.5 2.9 %slice_bitcast_fusion = (bf16[2,32,64,128]{3,0,2,1:T(2,128)(2,1)S(1)}, bf16[2,32,64,128]{3,0,2,1:T(2,128)(2,1)S(1)}) fusion(bf16[32,2,64,2,128]{4,3,2,1,0:T(2,128)(2,1)} %copy-done.2), kind=kLoop, calls=%fused_computation.13 | loop fusion | bytes 4194304 | tf_op jit(solution)/shard_map/transpose | solution.py:185
  153.4 1.3 copy.118
  154.7 1.3 copy.117
  156.0 8.1 %shard_map.68 = (f32[2,512,128]{2,1,0:T(8,128)}, f32[2,512,1]{2,1,0:T(8,128)}) custom-call(s32[1,2048]{1,0:T(1,128)} %reshape_select_fusion.1.refs_0_, bf16[2,512,128]{2,1,0:T(8,128)(2,1)} %get-tuple-element.71.refs_1_, bf16[2,2048,128]{2,1,0:T(8,128)(2,1)} %bitcast.99, bf16[2,2048,128]{2,1,0:T(8,128)(2,1)} %bitcast.98), custom_call_target="tpu_custom_call" | custom-call | flops 1073741824 | bytes 2621440 | tf_op jit(solution)/shard_map/pallas_call | solution.py:79
  164.1 1.2 reduce.29
  165.5 15.5 %all-to-all-done.1 = bf16[128,2,2112]{2,1,0:T(2,128)(2,1)S(1)} async-done(((bf16[128,2,2112]{2,1,0:T(2,128)(2,1)}), bf16[128,2,2112]{2,1,0:T(2,128)(2,1)S(1)}, u32[]{:S(2)}, u32[]{:S(2)}) %all-to-all-start.1) | async-done | bytes 1081376 | tf_op jit(solution)/shard_map/all_to_all | solution.py:178
  181.0 1.2 reshape.395
  182.2 2.7 %copy.121 = bf16[128,1,4224]{0,2,1:T(8,128)(2,1)S(1)} copy(bf16[128,1,4224]{2,1,0:T(2,128)(2,1)S(1)} %reshape.395) | data formatting | bytes 2162688 | tf_op jit(solution)/shard_map/all_to_all | solution.py:178
  185.1 0.2 convolution_bitcast_fusion
  185.7 0.5 fusion.5
  186.2 0.3 copy.144
  186.7 0.2 fusion.27
  187.3 0.5 multiply_reduce_fusion
  187.8 0.4 fusion.14
  188.3 10.8 %all_to_all.36 = bf16[4,16,2048]{2,1,0:T(8,128)(2,1)S(1)} all-to-all(bf16[4,16,2048]{2,1,0:T(8,128)(2,1)S(1)} %all_to_all.29), channel_id=1, replica_groups=mesh['seq'=128,'kvh'=4] {'kvh'}, dimensions={0} | all-to-all | bytes 524288 | tf_op jit(solution)/shard_map/all_to_all | solution.py:237
  199.1 0.7 copy.142
  (100 shorter events, 4.3 us)
Async XLA Ops:
  0.0 4.7 %copy-start = (bf16[64,16,128]{2,1,0:T(8,128)(2,1)S(1)}, bf16[64,16,128]{2,1,0:T(8,128)(2,1)}, u32[]{:S(2)}) copy-start(bf16[64,16,128]{2,1,0:T(8,128)(2,1)} %param.6) | copy-start | bytes 786436
  0.0 1.1 copy-start.1
  7.6 18.9 %copy-start.4 = (bf16[2,64,2,128]{3,2,1,0:T(2,128)(2,1)S(1)}, bf16[2,64,2,128]{3,2,1,0:T(2,128)(2,1)}, u32[]{:S(2)}) copy-start(bf16[2,64,2,128]{3,2,1,0:T(2,128)(2,1)} %param.7) | copy-start | bytes 196612
  7.6 26.2 %copy-start.3 = (bf16[2,1,2048,2,128]{4,3,2,1,0:T(2,128)(2,1)S(1)}, bf16[2,1,2048,2,128]{4,3,2,1,0:T(2,128)(2,1)}, u32[]{:S(2)}) copy-start(bf16[2,1,2048,2,128]{4,3,2,1,0:T(2,128)(2,1)} %param.8) | copy-start | bytes 6291460
  9.1 68.3 %all-to-all-start = ((bf16[128,2,16,128]{3,2,1,0:T(8,128)(2,1)}), bf16[128,2,16,128]{3,2,1,0:T(8,128)(2,1)S(1)}, u32[]{:S(2)}, u32[]{:S(2)}) async-start(bf16[128,2,16,128]{3,2,1,0:T(8,128)(2,1)} %reshape.216), calls=%async_computation | async-start | bytes 2097152 | tf_op jit(solution)/shard_map/all_to_all | solution.py:126
  26.5 30.0 %collective-permute-start = (bf16[1,2,64,2,128]{4,3,2,1,0:T(2,128)(2,1)S(1)}, bf16[1,2,64,2,128]{4,3,2,1,0:T(2,128)(2,1)S(1)}, u32[]{:S(2)}, u32[]{:S(2)}) collective-permute-start(bf16[1,2,64,2,128]{4,3,2,1,0:T(2,128)(2,1)S(1)} %bitcast.103), channel_id=1, source_target_pairs={{0,32},{4,36},{8,40},{12,44},{16,48},{20,52},{24,56},{28,60},{32,6... | collective-permute-start | bytes 196616 | tf_op jit(solution)/shard_map/ppermute | solution.py:19
  56.5 19.2 %copy-start.6 = (bf16[1,2,64,2,128]{4,3,2,1,0:T(2,128)(2,1)}, bf16[1,2,64,2,128]{4,3,2,1,0:T(2,128)(2,1)S(1)}, u32[]{:S(2)}) copy-start(bf16[1,2,64,2,128]{4,3,2,1,0:T(2,128)(2,1)S(1)} %collective-permute-done) | copy-start | bytes 196612
  56.7 11.4 %collective-permute-start.1 = (bf16[2,2,64,2,128]{4,3,2,1,0:T(2,128)(2,1)S(1)}, bf16[2,2,64,2,128]{4,3,2,1,0:T(2,128)(2,1)S(1)}, u32[]{:S(2)}, u32[]{:S(2)}) collective-permute-start(bf16[2,2,64,2,128]{4,3,2,1,0:T(2,128)(2,1)S(1)} %pad_maximum_fusion.3), channel_id=1, source_target_pairs={{0,16},{4,20},{8,24},{12,28},{16,32},{20,36},{24,40},{28,44},{32,4... | collective-permute-start | bytes 393224 | tf_op jit(solution)/shard_map/ppermute | solution.py:19
  59.0 9.1 %copy-start.5 = (bf16[2,64,2,128]{3,2,1,0:T(2,128)(2,1)S(1)}, bf16[2,64,2,128]{3,2,1,0:T(2,128)(2,1)}, u32[]{:S(2)}) copy-start(bf16[2,64,2,128]{3,2,1,0:T(2,128)(2,1)} %param.7) | copy-start | bytes 196612
  68.5 8.9 %collective-permute-start.2 = (bf16[4,2,64,2,128]{4,3,2,1,0:T(2,128)(2,1)S(1)}, bf16[4,2,64,2,128]{4,3,2,1,0:T(2,128)(2,1)}, u32[]{:S(2)}, u32[]{:S(2)}) collective-permute-start(bf16[4,2,64,2,128]{4,3,2,1,0:T(2,128)(2,1)S(1)} %pad_maximum_fusion.2), channel_id=1, source_target_pairs={{0,64},{4,68},{8,72},{12,76},{16,80},{20,84},{24,88},{28,92},{32,9... | collective-permute-start | bytes 786440 | tf_op jit(solution)/shard_map/ppermute | solution.py:19
  79.9 21.3 %collective-permute-start.3 = (bf16[8,2,64,2,128]{4,3,2,1,0:T(2,128)(2,1)}, bf16[8,2,64,2,128]{4,3,2,1,0:T(2,128)(2,1)}, u32[]{:S(2)}, u32[]{:S(2)}) collective-permute-start(bf16[8,2,64,2,128]{4,3,2,1,0:T(2,128)(2,1)} %pad_maximum_fusion.1), channel_id=1, source_target_pairs={{0,8},{4,12},{8,16},{12,20},{16,24},{20,28},{24,32},{28,36},{32,40... | collective-permute-start | bytes 1572872 | tf_op jit(solution)/shard_map/ppermute | solution.py:19
  92.1 7.7 %copy-start.12 = (bf16[16,2,64,2,128]{4,3,2,1,0:T(2,128)(2,1)S(1)}, bf16[16,2,64,2,128]{4,3,2,1,0:T(2,128)(2,1)}, u32[]{:S(2)}) copy-start(bf16[16,2,64,2,128]{4,3,2,1,0:T(2,128)(2,1)} %get-tuple-element.76) | copy-start | bytes 3145732
  103.3 1.0 copy-start.13
  104.3 20.3 %collective-permute-start.4 = (bf16[16,2,64,2,128]{4,3,2,1,0:T(2,128)(2,1)}, bf16[16,2,64,2,128]{4,3,2,1,0:T(2,128)(2,1)S(1)}, u32[]{:S(2)}, u32[]{:S(2)}) collective-permute-start(bf16[16,2,64,2,128]{4,3,2,1,0:T(2,128)(2,1)} %copy-done.13), channel_id=1, source_target_pairs={{0,4},{4,8},{8,12},{12,16},{16,20},{20,24},{24,28},{28,32},{32,36}... | collective-permute-start | bytes 3145736 | tf_op jit(solution)/shard_map/ppermute | solution.py:19
  127.4 1.0 copy-start.8
  127.4 1.0 copy-start.9
  127.4 1.1 copy-start.10
  127.4 1.2 copy-start.11
  128.6 1.4 copy-start.2
  134.2 46.9 %all-to-all-start.1 = ((bf16[128,2,2112]{2,1,0:T(2,128)(2,1)}), bf16[128,2,2112]{2,1,0:T(2,128)(2,1)S(1)}, u32[]{:S(2)}, u32[]{:S(2)}) async-start(bf16[128,2,2112]{2,1,0:T(2,128)(2,1)} %reshape.394), calls=%async_computation.1 | async-start | bytes 2228224 | tf_op jit(solution)/shard_map/all_to_all | solution.py:178
  186.5 1.2 copy-start.7

commit v5 on v2

--- a/solution.py
+++ b/solution.py
@@ -56,7 +56,8 @@
         / weight_sum
     )
     o_ref[...] = blended.astype(o_ref.dtype).reshape(o_ref.shape)
-    lse_ref[...] = highest * scaling + jnp.log(weight_sum)
+    log_sum = highest * scaling + jnp.log(weight_sum)
+    lse_ref[...] = jnp.transpose(jnp.broadcast_to(log_sum, (log_sum.shape[0], 128)))[:8]
 
 
 def attend(q, q_block, q_map, heads, tiles, keys, values, out_dtype, scaling, group_size, thr=None, out_rows=None, out_map=None):
@@ -80,11 +81,11 @@
         in_specs=in_specs,
         out_specs=[
             pl.BlockSpec(q_block, out_map or q_map),
-            pl.BlockSpec((None, rows, 1), lambda h, i: (h, i, 0)),
+            pl.BlockSpec((None, None, 8, rows), lambda h, i: (h, i, 0, 0)),
         ],
         out_shape=[
             jax.ShapeDtypeStruct(((out_rows or q.shape[0]),) + q.shape[1:], out_dtype),
-            jax.ShapeDtypeStruct((heads, total_rows, 1), jnp.float32),
+            jax.ShapeDtypeStruct((heads, tiles, 8, rows), jnp.float32),
         ],
         cost_estimate=cost,
     )(*operands)
@@ -150,7 +151,7 @@
     blocks = window.shape[0]
     served = jnp.concatenate([piece[0] for piece in served_pieces], axis=0)
     served_lse = jnp.concatenate(
-        [piece[1].reshape(kv_heads, sources_per_tile, slab) for piece in served_pieces], axis=1
+        [piece[1][:, :, 0].reshape(kv_heads, sources_per_tile, slab) for piece in served_pieces], axis=1
     )
     served_lse = jnp.swapaxes(served_lse, 0, 1)
     served, served_lse, window = lax.optimization_barrier((served, served_lse, window))
@@ -198,7 +199,7 @@
         threshold,
     )
     own_out = own_out.reshape(kv_heads, rows_local, group_size, head_dim)
-    own_lse = own_lse.reshape(kv_heads, rows_local, group_size)
+    own_lse = own_lse[:, :, 0].reshape(kv_heads, rows_local, group_size)
     head_rows = jnp.arange(kv_heads, dtype=jnp.int32)[:, None]
     picked = (
         jnp.einsum(

time: 198 us -> 199 us (level)
  local copies, waits for them, and re-layouts: 34.4 us -> 38.4 us
  other arithmetic: 9.93 us -> 7.57 us
    slice x0 -> x5, local copies, waits for them, and re-layouts: none -> 3.99 us  [the longest x4 3.21 us: per_device(): piece[1][:, :, 0].reshape(kv_heads, sources_per_tile, slab)]
    unnamed x34 -> x26, local copies, waits for them, and re-layouts: 9.18 us -> 9.17 us
  transfers between devices with their start and end apart: 7 -> 7, of which waited for: 6 -> 6; matrix products, arithmetic and copies ran while one was open for 10% -> 10% of each run, Pallas kernels for 20% -> 19%
where the time goes in v5:
time: 199 us; the launch traced here: 198 us
  waiting for transfers between devices  58.1 us (29%)
  starting transfers between devices  43.6 us (22%)
  local copies, waits for them, and re-layouts  38.4 us (19%)
  Pallas kernels  38 us (19%)
  blocking collectives  10.8 us (5%)
  other arithmetic  7.57 us (4%)
    pallas_call x5, Pallas kernels, attend(): pl.pallas_call(functools.partial(attend_kernel, thr is not None, scaling,...  38 us
    all_to_all x1, waiting for transfers between devices, per_device(): lax.all_to_all(outgoing, 'seq', split_axis=0, concat_axis=0, tiled=True)  28.6 us
    all_to_all x1, starting transfers between devices, per_device(): lax.all_to_all(outgoing, 'seq', split_axis=0, concat_axis=0, tiled=True)  17.4 us
    all_to_all x1, waiting for transfers between devices, per_device(): lax.all_to_all(payload, 'seq', split_axis=0, concat_axis=0, tiled=True)  16.4 us
    ppermute x5, starting transfers between devices, shifted(): lax.ppermute(value, axis, [(source, source + steps) for source in range(i...  13.7 us
    ppermute x5, waiting for transfers between devices, shifted(): lax.ppermute(value, axis, [(source, source + steps) for source in range(i...  13.1 us
    all_to_all x1, starting transfers between devices, per_device(): lax.all_to_all(payload, 'seq', split_axis=0, concat_axis=0, tiled=True)  12.5 us
    all_to_all x1, blocking collectives, per_device(): lax.all_to_all(heads_out, 'kvh', split_axis=0, concat_axis=1, tiled=True)  10.8 us
  transfers between devices with their start and end apart: 7, of which 6 were waited for; matrix products, arithmetic and copies ran while one was open for 10% of the time, Pallas kernels for 19%

profile of v5, /device:TPU:8, one launch (start us, length us, event | category | flops | bytes accessed | tf_op | source)
XLA Modules:
  0.0 198.2 jit_solution(1240279450401684064)
XLA Ops:
  0.0 0.7 compare_select_fusion.7
  0.9 0.2 reshape.254
  1.1 2.7 %gather_fusion = s32[384]{0:T(512)S(1)} fusion(s32[128]{0:T(128)S(1)} %copy-done.1, s32[1024]{0:T(1024)S(1)} %pad_clamp_fusion), kind=kCustom, calls=%fused_computation | custom fusion | bytes 4608 | tf_op jit(solution)/shard_map/gather | solution.py:106
  4.0 0.2 fusion.12
  4.4 0.2 fusion.16
  4.7 0.8 copy_bitcast_fusion.3
  5.6 0.3 reshape.340
  5.9 0.6 fusion.1
  6.5 1.1 copy.110
  7.6 1.5 reshape.201
  9.1 17.4 %all-to-all-start = ((bf16[128,2,16,128]{3,2,1,0:T(8,128)(2,1)}), bf16[128,2,16,128]{3,2,1,0:T(8,128)(2,1)S(1)}, u32[]{:S(2)}, u32[]{:S(2)}) async-start(bf16[128,2,16,128]{3,2,1,0:T(8,128)(2,1)} %reshape.201), calls=%async_computation | async-start | bytes 2097152 | tf_op jit(solution)/shard_map/all_to_all | solution.py:125
  26.5 2.7 %fusion.28 = (bf16[1,1,2048,2,128]{4,3,2,1,0:T(2,128)(2,1)S(1)}, bf16[1,1,2048,2,128]{4,3,2,1,0:T(2,128)(2,1)S(1)}) fusion(bf16[2,1,2048,2,128]{4,3,2,1,0:T(2,128)(2,1)} %param.8), kind=kLoop, calls=%fused_computation.120 | loop fusion | bytes 4194304 | tf_op jit(solution)/shard_map/slice | solution.py:128
  29.2 28.6 %all-to-all-done = bf16[128,2,16,128]{3,2,1,0:T(8,128)(2,1)S(1)} async-done(((bf16[128,2,16,128]{3,2,1,0:T(8,128)(2,1)}), bf16[128,2,16,128]{3,2,1,0:T(8,128)(2,1)S(1)}, u32[]{:S(2)}, u32[]{:S(2)}) %all-to-all-start) | async-done | bytes 1048608 | tf_op jit(solution)/shard_map/all_to_all | solution.py:125
  57.8 3.3 %collective-permute-start = (bf16[1,2,64,2,128]{4,3,2,1,0:T(2,128)(2,1)S(1)}, bf16[1,2,64,2,128]{4,3,2,1,0:T(2,128)(2,1)S(1)}, u32[]{:S(2)}, u32[]{:S(2)}) collective-permute-start(bf16[1,2,64,2,128]{4,3,2,1,0:T(2,128)(2,1)S(1)} %bitcast.102), channel_id=1, source_target_pairs={{0,32},{4,36},{8,40},{12,44},{16,48},{20,52},{24,56},{28,60},{32,6... | collective-permute-start | bytes 196616 | tf_op jit(solution)/shard_map/ppermute | solution.py:19
  61.1 1.6 copy_bitcast_fusion.1
  62.7 6.1 %collective-permute-done = bf16[1,2,64,2,128]{4,3,2,1,0:T(2,128)(2,1)S(1)} collective-permute-done((bf16[1,2,64,2,128]{4,3,2,1,0:T(2,128)(2,1)S(1)}, bf16[1,2,64,2,128]{4,3,2,1,0:T(2,128)(2,1)S(1)}, u32[]{:S(2)}, u32[]{:S(2)}) %collective-permute-start) | collective-permute-done | bytes 65568 | tf_op jit(solution)/shard_map/ppermute | solution.py:19
  68.9 0.2 pad_maximum_fusion.3
  69.0 2.4 %collective-permute-start.1 = (bf16[2,2,64,2,128]{4,3,2,1,0:T(2,128)(2,1)S(1)}, bf16[2,2,64,2,128]{4,3,2,1,0:T(2,128)(2,1)S(1)}, u32[]{:S(2)}, u32[]{:S(2)}) collective-permute-start(bf16[2,2,64,2,128]{4,3,2,1,0:T(2,128)(2,1)S(1)} %pad_maximum_fusion.3), channel_id=1, source_target_pairs={{0,16},{4,20},{8,24},{12,28},{16,32},{20,36},{24,40},{28,44},{32,4... | collective-permute-start | bytes 393224 | tf_op jit(solution)/shard_map/ppermute | solution.py:19
  71.4 1.1 fusion.29
  72.5 7.5 %shard_map.64 = (bf16[32,2,16,128]{3,2,1,0:T(8,128)(2,1)}, f32[2,1,8,512]{3,2,1,0:T(8,128)}) custom-call(bf16[32,2,16,128]{3,2,1,0:T(8,128)(2,1)} %get-tuple-element.72.refs_0_, bf16[2,2048,128]{2,1,0:T(8,128)(2,1)} %get-tuple-element.88.refs_1_, bf16[2,2048,128]{2,1,0:T(8,128)(2,1)} %get-tuple-element.87.refs_2_), custom_call_target="tpu_custom_call" | custom-call | flops 1073741824 | bytes 2621440 | tf_op jit(solution)/shard_map/pallas_call | solution.py:78
  79.9 0.2 collective-permute-done.1
  80.2 0.4 pad_maximum_fusion.2
  80.6 2.7 %collective-permute-start.2 = (bf16[4,2,64,2,128]{4,3,2,1,0:T(2,128)(2,1)S(1)}, bf16[4,2,64,2,128]{4,3,2,1,0:T(2,128)(2,1)S(1)}, u32[]{:S(2)}, u32[]{:S(2)}) collective-permute-start(bf16[4,2,64,2,128]{4,3,2,1,0:T(2,128)(2,1)S(1)} %pad_maximum_fusion.2), channel_id=1, source_target_pairs={{0,64},{4,68},{8,72},{12,76},{16,80},{20,84},{24,88},{28,92},{32,9... | collective-permute-start | bytes 786440 | tf_op jit(solution)/shard_map/ppermute | solution.py:19
  83.3 7.5 %shard_map.65 = (bf16[32,2,16,128]{3,2,1,0:T(8,128)(2,1)}, f32[2,1,8,512]{3,2,1,0:T(8,128)}) custom-call(bf16[32,2,16,128]{3,2,1,0:T(8,128)(2,1)} %get-tuple-element.71.refs_0_, bf16[2,2048,128]{2,1,0:T(8,128)(2,1)} %get-tuple-element.88.refs_1_, bf16[2,2048,128]{2,1,0:T(8,128)(2,1)} %get-tuple-element.87.refs_2_), custom_call_target="tpu_custom_call" | custom-call | flops 1073741824 | bytes 2621440 | tf_op jit(solution)/shard_map/pallas_call | solution.py:78
  90.8 0.7 pad_maximum_fusion.1
  91.6 3.4 %collective-permute-start.3 = (bf16[8,2,64,2,128]{4,3,2,1,0:T(2,128)(2,1)S(1)}, bf16[8,2,64,2,128]{4,3,2,1,0:T(2,128)(2,1)S(1)}, u32[]{:S(2)}, u32[]{:S(2)}) collective-permute-start(bf16[8,2,64,2,128]{4,3,2,1,0:T(2,128)(2,1)S(1)} %pad_maximum_fusion.1), channel_id=1, source_target_pairs={{0,8},{4,12},{8,16},{12,20},{16,24},{20,28},{24,32},{28,36},{32,40... | collective-permute-start | bytes 1572872 | tf_op jit(solution)/shard_map/ppermute | solution.py:19
  95.0 0.7 constant_dynamic-update-slice_fusion.10
  95.7 7.5 %shard_map.66 = (bf16[32,2,16,128]{3,2,1,0:T(8,128)(2,1)}, f32[2,1,8,512]{3,2,1,0:T(8,128)}) custom-call(bf16[32,2,16,128]{3,2,1,0:T(8,128)(2,1)} %get-tuple-element.70.refs_0_, bf16[2,2048,128]{2,1,0:T(8,128)(2,1)} %get-tuple-element.88.refs_1_, bf16[2,2048,128]{2,1,0:T(8,128)(2,1)} %get-tuple-element.87.refs_2_), custom_call_target="tpu_custom_call" | custom-call | flops 1073741824 | bytes 2621440 | tf_op jit(solution)/shard_map/pallas_call | solution.py:78
  103.2 0.7 constant_dynamic-update-slice_fusion.9
  103.9 0.8 constant_dynamic-update-slice_fusion.8
  104.7 1.2 constant_dynamic-update-slice_fusion.7
  105.9 0.6 collective-permute-done.3
  106.6 2.0 constant_dynamic-update-slice_fusion.6
  108.6 1.9 collective-permute-start.4
  110.5 7.5 %shard_map.67 = (bf16[32,2,16,128]{3,2,1,0:T(8,128)(2,1)}, f32[2,1,8,512]{3,2,1,0:T(8,128)}) custom-call(bf16[32,2,16,128]{3,2,1,0:T(8,128)(2,1)} %get-tuple-element.69.refs_0_, bf16[2,2048,128]{2,1,0:T(8,128)(2,1)} %get-tuple-element.88.refs_1_, bf16[2,2048,128]{2,1,0:T(8,128)(2,1)} %get-tuple-element.87.refs_2_), custom_call_target="tpu_custom_call" | custom-call | flops 1073741824 | bytes 2621440 | tf_op jit(solution)/shard_map/pallas_call | solution.py:78
  118.0 0.9 slice_reduce_fusion.4
  119.0 0.8 slice_reduce_fusion.3
  120.0 0.8 slice_reduce_fusion.2
  120.9 6.1 %collective-permute-done.4 = bf16[16,2,64,2,128]{4,3,2,1,0:T(2,128)(2,1)S(1)} collective-permute-done((bf16[16,2,64,2,128]{4,3,2,1,0:T(2,128)(2,1)}, bf16[16,2,64,2,128]{4,3,2,1,0:T(2,128)(2,1)S(1)}, u32[]{:S(2)}, u32[]{:S(2)}) %collective-permute-start.4) | collective-permute-done | bytes 1048608 | tf_op jit(solution)/shard_map/ppermute | solution.py:19
  127.0 0.8 slice_reduce_fusion.1
  127.9 1.9 constant_dynamic-update-slice_fusion.5
  130.1 0.5 copy.156
  130.7 0.5 broadcast.489
  131.3 1.4 reduce.60
  132.6 1.6 reshape.374
  134.2 12.5 %all-to-all-start.1 = ((bf16[128,2,2112]{2,1,0:T(2,128)(2,1)}), bf16[128,2,2112]{2,1,0:T(2,128)(2,1)S(1)}, u32[]{:S(2)}, u32[]{:S(2)}) async-start(bf16[128,2,2112]{2,1,0:T(2,128)(2,1)} %reshape.374), calls=%async_computation.1 | async-start | bytes 2228224 | tf_op jit(solution)/shard_map/all_to_all | solution.py:172
  148.0 0.6 reshape_select_fusion.1.refs_0_
  148.6 2.9 %slice_bitcast_fusion = (bf16[2,32,64,128]{3,0,2,1:T(2,128)(2,1)S(1)}, bf16[2,32,64,128]{3,0,2,1:T(2,128)(2,1)S(1)}) fusion(bf16[32,2,64,2,128]{4,3,2,1,0:T(2,128)(2,1)} %constant_dynamic-update-slice_fusion.5), kind=kLoop, calls=%fused_computation.13 | loop fusion | bytes 4194304 | tf_op jit(solution)/shard_map/transpose | solution.py:179
  151.5 1.3 copy.118
  152.8 1.3 copy.117
  154.1 8.0 %shard_map.68 = (f32[2,512,128]{2,1,0:T(8,128)}, f32[2,1,8,512]{3,2,1,0:T(8,128)}) custom-call(s32[1,2048]{1,0:T(1,128)} %reshape_select_fusion.1.refs_0_, bf16[2,512,128]{2,1,0:T(8,128)(2,1)} %get-tuple-element.75.refs_1_, bf16[2,2048,128]{2,1,0:T(8,128)(2,1)} %bitcast.99, bf16[2,2048,128]{2,1,0:T(8,128)(2,1)} %bitcast.98), custom_call_target="tpu_custom_call" | custom-call | flops 1073741824 | bytes 2621440 | tf_op jit(solution)/shard_map/pallas_call | solution.py:78
  162.1 0.8 slice_reduce_fusion
  163.0 16.4 %all-to-all-done.1 = bf16[128,2,2112]{2,1,0:T(2,128)(2,1)S(1)} async-done(((bf16[128,2,2112]{2,1,0:T(2,128)(2,1)}), bf16[128,2,2112]{2,1,0:T(2,128)(2,1)S(1)}, u32[]{:S(2)}, u32[]{:S(2)}) %all-to-all-start.1) | async-done | bytes 1081376 | tf_op jit(solution)/shard_map/all_to_all | solution.py:172
  179.4 1.2 reshape.375
  180.6 2.7 %copy.121 = bf16[128,1,4224]{0,2,1:T(8,128)(2,1)S(1)} copy(bf16[128,1,4224]{2,1,0:T(2,128)(2,1)S(1)} %reshape.375) | data formatting | bytes 2162688 | tf_op jit(solution)/shard_map/all_to_all | solution.py:172
  183.4 0.2 convolution_bitcast_fusion
  183.7 0.2 copy.123
  184.1 0.5 fusion.5
  184.6 0.3 copy.144
  185.1 0.2 fusion.27
  185.7 0.5 multiply_reduce_fusion
  186.2 0.4 fusion.14
  186.7 10.8 %all_to_all.36 = bf16[4,16,2048]{2,1,0:T(8,128)(2,1)S(1)} all-to-all(bf16[4,16,2048]{2,1,0:T(8,128)(2,1)S(1)} %all_to_all.29), channel_id=1, replica_groups=mesh['seq'=128,'kvh'=4] {'kvh'}, dimensions={0} | all-to-all | bytes 524288 | tf_op jit(solution)/shard_map/all_to_all | solution.py:231
  197.5 0.7 copy.142
  (88 shorter events, 4.0 us)
Async XLA Ops:
  0.0 4.7 %copy-start = (bf16[64,16,128]{2,1,0:T(8,128)(2,1)S(1)}, bf16[64,16,128]{2,1,0:T(8,128)(2,1)}, u32[]{:S(2)}) copy-start(bf16[64,16,128]{2,1,0:T(8,128)(2,1)} %param.6) | copy-start | bytes 786436
  0.0 1.1 copy-start.1
  9.1 48.7 %all-to-all-start = ((bf16[128,2,16,128]{3,2,1,0:T(8,128)(2,1)}), bf16[128,2,16,128]{3,2,1,0:T(8,128)(2,1)S(1)}, u32[]{:S(2)}, u32[]{:S(2)}) async-start(bf16[128,2,16,128]{3,2,1,0:T(8,128)(2,1)} %reshape.201), calls=%async_computation | async-start | bytes 2097152 | tf_op jit(solution)/shard_map/all_to_all | solution.py:125
  26.5 31.3 %copy-start.2 = (bf16[2,64,2,128]{3,2,1,0:T(2,128)(2,1)S(1)}, bf16[2,64,2,128]{3,2,1,0:T(2,128)(2,1)}, u32[]{:S(2)}) copy-start(bf16[2,64,2,128]{3,2,1,0:T(2,128)(2,1)} %param.7) | copy-start | bytes 196612
  57.8 11.0 %collective-permute-start = (bf16[1,2,64,2,128]{4,3,2,1,0:T(2,128)(2,1)S(1)}, bf16[1,2,64,2,128]{4,3,2,1,0:T(2,128)(2,1)S(1)}, u32[]{:S(2)}, u32[]{:S(2)}) collective-permute-start(bf16[1,2,64,2,128]{4,3,2,1,0:T(2,128)(2,1)S(1)} %bitcast.102), channel_id=1, source_target_pairs={{0,32},{4,36},{8,40},{12,44},{16,48},{20,52},{24,56},{28,60},{32,6... | collective-permute-start | bytes 196616 | tf_op jit(solution)/shard_map/ppermute | solution.py:19
  69.0 11.1 %collective-permute-start.1 = (bf16[2,2,64,2,128]{4,3,2,1,0:T(2,128)(2,1)S(1)}, bf16[2,2,64,2,128]{4,3,2,1,0:T(2,128)(2,1)S(1)}, u32[]{:S(2)}, u32[]{:S(2)}) collective-permute-start(bf16[2,2,64,2,128]{4,3,2,1,0:T(2,128)(2,1)S(1)} %pad_maximum_fusion.3), channel_id=1, source_target_pairs={{0,16},{4,20},{8,24},{12,28},{16,32},{20,36},{24,40},{28,44},{32,4... | collective-permute-start | bytes 393224 | tf_op jit(solution)/shard_map/ppermute | solution.py:19
  80.6 10.2 %collective-permute-start.2 = (bf16[4,2,64,2,128]{4,3,2,1,0:T(2,128)(2,1)S(1)}, bf16[4,2,64,2,128]{4,3,2,1,0:T(2,128)(2,1)S(1)}, u32[]{:S(2)}, u32[]{:S(2)}) collective-permute-start(bf16[4,2,64,2,128]{4,3,2,1,0:T(2,128)(2,1)S(1)} %pad_maximum_fusion.2), channel_id=1, source_target_pairs={{0,64},{4,68},{8,72},{12,76},{16,80},{20,84},{24,88},{28,92},{32,9... | collective-permute-start | bytes 786440 | tf_op jit(solution)/shard_map/ppermute | solution.py:19
  91.6 15.0 %collective-permute-start.3 = (bf16[8,2,64,2,128]{4,3,2,1,0:T(2,128)(2,1)S(1)}, bf16[8,2,64,2,128]{4,3,2,1,0:T(2,128)(2,1)S(1)}, u32[]{:S(2)}, u32[]{:S(2)}) collective-permute-start(bf16[8,2,64,2,128]{4,3,2,1,0:T(2,128)(2,1)S(1)} %pad_maximum_fusion.1), channel_id=1, source_target_pairs={{0,8},{4,12},{8,16},{12,20},{16,24},{20,28},{24,32},{28,36},{32,40... | collective-permute-start | bytes 1572872 | tf_op jit(solution)/shard_map/ppermute | solution.py:19
  108.6 18.4 %collective-permute-start.4 = (bf16[16,2,64,2,128]{4,3,2,1,0:T(2,128)(2,1)}, bf16[16,2,64,2,128]{4,3,2,1,0:T(2,128)(2,1)S(1)}, u32[]{:S(2)}, u32[]{:S(2)}) collective-permute-start(bf16[16,2,64,2,128]{4,3,2,1,0:T(2,128)(2,1)} %get-tuple-element.74), channel_id=1, source_target_pairs={{0,4},{4,8},{8,12},{12,16},{16,20},{20,24},{24,28},{28,32},{32,36}... | collective-permute-start | bytes 3145736 | tf_op jit(solution)/shard_map/ppermute | solution.py:19
  118.0 11.9 %copy-start.4 = (bf16[32,2,16,128]{3,2,1,0:T(8,128)(2,1)S(1)}, bf16[32,2,16,128]{3,2,1,0:T(8,128)(2,1)}, u32[]{:S(2)}) copy-start(bf16[32,2,16,128]{3,2,1,0:T(8,128)(2,1)} %get-tuple-element.36) | copy-start | bytes 786436
  118.0 11.9 %copy-start.5 = (bf16[32,2,16,128]{3,2,1,0:T(8,128)(2,1)S(1)}, bf16[32,2,16,128]{3,2,1,0:T(8,128)(2,1)}, u32[]{:S(2)}) copy-start(bf16[32,2,16,128]{3,2,1,0:T(8,128)(2,1)} %get-tuple-element.40) | copy-start | bytes 786436
  118.0 11.8 %copy-start.6 = (bf16[32,2,16,128]{3,2,1,0:T(8,128)(2,1)S(1)}, bf16[32,2,16,128]{3,2,1,0:T(8,128)(2,1)}, u32[]{:S(2)}) copy-start(bf16[32,2,16,128]{3,2,1,0:T(8,128)(2,1)} %get-tuple-element.44) | copy-start | bytes 786436
  118.0 11.8 %copy-start.7 = (bf16[32,2,16,128]{3,2,1,0:T(8,128)(2,1)S(1)}, bf16[32,2,16,128]{3,2,1,0:T(8,128)(2,1)}, u32[]{:S(2)}) copy-start(bf16[32,2,16,128]{3,2,1,0:T(8,128)(2,1)} %get-tuple-element.48) | copy-start | bytes 786436
  134.2 45.2 %all-to-all-start.1 = ((bf16[128,2,2112]{2,1,0:T(2,128)(2,1)}), bf16[128,2,2112]{2,1,0:T(2,128)(2,1)S(1)}, u32[]{:S(2)}, u32[]{:S(2)}) async-start(bf16[128,2,2112]{2,1,0:T(2,128)(2,1)} %reshape.374), calls=%async_computation.1 | async-start | bytes 2228224 | tf_op jit(solution)/shard_map/all_to_all | solution.py:172
  184.9 1.2 copy-start.3

commit v6 on v5

--- a/solution.py
+++ b/solution.py
@@ -11,6 +11,7 @@
 BLOCK_PICK_LIMIT = 2
 WINDOW_SHIFTS = (8, 4, 16, 2, 1)
 LOG2_E = 1.4426950408889634
+SERVE_SPLIT = ((0, 2), (2, 3), (3, 4), (4, 5), (5, 8))
 
 
 def shifted(value, axis, steps):
@@ -19,7 +20,7 @@
     return lax.ppermute(value, axis, [(source, source + steps) for source in range(initial, last)])
 
 
-def gather_window(stretch_kv, span_devices, companions):
+def gather_window(stretch_kv, span_devices, partner, companions):
     stack = stretch_kv[None]
     offsets = [0]
     results = []
@@ -28,8 +29,10 @@
             break
         arrived = shifted(stack, "seq", step)
         if index < len(companions) and companions[index] is not None:
-            arrived, done = lax.optimization_barrier((arrived, companions[index]()))
-            results.append(done)
+            arrived, done, partner = lax.optimization_barrier(
+                (arrived, companions[index](partner), partner)
+            )
+            results.extend(done)
         stack = jnp.concatenate([stack, arrived], axis=0)
         offsets = offsets + [o + step for o in offsets]
     return stack, offsets, results
@@ -126,10 +129,10 @@
     arrived, window_start = lax.optimization_barrier((arrived, stretch_kv))
     cache_keys = jnp.swapaxes(cache_kv[0, 0], 0, 1)
     cache_values = jnp.swapaxes(cache_kv[1, 0], 0, 1)
-    sources_per_tile = 32
+    sources_per_tile = 16
     pieces = seq_count // sources_per_tile
 
-    def serve_piece(piece):
+    def serve_piece(piece, arrived):
         return attend(
             arrived[piece * sources_per_tile : (piece + 1) * sources_per_tile],
             (sources_per_tile, None, slab, head_dim),
@@ -143,10 +146,14 @@
             group_size,
         )
 
+    def serve_pieces(first, last, arrived):
+        return tuple(serve_piece(piece, arrived) for piece in range(first, last))
+
     window, offsets, served_pieces = gather_window(
         window_start,
         span_devices,
-        [None] + [functools.partial(serve_piece, piece) for piece in range(pieces)],
+        arrived,
+        [functools.partial(serve_pieces, first, last) for first, last in SERVE_SPLIT],
     )
     blocks = window.shape[0]
     served = jnp.concatenate([piece[0] for piece in served_pieces], axis=0)

time: 199 us -> 204 us (1.025)
  waiting for transfers between devices: 58.1 us -> 49.7 us
  local copies, waits for them, and re-layouts: 38.4 us -> 45.9 us
  Pallas kernels: 38 us -> 40.4 us
  starting transfers between devices: 43.6 us -> 46 us
    ppermute x5, waiting for transfers between devices: 13.1 us -> 5.28 us  [shifted(): lax.ppermute(value, axis, [(source, source + steps) for source in range(i...]
    unnamed x26 -> x37, local copies, waits for them, and re-layouts: 9.17 us -> 12 us
    slice x4 -> x8, local copies, waits for them, and re-layouts: 3.21 us -> 5.92 us  [per_device(): piece[1][:, :, 0].reshape(kv_heads, sources_per_tile, slab)]
    ppermute x5, starting transfers between devices: 13.7 us -> 16.4 us  [shifted(): lax.ppermute(value, axis, [(source, source + steps) for source in range(i...]
    slice x1 -> x5, local copies, waits for them, and re-layouts: 1.07 us -> 3.48 us  [serve_piece(): arrived[piece * sources_per_tile:(piece + 1) * sources_per_tile]]
    pallas_call x5 -> x9, Pallas kernels: 38 us -> 40.4 us  [attend(): pl.pallas_call(functools.partial(attend_kernel, thr is not None, scaling,...]
  transfers between devices with their start and end apart: 7 -> 7, of which waited for: 6 -> 4; matrix products, arithmetic and copies ran while one was open for 10% -> 12% of each run, Pallas kernels for 19% -> 20%
where the time goes in v6:
time: 204 us; the launch traced here: 203 us
  waiting for transfers between devices  49.7 us (24%)
  starting transfers between devices  46 us (23%)
  local copies, waits for them, and re-layouts  45.9 us (22%)
  Pallas kernels  40.4 us (20%)
  blocking collectives  10.8 us (5%)
  other arithmetic  8.39 us (4%)
    pallas_call x9, Pallas kernels, attend(): pl.pallas_call(functools.partial(attend_kernel, thr is not None, scaling,...  40.4 us
    all_to_all x1, waiting for transfers between devices, per_device(): lax.all_to_all(outgoing, 'seq', split_axis=0, concat_axis=0, tiled=True)  28.2 us
    all_to_all x1, starting transfers between devices, per_device(): lax.all_to_all(outgoing, 'seq', split_axis=0, concat_axis=0, tiled=True)  17.4 us
    ppermute x5, starting transfers between devices, shifted(): lax.ppermute(value, axis, [(source, source + steps) for source in range(i...  16.4 us
    all_to_all x1, waiting for transfers between devices, per_device(): lax.all_to_all(payload, 'seq', split_axis=0, concat_axis=0, tiled=True)  16.2 us
    all_to_all x1, starting transfers between devices, per_device(): lax.all_to_all(payload, 'seq', split_axis=0, concat_axis=0, tiled=True)  12.2 us
    unnamed x37, local copies, waits for them, and re-layouts  12 us
    all_to_all x1, blocking collectives, per_device(): lax.all_to_all(heads_out, 'kvh', split_axis=0, concat_axis=1, tiled=True)  10.8 us
  transfers between devices with their start and end apart: 7, of which 4 were waited for; matrix products, arithmetic and copies ran while one was open for 12% of the time, Pallas kernels for 20%

profile of v6, /device:TPU:8, one launch (start us, length us, event | category | flops | bytes accessed | tf_op | source)
XLA Modules:
  0.0 203.0 jit_solution(291127251497787406)
XLA Ops:
  0.0 0.7 compare_select_fusion.7
  1.1 2.7 %gather_fusion = s32[384]{0:T(512)S(1)} fusion(s32[128]{0:T(128)S(1)} %copy-done.1, s32[1024]{0:T(1024)S(1)} %pad_clamp_fusion), kind=kCustom, calls=%fused_computation | custom fusion | bytes 4608 | tf_op jit(solution)/shard_map/gather | solution.py:109
  4.7 0.8 copy_bitcast_fusion.3
  5.9 0.6 fusion.1
  6.5 1.1 copy.132
  7.6 1.5 reshape.201
  9.1 17.4 %all-to-all-start = ((bf16[128,2,16,128]{3,2,1,0:T(8,128)(2,1)}), bf16[128,2,16,128]{3,2,1,0:T(8,128)(2,1)S(1)}, u32[]{:S(2)}, u32[]{:S(2)}) async-start(bf16[128,2,16,128]{3,2,1,0:T(8,128)(2,1)} %reshape.201), calls=%async_computation | async-start | bytes 2097152 | tf_op jit(solution)/shard_map/all_to_all | solution.py:128
  26.5 1.5 fusion.28
  28.0 1.6 copy_bitcast_fusion.1
  29.6 28.2 %all-to-all-done = bf16[128,2,16,128]{3,2,1,0:T(8,128)(2,1)S(1)} async-done(((bf16[128,2,16,128]{3,2,1,0:T(8,128)(2,1)}), bf16[128,2,16,128]{3,2,1,0:T(8,128)(2,1)S(1)}, u32[]{:S(2)}, u32[]{:S(2)}) %all-to-all-start) | async-done | bytes 1048608 | tf_op jit(solution)/shard_map/all_to_all | solution.py:128
  57.8 0.7 constant_dynamic-update-slice_fusion.18
  58.6 3.3 %collective-permute-start = (bf16[1,2,64,2,128]{4,3,2,1,0:T(2,128)(2,1)S(1)}, bf16[1,2,64,2,128]{4,3,2,1,0:T(2,128)(2,1)S(1)}, u32[]{:S(2)}, u32[]{:S(2)}) collective-permute-start(bf16[1,2,64,2,128]{4,3,2,1,0:T(2,128)(2,1)S(1)} %bitcast.101), channel_id=1, source_target_pairs={{0,32},{4,36},{8,40},{12,44},{16,48},{20,52},{24,56},{28,60},{32,6... | collective-permute-start | bytes 196616 | tf_op jit(solution)/shard_map/ppermute | solution.py:20
  61.9 0.7 fusion.30
  62.6 4.0 %shard_map.65 = (bf16[16,2,16,128]{3,2,1,0:T(8,128)(2,1)}, f32[2,1,8,256]{3,2,1,0:T(8,128)}) custom-call(bf16[16,2,16,128]{3,2,1,0:T(8,128)(2,1)} %get-tuple-element.114.refs_0_, bf16[2,2048,128]{2,1,0:T(8,128)(2,1)} %get-tuple-element.131.refs_1_, bf16[2,2048,128]{2,1,0:T(8,128)(2,1)} %get-tuple-element.130.refs_2_), custom_call_target="tpu_custom_call" | custom-call | flops 536870912 | bytes 2359296 | tf_op jit(solution)/shard_map/pallas_call | solution.py:81
  66.7 4.0 %shard_map.64 = (bf16[16,2,16,128]{3,2,1,0:T(8,128)(2,1)}, f32[2,1,8,256]{3,2,1,0:T(8,128)}) custom-call(bf16[16,2,16,128]{3,2,1,0:T(8,128)(2,1)} %get-tuple-element.115.refs_0_, bf16[2,2048,128]{2,1,0:T(8,128)(2,1)} %get-tuple-element.131.refs_1_, bf16[2,2048,128]{2,1,0:T(8,128)(2,1)} %get-tuple-element.130.refs_2_), custom_call_target="tpu_custom_call" | custom-call | flops 536870912 | bytes 2359296 | tf_op jit(solution)/shard_map/pallas_call | solution.py:81
  70.9 3.4 %collective-permute-start.1 = (bf16[2,2,64,2,128]{4,3,2,1,0:T(2,128)(2,1)S(1)}, bf16[2,2,64,2,128]{4,3,2,1,0:T(2,128)(2,1)S(1)}, u32[]{:S(2)}, u32[]{:S(2)}) collective-permute-start(bf16[2,2,64,2,128]{4,3,2,1,0:T(2,128)(2,1)S(1)} %pad_maximum_fusion.2), channel_id=1, source_target_pairs={{0,16},{4,20},{8,24},{12,28},{16,32},{20,36},{24,40},{28,44},{32,4... | collective-permute-start | bytes 393224 | tf_op jit(solution)/shard_map/ppermute | solution.py:20
  74.2 0.7 slice_reduce_fusion.7
  75.1 0.7 slice.91.refs_0_
  75.8 4.0 %shard_map.66 = (bf16[16,2,16,128]{3,2,1,0:T(8,128)(2,1)}, f32[2,1,8,256]{3,2,1,0:T(8,128)}) custom-call(bf16[16,2,16,128]{3,2,1,0:T(8,128)(2,1)} %slice.91.refs_0_, bf16[2,2048,128]{2,1,0:T(8,128)(2,1)} %get-tuple-element.131.refs_1_, bf16[2,2048,128]{2,1,0:T(8,128)(2,1)} %get-tuple-element.130.refs_2_), custom_call_target="tpu_custom_call" | custom-call | flops 536870912 | bytes 2359296 | tf_op jit(solution)/shard_map/pallas_call | solution.py:81
  79.8 3.0 %collective-permute-done.1 = bf16[2,2,64,2,128]{4,3,2,1,0:T(2,128)(2,1)S(1)} collective-permute-done((bf16[2,2,64,2,128]{4,3,2,1,0:T(2,128)(2,1)S(1)}, bf16[2,2,64,2,128]{4,3,2,1,0:T(2,128)(2,1)S(1)}, u32[]{:S(2)}, u32[]{:S(2)}) %collective-permute-start.1) | collective-permute-done | bytes 131104 | tf_op jit(solution)/shard_map/ppermute | solution.py:20
  83.3 2.9 %collective-permute-start.2 = (bf16[4,2,64,2,128]{4,3,2,1,0:T(2,128)(2,1)S(1)}, bf16[4,2,64,2,128]{4,3,2,1,0:T(2,128)(2,1)S(1)}, u32[]{:S(2)}, u32[]{:S(2)}) collective-permute-start(bf16[4,2,64,2,128]{4,3,2,1,0:T(2,128)(2,1)S(1)} %pad_maximum_fusion.1), channel_id=1, source_target_pairs={{0,64},{4,68},{8,72},{12,76},{16,80},{20,84},{24,88},{28,92},{32,9... | collective-permute-start | bytes 786440 | tf_op jit(solution)/shard_map/ppermute | solution.py:20
  86.1 0.7 slice_reduce_fusion.8
  87.1 0.6 slice.92.refs_0_
  87.7 4.0 %shard_map.67 = (bf16[16,2,16,128]{3,2,1,0:T(8,128)(2,1)}, f32[2,1,8,256]{3,2,1,0:T(8,128)}) custom-call(bf16[16,2,16,128]{3,2,1,0:T(8,128)(2,1)} %slice.92.refs_0_, bf16[2,2048,128]{2,1,0:T(8,128)(2,1)} %get-tuple-element.131.refs_1_, bf16[2,2048,128]{2,1,0:T(8,128)(2,1)} %get-tuple-element.130.refs_2_), custom_call_target="tpu_custom_call" | custom-call | flops 536870912 | bytes 2359296 | tf_op jit(solution)/shard_map/pallas_call | solution.py:81
  91.7 1.6 pad_maximum_fusion
  93.3 4.9 %collective-permute-start.3 = (bf16[8,2,64,2,128]{4,3,2,1,0:T(2,128)(2,1)}, bf16[8,2,64,2,128]{4,3,2,1,0:T(2,128)(2,1)S(1)}, u32[]{:S(2)}, u32[]{:S(2)}) collective-permute-start(bf16[8,2,64,2,128]{4,3,2,1,0:T(2,128)(2,1)} %pad_maximum_fusion), channel_id=1, source_target_pairs={{0,8},{4,12},{8,16},{12,20},{16,24},{20,28},{24,32},{28,36},{32,40... | collective-permute-start | bytes 1572872 | tf_op jit(solution)/shard_map/ppermute | solution.py:20
  98.3 0.9 constant_dynamic-update-slice_fusion.11
  99.2 0.7 constant_dynamic-update-slice_fusion.17
  99.9 0.8 constant_dynamic-update-slice_fusion.16
  100.7 0.7 slice.93.refs_0_
  101.4 4.0 %shard_map.68 = (bf16[16,2,16,128]{3,2,1,0:T(8,128)(2,1)}, f32[2,1,8,256]{3,2,1,0:T(8,128)}) custom-call(bf16[16,2,16,128]{3,2,1,0:T(8,128)(2,1)} %slice.93.refs_0_, bf16[2,2048,128]{2,1,0:T(8,128)(2,1)} %get-tuple-element.131.refs_1_, bf16[2,2048,128]{2,1,0:T(8,128)(2,1)} %get-tuple-element.130.refs_2_), custom_call_target="tpu_custom_call" | custom-call | flops 536870912 | bytes 2359296 | tf_op jit(solution)/shard_map/pallas_call | solution.py:81
  105.4 1.2 constant_dynamic-update-slice_fusion.15
  106.6 2.2 %collective-permute-done.3 = bf16[8,2,64,2,128]{4,3,2,1,0:T(2,128)(2,1)S(1)} collective-permute-done((bf16[8,2,64,2,128]{4,3,2,1,0:T(2,128)(2,1)}, bf16[8,2,64,2,128]{4,3,2,1,0:T(2,128)(2,1)S(1)}, u32[]{:S(2)}, u32[]{:S(2)}) %collective-permute-start.3) | collective-permute-done | bytes 524320 | tf_op jit(solution)/shard_map/ppermute | solution.py:20
  108.9 2.0 constant_dynamic-update-slice_fusion.14
  110.8 1.9 collective-permute-start.4
  112.7 0.7 slice_reduce_fusion.6
  113.6 0.9 constant_dynamic-update-slice_fusion.10
  114.6 0.7 slice_reduce_fusion.5
  115.4 0.9 constant_dynamic-update-slice_fusion.9
  116.4 0.7 slice_reduce_fusion.4
  117.3 0.8 fusion.29
  118.0 4.0 %shard_map.71 = (bf16[16,2,16,128]{3,2,1,0:T(8,128)(2,1)}, f32[2,1,8,256]{3,2,1,0:T(8,128)}) custom-call(bf16[16,2,16,128]{3,2,1,0:T(8,128)(2,1)} %get-tuple-element.111.refs_0_, bf16[2,2048,128]{2,1,0:T(8,128)(2,1)} %get-tuple-element.131.refs_1_, bf16[2,2048,128]{2,1,0:T(8,128)(2,1)} %get-tuple-element.130.refs_2_), custom_call_target="tpu_custom_call" | custom-call | flops 536870912 | bytes 2359296 | tf_op jit(solution)/shard_map/pallas_call | solution.py:81
  122.1 4.1 %shard_map.70 = (bf16[16,2,16,128]{3,2,1,0:T(8,128)(2,1)}, f32[2,1,8,256]{3,2,1,0:T(8,128)}) custom-call(bf16[16,2,16,128]{3,2,1,0:T(8,128)(2,1)} %get-tuple-element.112.refs_0_, bf16[2,2048,128]{2,1,0:T(8,128)(2,1)} %get-tuple-element.131.refs_1_, bf16[2,2048,128]{2,1,0:T(8,128)(2,1)} %get-tuple-element.130.refs_2_), custom_call_target="tpu_custom_call" | custom-call | flops 536870912 | bytes 2359296 | tf_op jit(solution)/shard_map/pallas_call | solution.py:81
  126.2 4.1 %shard_map.69 = (bf16[16,2,16,128]{3,2,1,0:T(8,128)(2,1)}, f32[2,1,8,256]{3,2,1,0:T(8,128)}) custom-call(bf16[16,2,16,128]{3,2,1,0:T(8,128)(2,1)} %get-tuple-element.113.refs_0_, bf16[2,2048,128]{2,1,0:T(8,128)(2,1)} %get-tuple-element.131.refs_1_, bf16[2,2048,128]{2,1,0:T(8,128)(2,1)} %get-tuple-element.130.refs_2_), custom_call_target="tpu_custom_call" | custom-call | flops 536870912 | bytes 2359296 | tf_op jit(solution)/shard_map/pallas_call | solution.py:81
  130.3 0.8 slice_reduce_fusion.3
  131.1 0.7 slice_reduce_fusion.2
  131.8 0.7 slice_reduce_fusion.1
  133.0 1.9 constant_dynamic-update-slice_fusion.13
  135.8 0.5 broadcast.493
  136.3 1.4 reduce.68
  137.7 1.6 reshape.378
  139.3 12.2 %all-to-all-start.1 = ((bf16[128,2,2112]{2,1,0:T(2,128)(2,1)}), bf16[128,2,2112]{2,1,0:T(2,128)(2,1)S(1)}, u32[]{:S(2)}, u32[]{:S(2)}) async-start(bf16[128,2,2112]{2,1,0:T(2,128)(2,1)} %reshape.378), calls=%async_computation.1 | async-start | bytes 2228224 | tf_op jit(solution)/shard_map/all_to_all | solution.py:179
  153.0 0.6 reshape_select_fusion.1.refs_0_
  153.6 2.9 %slice_bitcast_fusion = (bf16[2,32,64,128]{3,0,2,1:T(2,128)(2,1)S(1)}, bf16[2,32,64,128]{3,0,2,1:T(2,128)(2,1)S(1)}) fusion(bf16[32,2,64,2,128]{4,3,2,1,0:T(2,128)(2,1)} %constant_dynamic-update-slice_fusion.13), kind=kLoop, calls=%fused_computation.12 | loop fusion | bytes 4194304 | tf_op jit(solution)/shard_map/transpose | solution.py:186
  156.5 1.3 copy.144
  157.8 1.3 copy.143
  159.1 8.0 %shard_map.72 = (f32[2,512,128]{2,1,0:T(8,128)}, f32[2,1,8,512]{3,2,1,0:T(8,128)}) custom-call(s32[1,2048]{1,0:T(1,128)} %reshape_select_fusion.1.refs_0_, bf16[2,512,128]{2,1,0:T(8,128)(2,1)} %get-tuple-element.118.refs_1_, bf16[2,2048,128]{2,1,0:T(8,128)(2,1)} %bitcast.98, bf16[2,2048,128]{2,1,0:T(8,128)(2,1)} %bitcast.97), custom_call_target="tpu_custom_call" | custom-call | flops 1073741824 | bytes 2621440 | tf_op jit(solution)/shard_map/pallas_call | solution.py:81
  167.1 0.8 slice_reduce_fusion
  168.0 16.2 %all-to-all-done.1 = bf16[128,2,2112]{2,1,0:T(2,128)(2,1)S(1)} async-done(((bf16[128,2,2112]{2,1,0:T(2,128)(2,1)}), bf16[128,2,2112]{2,1,0:T(2,128)(2,1)S(1)}, u32[]{:S(2)}, u32[]{:S(2)}) %all-to-all-start.1) | async-done | bytes 1081376 | tf_op jit(solution)/shard_map/all_to_all | solution.py:179
  184.2 1.2 reshape.379
  185.4 2.7 %copy.147 = bf16[128,1,4224]{0,2,1:T(8,128)(2,1)S(1)} copy(bf16[128,1,4224]{2,1,0:T(2,128)(2,1)S(1)} %reshape.379) | data formatting | bytes 2162688 | tf_op jit(solution)/shard_map/all_to_all | solution.py:179
  190.4 0.5 multiply_reduce_fusion
  191.5 10.8 %all_to_all.36 = bf16[4,16,2048]{2,1,0:T(8,128)(2,1)S(1)} all-to-all(bf16[4,16,2048]{2,1,0:T(8,128)(2,1)S(1)} %all_to_all.29), channel_id=1, replica_groups=mesh['seq'=128,'kvh'=4] {'kvh'}, dimensions={0} | all-to-all | bytes 524288 | tf_op jit(solution)/shard_map/all_to_all | solution.py:238
  202.3 0.7 copy.168
  (119 shorter events, 8.6 us)
Async XLA Ops:
  0.0 4.7 %copy-start = (bf16[64,16,128]{2,1,0:T(8,128)(2,1)S(1)}, bf16[64,16,128]{2,1,0:T(8,128)(2,1)}, u32[]{:S(2)}) copy-start(bf16[64,16,128]{2,1,0:T(8,128)(2,1)} %param.6) | copy-start | bytes 786436
  0.0 1.1 copy-start.1
  7.6 18.9 %copy-start.2 = (bf16[2,1,2048,2,128]{4,3,2,1,0:T(2,128)(2,1)S(1)}, bf16[2,1,2048,2,128]{4,3,2,1,0:T(2,128)(2,1)}, u32[]{:S(2)}) copy-start(bf16[2,1,2048,2,128]{4,3,2,1,0:T(2,128)(2,1)} %param.8) | copy-start | bytes 6291460
  9.1 48.7 %all-to-all-start = ((bf16[128,2,16,128]{3,2,1,0:T(8,128)(2,1)}), bf16[128,2,16,128]{3,2,1,0:T(8,128)(2,1)S(1)}, u32[]{:S(2)}, u32[]{:S(2)}) async-start(bf16[128,2,16,128]{3,2,1,0:T(8,128)(2,1)} %reshape.201), calls=%async_computation | async-start | bytes 2097152 | tf_op jit(solution)/shard_map/all_to_all | solution.py:128
  28.0 29.8 %copy-start.3 = (bf16[2,64,2,128]{3,2,1,0:T(2,128)(2,1)S(1)}, bf16[2,64,2,128]{3,2,1,0:T(2,128)(2,1)}, u32[]{:S(2)}) copy-start(bf16[2,64,2,128]{3,2,1,0:T(2,128)(2,1)} %param.7) | copy-start | bytes 196612
  58.6 12.1 %collective-permute-start = (bf16[1,2,64,2,128]{4,3,2,1,0:T(2,128)(2,1)S(1)}, bf16[1,2,64,2,128]{4,3,2,1,0:T(2,128)(2,1)S(1)}, u32[]{:S(2)}, u32[]{:S(2)}) collective-permute-start(bf16[1,2,64,2,128]{4,3,2,1,0:T(2,128)(2,1)S(1)} %bitcast.101), channel_id=1, source_target_pairs={{0,32},{4,36},{8,40},{12,44},{16,48},{20,52},{24,56},{28,60},{32,6... | collective-permute-start | bytes 196616 | tf_op jit(solution)/shard_map/ppermute | solution.py:20
  70.7 16.4 %copy-start.8 = (bf16[16,2,16,128]{3,2,1,0:T(8,128)(2,1)S(1)}, bf16[16,2,16,128]{3,2,1,0:T(8,128)(2,1)}, u32[]{:S(2)}) copy-start(bf16[16,2,16,128]{3,2,1,0:T(8,128)(2,1)} %get-tuple-element.59) | copy-start | bytes 393220
  70.9 12.0 %collective-permute-start.1 = (bf16[2,2,64,2,128]{4,3,2,1,0:T(2,128)(2,1)S(1)}, bf16[2,2,64,2,128]{4,3,2,1,0:T(2,128)(2,1)S(1)}, u32[]{:S(2)}, u32[]{:S(2)}) collective-permute-start(bf16[2,2,64,2,128]{4,3,2,1,0:T(2,128)(2,1)S(1)} %pad_maximum_fusion.2), channel_id=1, source_target_pairs={{0,16},{4,20},{8,24},{12,28},{16,32},{20,36},{24,40},{28,44},{32,4... | collective-permute-start | bytes 393224 | tf_op jit(solution)/shard_map/ppermute | solution.py:20
  83.3 8.5 %collective-permute-start.2 = (bf16[4,2,64,2,128]{4,3,2,1,0:T(2,128)(2,1)S(1)}, bf16[4,2,64,2,128]{4,3,2,1,0:T(2,128)(2,1)S(1)}, u32[]{:S(2)}, u32[]{:S(2)}) collective-permute-start(bf16[4,2,64,2,128]{4,3,2,1,0:T(2,128)(2,1)S(1)} %pad_maximum_fusion.1), channel_id=1, source_target_pairs={{0,64},{4,68},{8,72},{12,76},{16,80},{20,84},{24,88},{28,92},{32,9... | collective-permute-start | bytes 786440 | tf_op jit(solution)/shard_map/ppermute | solution.py:20
  93.3 15.6 %collective-permute-start.3 = (bf16[8,2,64,2,128]{4,3,2,1,0:T(2,128)(2,1)}, bf16[8,2,64,2,128]{4,3,2,1,0:T(2,128)(2,1)S(1)}, u32[]{:S(2)}, u32[]{:S(2)}) collective-permute-start(bf16[8,2,64,2,128]{4,3,2,1,0:T(2,128)(2,1)} %pad_maximum_fusion), channel_id=1, source_target_pairs={{0,8},{4,12},{8,16},{12,20},{16,24},{20,28},{24,32},{28,36},{32,40... | collective-permute-start | bytes 1572872 | tf_op jit(solution)/shard_map/ppermute | solution.py:20
  110.8 19.5 %collective-permute-start.4 = (bf16[16,2,64,2,128]{4,3,2,1,0:T(2,128)(2,1)}, bf16[16,2,64,2,128]{4,3,2,1,0:T(2,128)(2,1)S(1)}, u32[]{:S(2)}, u32[]{:S(2)}) collective-permute-start(bf16[16,2,64,2,128]{4,3,2,1,0:T(2,128)(2,1)} %get-tuple-element.117), channel_id=1, source_target_pairs={{0,4},{4,8},{8,12},{12,16},{16,20},{20,24},{24,28},{28,32},{32,36}... | collective-permute-start | bytes 3145736 | tf_op jit(solution)/shard_map/ppermute | solution.py:20
  122.1 8.2 %copy-start.5 = (bf16[16,2,16,128]{3,2,1,0:T(8,128)(2,1)S(1)}, bf16[16,2,16,128]{3,2,1,0:T(8,128)(2,1)}, u32[]{:S(2)}) copy-start(bf16[16,2,16,128]{3,2,1,0:T(8,128)(2,1)} %get-tuple-element.75) | copy-start | bytes 393220
  126.2 8.8 %copy-start.7 = (bf16[16,2,16,128]{3,2,1,0:T(8,128)(2,1)S(1)}, bf16[16,2,16,128]{3,2,1,0:T(8,128)(2,1)}, u32[]{:S(2)}) copy-start(bf16[16,2,16,128]{3,2,1,0:T(8,128)(2,1)} %get-tuple-element.85) | copy-start | bytes 393220
  126.2 8.8 %copy-start.6 = (bf16[16,2,16,128]{3,2,1,0:T(8,128)(2,1)S(1)}, bf16[16,2,16,128]{3,2,1,0:T(8,128)(2,1)}, u32[]{:S(2)}) copy-start(bf16[16,2,16,128]{3,2,1,0:T(8,128)(2,1)} %get-tuple-element.86) | copy-start | bytes 393220
  130.3 4.7 %copy-start.9 = (bf16[16,2,16,128]{3,2,1,0:T(8,128)(2,1)S(1)}, bf16[16,2,16,128]{3,2,1,0:T(8,128)(2,1)}, u32[]{:S(2)}) copy-start(bf16[16,2,16,128]{3,2,1,0:T(8,128)(2,1)} %get-tuple-element.84) | copy-start | bytes 393220
  139.3 44.9 %all-to-all-start.1 = ((bf16[128,2,2112]{2,1,0:T(2,128)(2,1)}), bf16[128,2,2112]{2,1,0:T(2,128)(2,1)S(1)}, u32[]{:S(2)}, u32[]{:S(2)}) async-start(bf16[128,2,2112]{2,1,0:T(2,128)(2,1)} %reshape.378), calls=%async_computation.1 | async-start | bytes 2228224 | tf_op jit(solution)/shard_map/all_to_all | solution.py:179
  189.7 1.2 copy-start.4

commit v7 on v5

--- a/solution.py
+++ b/solution.py
@@ -103,7 +103,10 @@
     seq_place = lax.axis_index("seq")
     grouped = queries.reshape(rows_local, kv_heads, group_size, head_dim)
     requests = rows_local * top_count
-    targets = block_owner[selection].reshape(kv_heads, requests)
+    owners = jnp.arange(block_owner.shape[0], dtype=jnp.int32)
+    targets = jnp.sum(
+        jnp.where(selection[..., None] == owners, block_owner, 0), axis=-1
+    ).reshape(kv_heads, requests)
     matches = (targets[:, :, None] == jnp.arange(seq_count, dtype=jnp.int32)[None, None, :]).astype(
         jnp.int32
     )
@@ -114,11 +117,9 @@
         .astype(jnp.bfloat16)
         .reshape(kv_heads, seq_count, capacity, requests)
     )
-    requested = jnp.repeat(jnp.swapaxes(grouped, 0, 1), top_count, axis=1).reshape(
-        kv_heads, requests, group_size * head_dim
-    )
+    requested = jnp.repeat(jnp.swapaxes(grouped, 0, 1), top_count, axis=1)
     outgoing = jnp.einsum(
-        "htcr,hrx->thcx", one_hot, requested, preferred_element_type=jnp.float32
+        "htcr,hrgd->thcgd", one_hot, requested, preferred_element_type=jnp.float32
     ).astype(jnp.bfloat16)
     slab = capacity * group_size
     outgoing = outgoing.reshape(seq_count, kv_heads, slab, head_dim)

time: 199 us -> 196 us (0.985)
  local copies, waits for them, and re-layouts: 38.4 us -> 35.1 us
    gather x1 -> x0, local copies, waits for them, and re-layouts: 2.69 us -> none  [per_device(): targets = block_owner[selection].reshape(kv_heads, requests)]
    unnamed x26 -> x25, local copies, waits for them, and re-layouts: 9.17 us -> 9.89 us
  transfers between devices with their start and end apart: 7 -> 7, of which waited for: 6 -> 6; matrix products, arithmetic and copies ran while one was open for 10% -> 10% of each run, Pallas kernels for 19% -> 20%
where the time goes in v7:
time: 196 us; the launch traced here: 195 us
  waiting for transfers between devices  57.7 us (29%)
  starting transfers between devices  43.3 us (22%)
  Pallas kernels  38 us (19%)
  local copies, waits for them, and re-layouts  35.1 us (18%)
  blocking collectives  10.8 us (6%)
  other arithmetic  7.98 us (4%)
    pallas_call x5, Pallas kernels, attend(): pl.pallas_call(functools.partial(attend_kernel, thr is not None, scaling,...  38 us
    all_to_all x1, waiting for transfers between devices, per_device(): lax.all_to_all(outgoing, 'seq', split_axis=0, concat_axis=0, tiled=True)  28.6 us
    all_to_all x1, starting transfers between devices, per_device(): lax.all_to_all(outgoing, 'seq', split_axis=0, concat_axis=0, tiled=True)  17.4 us
    all_to_all x1, waiting for transfers between devices, per_device(): lax.all_to_all(payload, 'seq', split_axis=0, concat_axis=0, tiled=True)  16.2 us
    ppermute x5, starting transfers between devices, shifted(): lax.ppermute(value, axis, [(source, source + steps) for source in range(i...  13.7 us
    ppermute x5, waiting for transfers between devices, shifted(): lax.ppermute(value, axis, [(source, source + steps) for source in range(i...  12.9 us
    all_to_all x1, starting transfers between devices, per_device(): lax.all_to_all(payload, 'seq', split_axis=0, concat_axis=0, tiled=True)  12.2 us
    all_to_all x1, blocking collectives, per_device(): lax.all_to_all(heads_out, 'kvh', split_axis=0, concat_axis=1, tiled=True)  10.8 us
  transfers between devices with their start and end apart: 7, of which 6 were waited for; matrix products, arithmetic and copies ran while one was open for 10% of the time, Pallas kernels for 20%

profile of v7, /device:TPU:8, one launch (start us, length us, event | category | flops | bytes accessed | tf_op | source)
XLA Modules:
  0.0 194.6 jit_solution(15370552582214555765)
XLA Ops:
  0.0 0.7 copy.141
  0.7 0.9 select_reduce_fusion
  1.8 0.1 reshape.202
  2.1 0.2 fusion.11
  2.5 0.2 fusion.15
  2.8 0.8 copy_bitcast_fusion.4
  3.6 0.6 fusion.1
  4.2 1.7 copy.199
  5.9 17.4 %all-to-all-start = ((bf16[128,2,16,128]{3,2,1,0:T(8,128)(2,1)}), bf16[128,2,16,128]{3,2,1,0:T(8,128)(2,1)S(1)}, u32[]{:S(2)}, u32[]{:S(2)}) async-start(bf16[128,2,16,128]{3,2,1,0:T(8,128)(2,1)} %bitcast.94), calls=%async_computation | async-start | bytes 2097152 | tf_op jit(solution)/shard_map/all_to_all | solution.py:126
  23.3 2.7 %fusion.27 = (bf16[1,1,2048,2,128]{4,3,2,1,0:T(2,128)(2,1)S(1)}, bf16[1,1,2048,2,128]{4,3,2,1,0:T(2,128)(2,1)S(1)}) fusion(bf16[2,1,2048,2,128]{4,3,2,1,0:T(2,128)(2,1)} %param.8), kind=kLoop, calls=%fused_computation.120 | loop fusion | bytes 4194304 | tf_op jit(solution)/shard_map/slice | solution.py:129
  26.0 28.6 %all-to-all-done = bf16[128,2,16,128]{3,2,1,0:T(8,128)(2,1)S(1)} async-done(((bf16[128,2,16,128]{3,2,1,0:T(8,128)(2,1)}), bf16[128,2,16,128]{3,2,1,0:T(8,128)(2,1)S(1)}, u32[]{:S(2)}, u32[]{:S(2)}) %all-to-all-start) | async-done | bytes 1048608 | tf_op jit(solution)/shard_map/all_to_all | solution.py:126
  54.6 3.3 %collective-permute-start = (bf16[1,2,64,2,128]{4,3,2,1,0:T(2,128)(2,1)S(1)}, bf16[1,2,64,2,128]{4,3,2,1,0:T(2,128)(2,1)S(1)}, u32[]{:S(2)}, u32[]{:S(2)}) collective-permute-start(bf16[1,2,64,2,128]{4,3,2,1,0:T(2,128)(2,1)S(1)} %bitcast.109), channel_id=1, source_target_pairs={{0,32},{4,36},{8,40},{12,44},{16,48},{20,52},{24,56},{28,60},{32,6... | collective-permute-start | bytes 196616 | tf_op jit(solution)/shard_map/ppermute | solution.py:19
  57.9 1.6 copy_bitcast_fusion.1
  59.5 6.1 %collective-permute-done = bf16[1,2,64,2,128]{4,3,2,1,0:T(2,128)(2,1)S(1)} collective-permute-done((bf16[1,2,64,2,128]{4,3,2,1,0:T(2,128)(2,1)S(1)}, bf16[1,2,64,2,128]{4,3,2,1,0:T(2,128)(2,1)S(1)}, u32[]{:S(2)}, u32[]{:S(2)}) %collective-permute-start) | collective-permute-done | bytes 65568 | tf_op jit(solution)/shard_map/ppermute | solution.py:19
  65.7 0.2 pad_maximum_fusion.3
  65.8 2.4 %collective-permute-start.1 = (bf16[2,2,64,2,128]{4,3,2,1,0:T(2,128)(2,1)S(1)}, bf16[2,2,64,2,128]{4,3,2,1,0:T(2,128)(2,1)S(1)}, u32[]{:S(2)}, u32[]{:S(2)}) collective-permute-start(bf16[2,2,64,2,128]{4,3,2,1,0:T(2,128)(2,1)S(1)} %pad_maximum_fusion.3), channel_id=1, source_target_pairs={{0,16},{4,20},{8,24},{12,28},{16,32},{20,36},{24,40},{28,44},{32,4... | collective-permute-start | bytes 393224 | tf_op jit(solution)/shard_map/ppermute | solution.py:19
  68.2 1.1 fusion.28
  69.3 7.5 %shard_map.64 = (bf16[32,2,16,128]{3,2,1,0:T(8,128)(2,1)}, f32[2,1,8,512]{3,2,1,0:T(8,128)}) custom-call(bf16[32,2,16,128]{3,2,1,0:T(8,128)(2,1)} %get-tuple-element.72.refs_0_, bf16[2,2048,128]{2,1,0:T(8,128)(2,1)} %get-tuple-element.88.refs_1_, bf16[2,2048,128]{2,1,0:T(8,128)(2,1)} %get-tuple-element.87.refs_2_), custom_call_target="tpu_custom_call" | custom-call | flops 1073741824 | bytes 2621440 | tf_op jit(solution)/shard_map/pallas_call | solution.py:78
  76.7 0.2 collective-permute-done.1
  77.0 0.4 pad_maximum_fusion.2
  77.4 2.5 %collective-permute-start.2 = (bf16[4,2,64,2,128]{4,3,2,1,0:T(2,128)(2,1)S(1)}, bf16[4,2,64,2,128]{4,3,2,1,0:T(2,128)(2,1)S(1)}, u32[]{:S(2)}, u32[]{:S(2)}) collective-permute-start(bf16[4,2,64,2,128]{4,3,2,1,0:T(2,128)(2,1)S(1)} %pad_maximum_fusion.2), channel_id=1, source_target_pairs={{0,64},{4,68},{8,72},{12,76},{16,80},{20,84},{24,88},{28,92},{32,9... | collective-permute-start | bytes 786440 | tf_op jit(solution)/shard_map/ppermute | solution.py:19
  79.9 7.5 %shard_map.65 = (bf16[32,2,16,128]{3,2,1,0:T(8,128)(2,1)}, f32[2,1,8,512]{3,2,1,0:T(8,128)}) custom-call(bf16[32,2,16,128]{3,2,1,0:T(8,128)(2,1)} %get-tuple-element.71.refs_0_, bf16[2,2048,128]{2,1,0:T(8,128)(2,1)} %get-tuple-element.88.refs_1_, bf16[2,2048,128]{2,1,0:T(8,128)(2,1)} %get-tuple-element.87.refs_2_), custom_call_target="tpu_custom_call" | custom-call | flops 1073741824 | bytes 2621440 | tf_op jit(solution)/shard_map/pallas_call | solution.py:78
  87.4 0.7 pad_maximum_fusion.1
  88.2 3.6 %collective-permute-start.3 = (bf16[8,2,64,2,128]{4,3,2,1,0:T(2,128)(2,1)S(1)}, bf16[8,2,64,2,128]{4,3,2,1,0:T(2,128)(2,1)S(1)}, u32[]{:S(2)}, u32[]{:S(2)}) collective-permute-start(bf16[8,2,64,2,128]{4,3,2,1,0:T(2,128)(2,1)S(1)} %pad_maximum_fusion.1), channel_id=1, source_target_pairs={{0,8},{4,12},{8,16},{12,20},{16,24},{20,28},{24,32},{28,36},{32,40... | collective-permute-start | bytes 1572872 | tf_op jit(solution)/shard_map/ppermute | solution.py:19
  91.8 0.7 constant_dynamic-update-slice_fusion.10
  92.5 7.5 %shard_map.66 = (bf16[32,2,16,128]{3,2,1,0:T(8,128)(2,1)}, f32[2,1,8,512]{3,2,1,0:T(8,128)}) custom-call(bf16[32,2,16,128]{3,2,1,0:T(8,128)(2,1)} %get-tuple-element.70.refs_0_, bf16[2,2048,128]{2,1,0:T(8,128)(2,1)} %get-tuple-element.88.refs_1_, bf16[2,2048,128]{2,1,0:T(8,128)(2,1)} %get-tuple-element.87.refs_2_), custom_call_target="tpu_custom_call" | custom-call | flops 1073741824 | bytes 2621440 | tf_op jit(solution)/shard_map/pallas_call | solution.py:78
  100.0 0.7 constant_dynamic-update-slice_fusion.9
  100.7 0.8 constant_dynamic-update-slice_fusion.8
  101.5 1.2 constant_dynamic-update-slice_fusion.7
  102.7 0.5 collective-permute-done.3
  103.2 2.0 %constant_dynamic-update-slice_fusion.6 = (bf16[32,2,64,2,128]{4,3,2,1,0:T(2,128)(2,1)}, bf16[16,2,64,2,128]{4,3,2,1,0:T(2,128)(2,1)}) fusion(bf16[32,2,64,2,128]{4,3,2,1,0:T(2,128)(2,1)} %get-tuple-element.77, bf16[8,2,64,2,128]{4,3,2,1,0:T(2,128)(2,1)S(1)} %collective-permute-done.3, bf16[16,2,64,2,128]{4,3,2,1,0:T(2,128)(2,1)} %get-tuple-element.78), kind=kLoop, calls=%fused_computation.90 | loop fusion | bytes 1572864
  105.2 1.9 collective-permute-start.4
  107.1 7.5 %shard_map.67 = (bf16[32,2,16,128]{3,2,1,0:T(8,128)(2,1)}, f32[2,1,8,512]{3,2,1,0:T(8,128)}) custom-call(bf16[32,2,16,128]{3,2,1,0:T(8,128)(2,1)} %get-tuple-element.69.refs_0_, bf16[2,2048,128]{2,1,0:T(8,128)(2,1)} %get-tuple-element.88.refs_1_, bf16[2,2048,128]{2,1,0:T(8,128)(2,1)} %get-tuple-element.87.refs_2_), custom_call_target="tpu_custom_call" | custom-call | flops 1073741824 | bytes 2621440 | tf_op jit(solution)/shard_map/pallas_call | solution.py:78
  114.6 0.9 slice_reduce_fusion.4
  115.6 0.8 slice_reduce_fusion.3
  116.6 0.8 slice_reduce_fusion.2
  117.5 6.1 %collective-permute-done.4 = bf16[16,2,64,2,128]{4,3,2,1,0:T(2,128)(2,1)S(1)} collective-permute-done((bf16[16,2,64,2,128]{4,3,2,1,0:T(2,128)(2,1)}, bf16[16,2,64,2,128]{4,3,2,1,0:T(2,128)(2,1)S(1)}, u32[]{:S(2)}, u32[]{:S(2)}) %collective-permute-start.4) | collective-permute-done | bytes 1048608 | tf_op jit(solution)/shard_map/ppermute | solution.py:19
  123.6 0.8 slice_reduce_fusion.1
  124.5 1.9 constant_dynamic-update-slice_fusion.5
  126.7 0.5 copy.198
  127.4 0.5 broadcast.486
  127.9 1.4 reduce.60
  129.3 1.6 reshape.368
  130.9 12.2 %all-to-all-start.1 = ((bf16[128,2,2112]{2,1,0:T(2,128)(2,1)}), bf16[128,2,2112]{2,1,0:T(2,128)(2,1)S(1)}, u32[]{:S(2)}, u32[]{:S(2)}) async-start(bf16[128,2,2112]{2,1,0:T(2,128)(2,1)} %reshape.368), calls=%async_computation.1 | async-start | bytes 2228224 | tf_op jit(solution)/shard_map/all_to_all | solution.py:173
  144.2 0.3 compare_reduce_fusion
  144.6 0.6 reshape_select_fusion.1.refs_0_
  145.2 2.9 %slice_bitcast_fusion = (bf16[2,32,64,128]{3,0,2,1:T(2,128)(2,1)S(1)}, bf16[2,32,64,128]{3,0,2,1:T(2,128)(2,1)S(1)}) fusion(bf16[32,2,64,2,128]{4,3,2,1,0:T(2,128)(2,1)} %constant_dynamic-update-slice_fusion.5), kind=kLoop, calls=%fused_computation.13 | loop fusion | bytes 4194304 | tf_op jit(solution)/shard_map/transpose | solution.py:180
  148.1 1.3 copy.154
  149.5 1.3 copy.153
  150.7 8.0 %shard_map.68 = (f32[2,512,128]{2,1,0:T(8,128)}, f32[2,1,8,512]{3,2,1,0:T(8,128)}) custom-call(s32[1,2048]{1,0:T(1,128)} %reshape_select_fusion.1.refs_0_, bf16[2,512,128]{2,1,0:T(8,128)(2,1)} %get-tuple-element.75.refs_1_, bf16[2,2048,128]{2,1,0:T(8,128)(2,1)} %bitcast.106, bf16[2,2048,128]{2,1,0:T(8,128)(2,1)} %bitcast.105), custom_call_target="tpu_custom_call" | custom-call | flops 1073741824 | bytes 2621440 | tf_op jit(solution)/shard_map/pallas_call | solution.py:78
  158.7 0.8 slice_reduce_fusion
  159.7 16.2 %all-to-all-done.1 = bf16[128,2,2112]{2,1,0:T(2,128)(2,1)S(1)} async-done(((bf16[128,2,2112]{2,1,0:T(2,128)(2,1)}), bf16[128,2,2112]{2,1,0:T(2,128)(2,1)S(1)}, u32[]{:S(2)}, u32[]{:S(2)}) %all-to-all-start.1) | async-done | bytes 1081376 | tf_op jit(solution)/shard_map/all_to_all | solution.py:173
  175.8 1.2 reshape.369
  177.0 2.7 %copy.157 = bf16[128,1,4224]{0,2,1:T(8,128)(2,1)S(1)} copy(bf16[128,1,4224]{2,1,0:T(2,128)(2,1)S(1)} %reshape.369) | data formatting | bytes 2162688 | tf_op jit(solution)/shard_map/all_to_all | solution.py:173
  179.8 0.2 convolution_bitcast_fusion
  180.1 0.2 copy.159
  180.3 0.1 reduce_max.9
  180.5 0.5 fusion.5
  181.0 0.3 copy.183
  181.5 0.2 fusion.26
  182.1 0.5 multiply_reduce_fusion
  182.6 0.4 fusion.13
  183.1 10.8 %all_to_all.36 = bf16[4,16,2048]{2,1,0:T(8,128)(2,1)S(1)} all-to-all(bf16[4,16,2048]{2,1,0:T(8,128)(2,1)S(1)} %all_to_all.29), channel_id=1, replica_groups=mesh['seq'=128,'kvh'=4] {'kvh'}, dimensions={0} | all-to-all | bytes 524288 | tf_op jit(solution)/shard_map/all_to_all | solution.py:232
  193.9 0.7 copy.181
  (82 shorter events, 3.7 us)
Async XLA Ops:
  0.0 2.7 %copy-start = (bf16[64,16,128]{2,1,0:T(8,128)(2,1)S(1)}, bf16[64,16,128]{2,1,0:T(8,128)(2,1)}, u32[]{:S(2)}) copy-start(bf16[64,16,128]{2,1,0:T(8,128)(2,1)} %param.6) | copy-start | bytes 786436
  5.9 48.7 %all-to-all-start = ((bf16[128,2,16,128]{3,2,1,0:T(8,128)(2,1)}), bf16[128,2,16,128]{3,2,1,0:T(8,128)(2,1)S(1)}, u32[]{:S(2)}, u32[]{:S(2)}) async-start(bf16[128,2,16,128]{3,2,1,0:T(8,128)(2,1)} %bitcast.94), calls=%async_computation | async-start | bytes 2097152 | tf_op jit(solution)/shard_map/all_to_all | solution.py:126
  23.3 31.3 %copy-start.1 = (bf16[2,64,2,128]{3,2,1,0:T(2,128)(2,1)S(1)}, bf16[2,64,2,128]{3,2,1,0:T(2,128)(2,1)}, u32[]{:S(2)}) copy-start(bf16[2,64,2,128]{3,2,1,0:T(2,128)(2,1)} %param.7) | copy-start | bytes 196612
  54.6 11.0 %collective-permute-start = (bf16[1,2,64,2,128]{4,3,2,1,0:T(2,128)(2,1)S(1)}, bf16[1,2,64,2,128]{4,3,2,1,0:T(2,128)(2,1)S(1)}, u32[]{:S(2)}, u32[]{:S(2)}) collective-permute-start(bf16[1,2,64,2,128]{4,3,2,1,0:T(2,128)(2,1)S(1)} %bitcast.109), channel_id=1, source_target_pairs={{0,32},{4,36},{8,40},{12,44},{16,48},{20,52},{24,56},{28,60},{32,6... | collective-permute-start | bytes 196616 | tf_op jit(solution)/shard_map/ppermute | solution.py:19
  65.8 11.1 %collective-permute-start.1 = (bf16[2,2,64,2,128]{4,3,2,1,0:T(2,128)(2,1)S(1)}, bf16[2,2,64,2,128]{4,3,2,1,0:T(2,128)(2,1)S(1)}, u32[]{:S(2)}, u32[]{:S(2)}) collective-permute-start(bf16[2,2,64,2,128]{4,3,2,1,0:T(2,128)(2,1)S(1)} %pad_maximum_fusion.3), channel_id=1, source_target_pairs={{0,16},{4,20},{8,24},{12,28},{16,32},{20,36},{24,40},{28,44},{32,4... | collective-permute-start | bytes 393224 | tf_op jit(solution)/shard_map/ppermute | solution.py:19
  77.4 10.1 %collective-permute-start.2 = (bf16[4,2,64,2,128]{4,3,2,1,0:T(2,128)(2,1)S(1)}, bf16[4,2,64,2,128]{4,3,2,1,0:T(2,128)(2,1)S(1)}, u32[]{:S(2)}, u32[]{:S(2)}) collective-permute-start(bf16[4,2,64,2,128]{4,3,2,1,0:T(2,128)(2,1)S(1)} %pad_maximum_fusion.2), channel_id=1, source_target_pairs={{0,64},{4,68},{8,72},{12,76},{16,80},{20,84},{24,88},{28,92},{32,9... | collective-permute-start | bytes 786440 | tf_op jit(solution)/shard_map/ppermute | solution.py:19
  88.2 15.0 %collective-permute-start.3 = (bf16[8,2,64,2,128]{4,3,2,1,0:T(2,128)(2,1)S(1)}, bf16[8,2,64,2,128]{4,3,2,1,0:T(2,128)(2,1)S(1)}, u32[]{:S(2)}, u32[]{:S(2)}) collective-permute-start(bf16[8,2,64,2,128]{4,3,2,1,0:T(2,128)(2,1)S(1)} %pad_maximum_fusion.1), channel_id=1, source_target_pairs={{0,8},{4,12},{8,16},{12,20},{16,24},{20,28},{24,32},{28,36},{32,40... | collective-permute-start | bytes 1572872 | tf_op jit(solution)/shard_map/ppermute | solution.py:19
  105.2 18.4 %collective-permute-start.4 = (bf16[16,2,64,2,128]{4,3,2,1,0:T(2,128)(2,1)}, bf16[16,2,64,2,128]{4,3,2,1,0:T(2,128)(2,1)S(1)}, u32[]{:S(2)}, u32[]{:S(2)}) collective-permute-start(bf16[16,2,64,2,128]{4,3,2,1,0:T(2,128)(2,1)} %get-tuple-element.74), channel_id=1, source_target_pairs={{0,4},{4,8},{8,12},{12,16},{16,20},{20,24},{24,28},{28,32},{32,36}... | collective-permute-start | bytes 3145736 | tf_op jit(solution)/shard_map/ppermute | solution.py:19
  114.6 11.9 %copy-start.3 = (bf16[32,2,16,128]{3,2,1,0:T(8,128)(2,1)S(1)}, bf16[32,2,16,128]{3,2,1,0:T(8,128)(2,1)}, u32[]{:S(2)}) copy-start(bf16[32,2,16,128]{3,2,1,0:T(8,128)(2,1)} %get-tuple-element.36) | copy-start | bytes 786436
  114.6 11.9 %copy-start.4 = (bf16[32,2,16,128]{3,2,1,0:T(8,128)(2,1)S(1)}, bf16[32,2,16,128]{3,2,1,0:T(8,128)(2,1)}, u32[]{:S(2)}) copy-start(bf16[32,2,16,128]{3,2,1,0:T(8,128)(2,1)} %get-tuple-element.40) | copy-start | bytes 786436
  114.6 11.8 %copy-start.5 = (bf16[32,2,16,128]{3,2,1,0:T(8,128)(2,1)S(1)}, bf16[32,2,16,128]{3,2,1,0:T(8,128)(2,1)}, u32[]{:S(2)}) copy-start(bf16[32,2,16,128]{3,2,1,0:T(8,128)(2,1)} %get-tuple-element.44) | copy-start | bytes 786436
  114.6 11.8 %copy-start.6 = (bf16[32,2,16,128]{3,2,1,0:T(8,128)(2,1)S(1)}, bf16[32,2,16,128]{3,2,1,0:T(8,128)(2,1)}, u32[]{:S(2)}) copy-start(bf16[32,2,16,128]{3,2,1,0:T(8,128)(2,1)} %get-tuple-element.48) | copy-start | bytes 786436
  130.9 45.0 %all-to-all-start.1 = ((bf16[128,2,2112]{2,1,0:T(2,128)(2,1)}), bf16[128,2,2112]{2,1,0:T(2,128)(2,1)S(1)}, u32[]{:S(2)}, u32[]{:S(2)}) async-start(bf16[128,2,2112]{2,1,0:T(2,128)(2,1)} %reshape.368), calls=%async_computation.1 | async-start | bytes 2228224 | tf_op jit(solution)/shard_map/all_to_all | solution.py:173
  181.3 1.2 copy-start.2

commit v8 on v7

--- a/solution.py
+++ b/solution.py
@@ -9,7 +9,7 @@
 
 BLOCK_TOKENS = 2048
 BLOCK_PICK_LIMIT = 2
-WINDOW_SHIFTS = (8, 4, 16, 2, 1)
+WINDOW_SHIFTS = (16, 8, 4, 2, 1)
 LOG2_E = 1.4426950408889634
 
 

time: 196 us -> 198 us (1.010)
  transfers between devices with their start and end apart: 7 -> 7, of which waited for: 6 -> 7; matrix products, arithmetic and copies ran while one was open for 10% -> 10% of each run, Pallas kernels for 20% -> 19%
where the time goes in v8:
time: 198 us; the launch traced here: 197 us
  waiting for transfers between devices  59 us (30%)
  starting transfers between devices  44 us (22%)
  Pallas kernels  38 us (19%)
  local copies, waits for them, and re-layouts  35.1 us (18%)
  blocking collectives  10.8 us (5%)
  other arithmetic  7.98 us (4%)
    pallas_call x5, Pallas kernels, attend(): pl.pallas_call(functools.partial(attend_kernel, thr is not None, scaling,...  38 us
    all_to_all x1, waiting for transfers between devices, per_device(): lax.all_to_all(outgoing, 'seq', split_axis=0, concat_axis=0, tiled=True)  28.6 us
    all_to_all x1, starting transfers between devices, per_device(): lax.all_to_all(outgoing, 'seq', split_axis=0, concat_axis=0, tiled=True)  17.4 us
    all_to_all x1, waiting for transfers between devices, per_device(): lax.all_to_all(payload, 'seq', split_axis=0, concat_axis=0, tiled=True)  16.2 us
    ppermute x5, starting transfers between devices, shifted(): lax.ppermute(value, axis, [(source, source + steps) for source in range(i...  14.7 us
    ppermute x5, waiting for transfers between devices, shifted(): lax.ppermute(value, axis, [(source, source + steps) for source in range(i...  14.3 us
    all_to_all x1, starting transfers between devices, per_device(): lax.all_to_all(payload, 'seq', split_axis=0, concat_axis=0, tiled=True)  11.9 us
    all_to_all x1, blocking collectives, per_device(): lax.all_to_all(heads_out, 'kvh', split_axis=0, concat_axis=1, tiled=True)  10.8 us
  transfers between devices with their start and end apart: 7, of which 7 were waited for; matrix products, arithmetic and copies ran while one was open for 10% of the time, Pallas kernels for 19%

profile of v8, /device:TPU:8, one launch (start us, length us, event | category | flops | bytes accessed | tf_op | source)
XLA Modules:
  0.0 196.6 jit_solution(7471184953157864514)
XLA Ops:
  0.0 0.7 copy.141
  0.7 0.9 select_reduce_fusion
  1.8 0.1 reshape.202
  2.1 0.2 fusion.11
  2.5 0.2 fusion.15
  2.8 0.8 copy_bitcast_fusion.4
  3.6 0.6 fusion.1
  4.2 1.7 copy.199
  5.9 17.4 %all-to-all-start = ((bf16[128,2,16,128]{3,2,1,0:T(8,128)(2,1)}), bf16[128,2,16,128]{3,2,1,0:T(8,128)(2,1)S(1)}, u32[]{:S(2)}, u32[]{:S(2)}) async-start(bf16[128,2,16,128]{3,2,1,0:T(8,128)(2,1)} %bitcast.94), calls=%async_computation | async-start | bytes 2097152 | tf_op jit(solution)/shard_map/all_to_all | solution.py:126
  23.3 2.7 %fusion.27 = (bf16[1,1,2048,2,128]{4,3,2,1,0:T(2,128)(2,1)S(1)}, bf16[1,1,2048,2,128]{4,3,2,1,0:T(2,128)(2,1)S(1)}) fusion(bf16[2,1,2048,2,128]{4,3,2,1,0:T(2,128)(2,1)} %param.8), kind=kLoop, calls=%fused_computation.120 | loop fusion | bytes 4194304 | tf_op jit(solution)/shard_map/slice | solution.py:129
  26.0 28.6 %all-to-all-done = bf16[128,2,16,128]{3,2,1,0:T(8,128)(2,1)S(1)} async-done(((bf16[128,2,16,128]{3,2,1,0:T(8,128)(2,1)}), bf16[128,2,16,128]{3,2,1,0:T(8,128)(2,1)S(1)}, u32[]{:S(2)}, u32[]{:S(2)}) %all-to-all-start) | async-done | bytes 1048608 | tf_op jit(solution)/shard_map/all_to_all | solution.py:126
  54.6 1.9 collective-permute-start
  56.5 1.6 copy_bitcast_fusion.1
  58.1 2.7 %collective-permute-done = bf16[1,2,64,2,128]{4,3,2,1,0:T(2,128)(2,1)S(1)} collective-permute-done((bf16[1,2,64,2,128]{4,3,2,1,0:T(2,128)(2,1)S(1)}, bf16[1,2,64,2,128]{4,3,2,1,0:T(2,128)(2,1)S(1)}, u32[]{:S(2)}, u32[]{:S(2)}) %collective-permute-start) | collective-permute-done | bytes 65568 | tf_op jit(solution)/shard_map/ppermute | solution.py:19
  60.8 0.2 pad_maximum_fusion.3
  61.0 3.3 %collective-permute-start.1 = (bf16[2,2,64,2,128]{4,3,2,1,0:T(2,128)(2,1)S(1)}, bf16[2,2,64,2,128]{4,3,2,1,0:T(2,128)(2,1)S(1)}, u32[]{:S(2)}, u32[]{:S(2)}) collective-permute-start(bf16[2,2,64,2,128]{4,3,2,1,0:T(2,128)(2,1)S(1)} %pad_maximum_fusion.3), channel_id=1, source_target_pairs={{0,32},{4,36},{8,40},{12,44},{16,48},{20,52},{24,56},{28,60},{32,6... | collective-permute-start | bytes 393224 | tf_op jit(solution)/shard_map/ppermute | solution.py:19
  64.3 1.1 fusion.28
  65.4 7.5 %shard_map.64 = (bf16[32,2,16,128]{3,2,1,0:T(8,128)(2,1)}, f32[2,1,8,512]{3,2,1,0:T(8,128)}) custom-call(bf16[32,2,16,128]{3,2,1,0:T(8,128)(2,1)} %get-tuple-element.72.refs_0_, bf16[2,2048,128]{2,1,0:T(8,128)(2,1)} %get-tuple-element.88.refs_1_, bf16[2,2048,128]{2,1,0:T(8,128)(2,1)} %get-tuple-element.87.refs_2_), custom_call_target="tpu_custom_call" | custom-call | flops 1073741824 | bytes 2621440 | tf_op jit(solution)/shard_map/pallas_call | solution.py:78
  72.8 1.1 collective-permute-done.1
  73.9 0.4 pad_maximum_fusion.2
  74.3 2.3 %collective-permute-start.2 = (bf16[4,2,64,2,128]{4,3,2,1,0:T(2,128)(2,1)S(1)}, bf16[4,2,64,2,128]{4,3,2,1,0:T(2,128)(2,1)S(1)}, u32[]{:S(2)}, u32[]{:S(2)}) collective-permute-start(bf16[4,2,64,2,128]{4,3,2,1,0:T(2,128)(2,1)S(1)} %pad_maximum_fusion.2), channel_id=1, source_target_pairs={{0,16},{4,20},{8,24},{12,28},{16,32},{20,36},{24,40},{28,44},{32,4... | collective-permute-start | bytes 786440 | tf_op jit(solution)/shard_map/ppermute | solution.py:19
  76.6 7.5 %shard_map.65 = (bf16[32,2,16,128]{3,2,1,0:T(8,128)(2,1)}, f32[2,1,8,512]{3,2,1,0:T(8,128)}) custom-call(bf16[32,2,16,128]{3,2,1,0:T(8,128)(2,1)} %get-tuple-element.71.refs_0_, bf16[2,2048,128]{2,1,0:T(8,128)(2,1)} %get-tuple-element.88.refs_1_, bf16[2,2048,128]{2,1,0:T(8,128)(2,1)} %get-tuple-element.87.refs_2_), custom_call_target="tpu_custom_call" | custom-call | flops 1073741824 | bytes 2621440 | tf_op jit(solution)/shard_map/pallas_call | solution.py:78
  84.1 4.3 %collective-permute-done.2 = bf16[4,2,64,2,128]{4,3,2,1,0:T(2,128)(2,1)S(1)} collective-permute-done((bf16[4,2,64,2,128]{4,3,2,1,0:T(2,128)(2,1)S(1)}, bf16[4,2,64,2,128]{4,3,2,1,0:T(2,128)(2,1)S(1)}, u32[]{:S(2)}, u32[]{:S(2)}) %collective-permute-start.2) | collective-permute-done | bytes 262176 | tf_op jit(solution)/shard_map/ppermute | solution.py:19
  88.4 0.7 pad_maximum_fusion.1
  89.2 5.3 %collective-permute-start.3 = (bf16[8,2,64,2,128]{4,3,2,1,0:T(2,128)(2,1)S(1)}, bf16[8,2,64,2,128]{4,3,2,1,0:T(2,128)(2,1)S(1)}, u32[]{:S(2)}, u32[]{:S(2)}) collective-permute-start(bf16[8,2,64,2,128]{4,3,2,1,0:T(2,128)(2,1)S(1)} %pad_maximum_fusion.1), channel_id=1, source_target_pairs={{0,8},{4,12},{8,16},{12,20},{16,24},{20,28},{24,32},{28,36},{32,40... | collective-permute-start | bytes 1572872 | tf_op jit(solution)/shard_map/ppermute | solution.py:19
  94.5 0.7 constant_dynamic-update-slice_fusion.10
  95.2 7.5 %shard_map.66 = (bf16[32,2,16,128]{3,2,1,0:T(8,128)(2,1)}, f32[2,1,8,512]{3,2,1,0:T(8,128)}) custom-call(bf16[32,2,16,128]{3,2,1,0:T(8,128)(2,1)} %get-tuple-element.70.refs_0_, bf16[2,2048,128]{2,1,0:T(8,128)(2,1)} %get-tuple-element.88.refs_1_, bf16[2,2048,128]{2,1,0:T(8,128)(2,1)} %get-tuple-element.87.refs_2_), custom_call_target="tpu_custom_call" | custom-call | flops 1073741824 | bytes 2621440 | tf_op jit(solution)/shard_map/pallas_call | solution.py:78
  102.7 0.7 constant_dynamic-update-slice_fusion.9
  103.4 0.8 constant_dynamic-update-slice_fusion.8
  104.2 1.2 constant_dynamic-update-slice_fusion.7
  105.6 2.0 constant_dynamic-update-slice_fusion.6
  107.5 1.9 collective-permute-start.4
  109.4 7.5 %shard_map.67 = (bf16[32,2,16,128]{3,2,1,0:T(8,128)(2,1)}, f32[2,1,8,512]{3,2,1,0:T(8,128)}) custom-call(bf16[32,2,16,128]{3,2,1,0:T(8,128)(2,1)} %get-tuple-element.69.refs_0_, bf16[2,2048,128]{2,1,0:T(8,128)(2,1)} %get-tuple-element.88.refs_1_, bf16[2,2048,128]{2,1,0:T(8,128)(2,1)} %get-tuple-element.87.refs_2_), custom_call_target="tpu_custom_call" | custom-call | flops 1073741824 | bytes 2621440 | tf_op jit(solution)/shard_map/pallas_call | solution.py:78
  117.0 0.9 slice_reduce_fusion.4
  118.0 0.8 slice_reduce_fusion.3
  118.9 0.8 slice_reduce_fusion.2
  119.9 6.1 %collective-permute-done.4 = bf16[16,2,64,2,128]{4,3,2,1,0:T(2,128)(2,1)S(1)} collective-permute-done((bf16[16,2,64,2,128]{4,3,2,1,0:T(2,128)(2,1)}, bf16[16,2,64,2,128]{4,3,2,1,0:T(2,128)(2,1)S(1)}, u32[]{:S(2)}, u32[]{:S(2)}) %collective-permute-start.4) | collective-permute-done | bytes 1048608 | tf_op jit(solution)/shard_map/ppermute | solution.py:19
  126.0 0.8 slice_reduce_fusion.1
  126.9 1.9 constant_dynamic-update-slice_fusion.5
  129.0 0.5 copy.198
  129.7 0.5 broadcast.486
  130.2 1.4 reduce.60
  131.6 1.6 reshape.368
  133.2 11.9 %all-to-all-start.1 = ((bf16[128,2,2112]{2,1,0:T(2,128)(2,1)}), bf16[128,2,2112]{2,1,0:T(2,128)(2,1)S(1)}, u32[]{:S(2)}, u32[]{:S(2)}) async-start(bf16[128,2,2112]{2,1,0:T(2,128)(2,1)} %reshape.368), calls=%async_computation.1 | async-start | bytes 2228224 | tf_op jit(solution)/shard_map/all_to_all | solution.py:173
  146.3 0.3 compare_reduce_fusion
  146.6 0.6 reshape_select_fusion.1.refs_0_
  147.2 2.9 %slice_bitcast_fusion = (bf16[2,32,64,128]{3,0,2,1:T(2,128)(2,1)S(1)}, bf16[2,32,64,128]{3,0,2,1:T(2,128)(2,1)S(1)}) fusion(bf16[32,2,64,2,128]{4,3,2,1,0:T(2,128)(2,1)} %constant_dynamic-update-slice_fusion.5), kind=kLoop, calls=%fused_computation.13 | loop fusion | bytes 4194304 | tf_op jit(solution)/shard_map/transpose | solution.py:180
  150.2 1.3 copy.154
  151.5 1.3 copy.153
  152.7 8.0 %shard_map.68 = (f32[2,512,128]{2,1,0:T(8,128)}, f32[2,1,8,512]{3,2,1,0:T(8,128)}) custom-call(s32[1,2048]{1,0:T(1,128)} %reshape_select_fusion.1.refs_0_, bf16[2,512,128]{2,1,0:T(8,128)(2,1)} %get-tuple-element.75.refs_1_, bf16[2,2048,128]{2,1,0:T(8,128)(2,1)} %bitcast.106, bf16[2,2048,128]{2,1,0:T(8,128)(2,1)} %bitcast.105), custom_call_target="tpu_custom_call" | custom-call | flops 1073741824 | bytes 2621440 | tf_op jit(solution)/shard_map/pallas_call | solution.py:78
  160.7 0.8 slice_reduce_fusion
  161.7 16.2 %all-to-all-done.1 = bf16[128,2,2112]{2,1,0:T(2,128)(2,1)S(1)} async-done(((bf16[128,2,2112]{2,1,0:T(2,128)(2,1)}), bf16[128,2,2112]{2,1,0:T(2,128)(2,1)S(1)}, u32[]{:S(2)}, u32[]{:S(2)}) %all-to-all-start.1) | async-done | bytes 1081376 | tf_op jit(solution)/shard_map/all_to_all | solution.py:173
  177.8 1.2 reshape.369
  179.0 2.7 %copy.157 = bf16[128,1,4224]{0,2,1:T(8,128)(2,1)S(1)} copy(bf16[128,1,4224]{2,1,0:T(2,128)(2,1)S(1)} %reshape.369) | data formatting | bytes 2162688 | tf_op jit(solution)/shard_map/all_to_all | solution.py:173
  181.9 0.2 convolution_bitcast_fusion
  182.1 0.2 copy.159
  182.3 0.1 reduce_max.9
  182.5 0.5 fusion.5
  183.0 0.3 copy.183
  183.5 0.2 fusion.26
  184.1 0.5 multiply_reduce_fusion
  184.6 0.4 fusion.13
  185.1 10.8 %all_to_all.36 = bf16[4,16,2048]{2,1,0:T(8,128)(2,1)S(1)} all-to-all(bf16[4,16,2048]{2,1,0:T(8,128)(2,1)S(1)} %all_to_all.29), channel_id=1, replica_groups=mesh['seq'=128,'kvh'=4] {'kvh'}, dimensions={0} | all-to-all | bytes 524288 | tf_op jit(solution)/shard_map/all_to_all | solution.py:232
  195.9 0.7 copy.181
  (82 shorter events, 3.8 us)
Async XLA Ops:
  0.0 2.7 %copy-start = (bf16[64,16,128]{2,1,0:T(8,128)(2,1)S(1)}, bf16[64,16,128]{2,1,0:T(8,128)(2,1)}, u32[]{:S(2)}) copy-start(bf16[64,16,128]{2,1,0:T(8,128)(2,1)} %param.6) | copy-start | bytes 786436
  5.9 48.7 %all-to-all-start = ((bf16[128,2,16,128]{3,2,1,0:T(8,128)(2,1)}), bf16[128,2,16,128]{3,2,1,0:T(8,128)(2,1)S(1)}, u32[]{:S(2)}, u32[]{:S(2)}) async-start(bf16[128,2,16,128]{3,2,1,0:T(8,128)(2,1)} %bitcast.94), calls=%async_computation | async-start | bytes 2097152 | tf_op jit(solution)/shard_map/all_to_all | solution.py:126
  23.3 31.3 %copy-start.1 = (bf16[2,64,2,128]{3,2,1,0:T(2,128)(2,1)S(1)}, bf16[2,64,2,128]{3,2,1,0:T(2,128)(2,1)}, u32[]{:S(2)}) copy-start(bf16[2,64,2,128]{3,2,1,0:T(2,128)(2,1)} %param.7) | copy-start | bytes 196612
  54.6 6.1 %collective-permute-start = (bf16[1,2,64,2,128]{4,3,2,1,0:T(2,128)(2,1)S(1)}, bf16[1,2,64,2,128]{4,3,2,1,0:T(2,128)(2,1)S(1)}, u32[]{:S(2)}, u32[]{:S(2)}) collective-permute-start(bf16[1,2,64,2,128]{4,3,2,1,0:T(2,128)(2,1)S(1)} %bitcast.109), channel_id=1, source_target_pairs={{0,64},{4,68},{8,72},{12,76},{16,80},{20,84},{24,88},{28,92},{32,9... | collective-permute-start | bytes 196616 | tf_op jit(solution)/shard_map/ppermute | solution.py:19
  61.0 12.9 %collective-permute-start.1 = (bf16[2,2,64,2,128]{4,3,2,1,0:T(2,128)(2,1)S(1)}, bf16[2,2,64,2,128]{4,3,2,1,0:T(2,128)(2,1)S(1)}, u32[]{:S(2)}, u32[]{:S(2)}) collective-permute-start(bf16[2,2,64,2,128]{4,3,2,1,0:T(2,128)(2,1)S(1)} %pad_maximum_fusion.3), channel_id=1, source_target_pairs={{0,32},{4,36},{8,40},{12,44},{16,48},{20,52},{24,56},{28,60},{32,6... | collective-permute-start | bytes 393224 | tf_op jit(solution)/shard_map/ppermute | solution.py:19
  74.3 14.1 %collective-permute-start.2 = (bf16[4,2,64,2,128]{4,3,2,1,0:T(2,128)(2,1)S(1)}, bf16[4,2,64,2,128]{4,3,2,1,0:T(2,128)(2,1)S(1)}, u32[]{:S(2)}, u32[]{:S(2)}) collective-permute-start(bf16[4,2,64,2,128]{4,3,2,1,0:T(2,128)(2,1)S(1)} %pad_maximum_fusion.2), channel_id=1, source_target_pairs={{0,16},{4,20},{8,24},{12,28},{16,32},{20,36},{24,40},{28,44},{32,4... | collective-permute-start | bytes 786440 | tf_op jit(solution)/shard_map/ppermute | solution.py:19
  89.2 16.4 %collective-permute-start.3 = (bf16[8,2,64,2,128]{4,3,2,1,0:T(2,128)(2,1)S(1)}, bf16[8,2,64,2,128]{4,3,2,1,0:T(2,128)(2,1)S(1)}, u32[]{:S(2)}, u32[]{:S(2)}) collective-permute-start(bf16[8,2,64,2,128]{4,3,2,1,0:T(2,128)(2,1)S(1)} %pad_maximum_fusion.1), channel_id=1, source_target_pairs={{0,8},{4,12},{8,16},{12,20},{16,24},{20,28},{24,32},{28,36},{32,40... | collective-permute-start | bytes 1572872 | tf_op jit(solution)/shard_map/ppermute | solution.py:19
  107.5 18.4 %collective-permute-start.4 = (bf16[16,2,64,2,128]{4,3,2,1,0:T(2,128)(2,1)}, bf16[16,2,64,2,128]{4,3,2,1,0:T(2,128)(2,1)S(1)}, u32[]{:S(2)}, u32[]{:S(2)}) collective-permute-start(bf16[16,2,64,2,128]{4,3,2,1,0:T(2,128)(2,1)} %get-tuple-element.74), channel_id=1, source_target_pairs={{0,4},{4,8},{8,12},{12,16},{16,20},{20,24},{24,28},{28,32},{32,36}... | collective-permute-start | bytes 3145736 | tf_op jit(solution)/shard_map/ppermute | solution.py:19
  116.9 11.9 %copy-start.3 = (bf16[32,2,16,128]{3,2,1,0:T(8,128)(2,1)S(1)}, bf16[32,2,16,128]{3,2,1,0:T(8,128)(2,1)}, u32[]{:S(2)}) copy-start(bf16[32,2,16,128]{3,2,1,0:T(8,128)(2,1)} %get-tuple-element.36) | copy-start | bytes 786436
  116.9 11.9 %copy-start.4 = (bf16[32,2,16,128]{3,2,1,0:T(8,128)(2,1)S(1)}, bf16[32,2,16,128]{3,2,1,0:T(8,128)(2,1)}, u32[]{:S(2)}) copy-start(bf16[32,2,16,128]{3,2,1,0:T(8,128)(2,1)} %get-tuple-element.40) | copy-start | bytes 786436
  117.0 11.9 %copy-start.5 = (bf16[32,2,16,128]{3,2,1,0:T(8,128)(2,1)S(1)}, bf16[32,2,16,128]{3,2,1,0:T(8,128)(2,1)}, u32[]{:S(2)}) copy-start(bf16[32,2,16,128]{3,2,1,0:T(8,128)(2,1)} %get-tuple-element.44) | copy-start | bytes 786436
  117.0 11.8 %copy-start.6 = (bf16[32,2,16,128]{3,2,1,0:T(8,128)(2,1)S(1)}, bf16[32,2,16,128]{3,2,1,0:T(8,128)(2,1)}, u32[]{:S(2)}) copy-start(bf16[32,2,16,128]{3,2,1,0:T(8,128)(2,1)} %get-tuple-element.48) | copy-start | bytes 786436
  133.2 44.6 %all-to-all-start.1 = ((bf16[128,2,2112]{2,1,0:T(2,128)(2,1)}), bf16[128,2,2112]{2,1,0:T(2,128)(2,1)S(1)}, u32[]{:S(2)}, u32[]{:S(2)}) async-start(bf16[128,2,2112]{2,1,0:T(2,128)(2,1)} %reshape.368), calls=%async_computation.1 | async-start | bytes 2228224 | tf_op jit(solution)/shard_map/all_to_all | solution.py:173
  183.4 1.2 copy-start.2

commit v9 on v7

--- a/solution.py
+++ b/solution.py
@@ -151,9 +151,8 @@
     )
     blocks = window.shape[0]
     served = jnp.concatenate([piece[0] for piece in served_pieces], axis=0)
-    served_lse = jnp.concatenate(
-        [piece[1][:, :, 0].reshape(kv_heads, sources_per_tile, slab) for piece in served_pieces], axis=1
-    )
+    served_lse = jnp.concatenate([piece[1] for piece in served_pieces], axis=1)[:, :, 0]
+    served_lse = served_lse.reshape(kv_heads, seq_count, slab)
     served_lse = jnp.swapaxes(served_lse, 0, 1)
     served, served_lse, window = lax.optimization_barrier((served, served_lse, window))
     lse_rounded = lax.reduce_precision(served_lse, exponent_bits=8, mantissa_bits=7)

time: 196 us -> 196 us (level)
  local copies, waits for them, and re-layouts: 35.1 us -> 31.5 us
  waiting for transfers between devices: 57.7 us -> 60.6 us
    slice x4 -> x0, local copies, waits for them, and re-layouts: 3.21 us -> none  [per_device(): piece[1][:, :, 0].reshape(kv_heads, sources_per_tile, slab)]
    ppermute x5, waiting for transfers between devices: 12.9 us -> 15.8 us  [shifted(): lax.ppermute(value, axis, [(source, source + steps) for source in range(i...]
    unnamed x25 -> x31, local copies, waits for them, and re-layouts: 9.89 us -> 9.93 us
  transfers between devices with their start and end apart: 7 -> 7, of which waited for: 6 -> 6; matrix products, arithmetic and copies ran while one was open for 10% -> 9% of each run, Pallas kernels for 20% -> 19%
where the time goes in v9:
time: 196 us; the launch traced here: 195 us
  waiting for transfers between devices  60.6 us (31%)
  starting transfers between devices  43.5 us (22%)
  Pallas kernels  38 us (19%)
  local copies, waits for them, and re-layouts  31.5 us (16%)
  blocking collectives  10.8 us (6%)
  other arithmetic  8.73 us (4%)
    pallas_call x5, Pallas kernels, attend(): pl.pallas_call(functools.partial(attend_kernel, thr is not None, scaling,...  38 us
    all_to_all x1, waiting for transfers between devices, per_device(): lax.all_to_all(outgoing, 'seq', split_axis=0, concat_axis=0, tiled=True)  28.6 us
    all_to_all x1, starting transfers between devices, per_device(): lax.all_to_all(outgoing, 'seq', split_axis=0, concat_axis=0, tiled=True)  17.4 us
    all_to_all x1, waiting for transfers between devices, per_device(): lax.all_to_all(payload, 'seq', split_axis=0, concat_axis=0, tiled=True)  16.2 us
    ppermute x5, waiting for transfers between devices, shifted(): lax.ppermute(value, axis, [(source, source + steps) for source in range(i...  15.8 us
    ppermute x5, starting transfers between devices, shifted(): lax.ppermute(value, axis, [(source, source + steps) for source in range(i...  13.9 us
    all_to_all x1, starting transfers between devices, per_device(): lax.all_to_all(payload, 'seq', split_axis=0, concat_axis=0, tiled=True)  12.2 us
    all_to_all x1, blocking collectives, per_device(): lax.all_to_all(heads_out, 'kvh', split_axis=0, concat_axis=1, tiled=True)  10.8 us
  transfers between devices with their start and end apart: 7, of which 6 were waited for; matrix products, arithmetic and copies ran while one was open for 9% of the time, Pallas kernels for 19%

profile of v9, /device:TPU:8, one launch (start us, length us, event | category | flops | bytes accessed | tf_op | source)
XLA Modules:
  0.0 194.9 jit_solution(7467772908315791591)
XLA Ops:
  0.0 0.7 copy.135
  0.7 0.9 select_reduce_fusion
  1.8 0.1 reshape.202
  1.9 0.1 iota_compare_fusion.1
  2.1 0.2 fusion.11
  2.5 0.2 fusion.15
  2.8 0.8 copy_bitcast_fusion.4
  3.6 0.6 fusion.1
  4.2 1.7 copy.191
  5.9 17.4 %all-to-all-start = ((bf16[128,2,16,128]{3,2,1,0:T(8,128)(2,1)}), bf16[128,2,16,128]{3,2,1,0:T(8,128)(2,1)S(1)}, u32[]{:S(2)}, u32[]{:S(2)}) async-start(bf16[128,2,16,128]{3,2,1,0:T(8,128)(2,1)} %bitcast.93), calls=%async_computation | async-start | bytes 2097152 | tf_op jit(solution)/shard_map/all_to_all | solution.py:126
  23.3 2.7 %fusion.27 = (bf16[1,1,2048,2,128]{4,3,2,1,0:T(2,128)(2,1)S(1)}, bf16[1,1,2048,2,128]{4,3,2,1,0:T(2,128)(2,1)S(1)}) fusion(bf16[2,1,2048,2,128]{4,3,2,1,0:T(2,128)(2,1)} %param.8), kind=kLoop, calls=%fused_computation.118 | loop fusion | bytes 4194304 | tf_op jit(solution)/shard_map/slice | solution.py:129
  26.0 28.6 %all-to-all-done = bf16[128,2,16,128]{3,2,1,0:T(8,128)(2,1)S(1)} async-done(((bf16[128,2,16,128]{3,2,1,0:T(8,128)(2,1)}), bf16[128,2,16,128]{3,2,1,0:T(8,128)(2,1)S(1)}, u32[]{:S(2)}, u32[]{:S(2)}) %all-to-all-start) | async-done | bytes 1048608 | tf_op jit(solution)/shard_map/all_to_all | solution.py:126
  54.6 3.3 %collective-permute-start = (bf16[1,2,64,2,128]{4,3,2,1,0:T(2,128)(2,1)S(1)}, bf16[1,2,64,2,128]{4,3,2,1,0:T(2,128)(2,1)S(1)}, u32[]{:S(2)}, u32[]{:S(2)}) collective-permute-start(bf16[1,2,64,2,128]{4,3,2,1,0:T(2,128)(2,1)S(1)} %bitcast.110), channel_id=1, source_target_pairs={{0,32},{4,36},{8,40},{12,44},{16,48},{20,52},{24,56},{28,60},{32,6... | collective-permute-start | bytes 196616 | tf_op jit(solution)/shard_map/ppermute | solution.py:19
  57.9 1.6 copy_bitcast_fusion.1
  59.5 6.1 %collective-permute-done = bf16[1,2,64,2,128]{4,3,2,1,0:T(2,128)(2,1)S(1)} collective-permute-done((bf16[1,2,64,2,128]{4,3,2,1,0:T(2,128)(2,1)S(1)}, bf16[1,2,64,2,128]{4,3,2,1,0:T(2,128)(2,1)S(1)}, u32[]{:S(2)}, u32[]{:S(2)}) %collective-permute-start) | collective-permute-done | bytes 65568 | tf_op jit(solution)/shard_map/ppermute | solution.py:19
  65.7 0.2 pad_maximum_fusion.3
  65.8 2.4 %collective-permute-start.1 = (bf16[2,2,64,2,128]{4,3,2,1,0:T(2,128)(2,1)S(1)}, bf16[2,2,64,2,128]{4,3,2,1,0:T(2,128)(2,1)S(1)}, u32[]{:S(2)}, u32[]{:S(2)}) collective-permute-start(bf16[2,2,64,2,128]{4,3,2,1,0:T(2,128)(2,1)S(1)} %pad_maximum_fusion.3), channel_id=1, source_target_pairs={{0,16},{4,20},{8,24},{12,28},{16,32},{20,36},{24,40},{28,44},{32,4... | collective-permute-start | bytes 393224 | tf_op jit(solution)/shard_map/ppermute | solution.py:19
  68.2 1.1 fusion.28
  69.3 7.5 %shard_map.64 = (bf16[32,2,16,128]{3,2,1,0:T(8,128)(2,1)}, f32[2,1,8,512]{3,2,1,0:T(8,128)}) custom-call(bf16[32,2,16,128]{3,2,1,0:T(8,128)(2,1)} %get-tuple-element.72.refs_0_, bf16[2,2048,128]{2,1,0:T(8,128)(2,1)} %get-tuple-element.86.refs_1_, bf16[2,2048,128]{2,1,0:T(8,128)(2,1)} %get-tuple-element.85.refs_2_), custom_call_target="tpu_custom_call" | custom-call | flops 1073741824 | bytes 2621440 | tf_op jit(solution)/shard_map/pallas_call | solution.py:78
  76.7 0.2 collective-permute-done.1
  77.0 0.4 pad_maximum_fusion.2
  77.4 2.5 %collective-permute-start.2 = (bf16[4,2,64,2,128]{4,3,2,1,0:T(2,128)(2,1)S(1)}, bf16[4,2,64,2,128]{4,3,2,1,0:T(2,128)(2,1)S(1)}, u32[]{:S(2)}, u32[]{:S(2)}) collective-permute-start(bf16[4,2,64,2,128]{4,3,2,1,0:T(2,128)(2,1)S(1)} %pad_maximum_fusion.2), channel_id=1, source_target_pairs={{0,64},{4,68},{8,72},{12,76},{16,80},{20,84},{24,88},{28,92},{32,9... | collective-permute-start | bytes 786440 | tf_op jit(solution)/shard_map/ppermute | solution.py:19
  79.9 7.5 %shard_map.65 = (bf16[32,2,16,128]{3,2,1,0:T(8,128)(2,1)}, f32[2,1,8,512]{3,2,1,0:T(8,128)}) custom-call(bf16[32,2,16,128]{3,2,1,0:T(8,128)(2,1)} %get-tuple-element.71.refs_0_, bf16[2,2048,128]{2,1,0:T(8,128)(2,1)} %get-tuple-element.86.refs_1_, bf16[2,2048,128]{2,1,0:T(8,128)(2,1)} %get-tuple-element.85.refs_2_), custom_call_target="tpu_custom_call" | custom-call | flops 1073741824 | bytes 2621440 | tf_op jit(solution)/shard_map/pallas_call | solution.py:78
  87.4 0.7 pad_maximum_fusion.1
  88.2 3.6 %collective-permute-start.3 = (bf16[8,2,64,2,128]{4,3,2,1,0:T(2,128)(2,1)S(1)}, bf16[8,2,64,2,128]{4,3,2,1,0:T(2,128)(2,1)S(1)}, u32[]{:S(2)}, u32[]{:S(2)}) collective-permute-start(bf16[8,2,64,2,128]{4,3,2,1,0:T(2,128)(2,1)S(1)} %pad_maximum_fusion.1), channel_id=1, source_target_pairs={{0,8},{4,12},{8,16},{12,20},{16,24},{20,28},{24,32},{28,36},{32,40... | collective-permute-start | bytes 1572872 | tf_op jit(solution)/shard_map/ppermute | solution.py:19
  91.8 0.7 constant_dynamic-update-slice_fusion.10
  92.5 7.5 %shard_map.66 = (bf16[32,2,16,128]{3,2,1,0:T(8,128)(2,1)}, f32[2,1,8,512]{3,2,1,0:T(8,128)}) custom-call(bf16[32,2,16,128]{3,2,1,0:T(8,128)(2,1)} %get-tuple-element.70.refs_0_, bf16[2,2048,128]{2,1,0:T(8,128)(2,1)} %get-tuple-element.86.refs_1_, bf16[2,2048,128]{2,1,0:T(8,128)(2,1)} %get-tuple-element.85.refs_2_), custom_call_target="tpu_custom_call" | custom-call | flops 1073741824 | bytes 2621440 | tf_op jit(solution)/shard_map/pallas_call | solution.py:78
  100.0 0.7 constant_dynamic-update-slice_fusion.9
  100.7 0.8 constant_dynamic-update-slice_fusion.8
  101.5 1.2 constant_dynamic-update-slice_fusion.7
  102.7 0.5 collective-permute-done.3
  103.2 2.0 %constant_dynamic-update-slice_fusion.6 = (bf16[32,2,64,2,128]{4,3,2,1,0:T(2,128)(2,1)}, bf16[16,2,64,2,128]{4,3,2,1,0:T(2,128)(2,1)}) fusion(bf16[32,2,64,2,128]{4,3,2,1,0:T(2,128)(2,1)} %get-tuple-element.77, bf16[8,2,64,2,128]{4,3,2,1,0:T(2,128)(2,1)S(1)} %collective-permute-done.3, bf16[16,2,64,2,128]{4,3,2,1,0:T(2,128)(2,1)} %get-tuple-element.78), kind=kLoop, calls=%fused_computation.92 | loop fusion | bytes 1572864
  105.2 2.0 %collective-permute-start.4 = (bf16[16,2,64,2,128]{4,3,2,1,0:T(2,128)(2,1)}, bf16[16,2,64,2,128]{4,3,2,1,0:T(2,128)(2,1)S(1)}, u32[]{:S(2)}, u32[]{:S(2)}) collective-permute-start(bf16[16,2,64,2,128]{4,3,2,1,0:T(2,128)(2,1)} %get-tuple-element.74), channel_id=1, source_target_pairs={{0,4},{4,8},{8,12},{12,16},{16,20},{20,24},{24,28},{28,32},{32,36}... | collective-permute-start | bytes 3145736 | tf_op jit(solution)/shard_map/ppermute | solution.py:19
  107.2 7.5 %shard_map.67 = (bf16[32,2,16,128]{3,2,1,0:T(8,128)(2,1)}, f32[2,1,8,512]{3,2,1,0:T(8,128)}) custom-call(bf16[32,2,16,128]{3,2,1,0:T(8,128)(2,1)} %get-tuple-element.69.refs_0_, bf16[2,2048,128]{2,1,0:T(8,128)(2,1)} %get-tuple-element.86.refs_1_, bf16[2,2048,128]{2,1,0:T(8,128)(2,1)} %get-tuple-element.85.refs_2_), custom_call_target="tpu_custom_call" | custom-call | flops 1073741824 | bytes 2621440 | tf_op jit(solution)/shard_map/pallas_call | solution.py:78
  114.8 9.0 %collective-permute-done.4 = bf16[16,2,64,2,128]{4,3,2,1,0:T(2,128)(2,1)S(1)} collective-permute-done((bf16[16,2,64,2,128]{4,3,2,1,0:T(2,128)(2,1)}, bf16[16,2,64,2,128]{4,3,2,1,0:T(2,128)(2,1)S(1)}, u32[]{:S(2)}, u32[]{:S(2)}) %collective-permute-start.4) | collective-permute-done | bytes 1048608 | tf_op jit(solution)/shard_map/ppermute | solution.py:19
  123.7 0.8 fusion.22
  124.7 1.9 constant_dynamic-update-slice_fusion.5
  126.6 0.1 pad_maximum_fusion
  126.8 0.5 copy.190
  127.4 0.1 copy.172
  127.6 0.5 broadcast.483
  128.1 1.4 reduce.54
  129.5 1.6 reshape.365
  131.1 12.2 %all-to-all-start.1 = ((bf16[128,2,2112]{2,1,0:T(2,128)(2,1)}), bf16[128,2,2112]{2,1,0:T(2,128)(2,1)S(1)}, u32[]{:S(2)}, u32[]{:S(2)}) async-start(bf16[128,2,2112]{2,1,0:T(2,128)(2,1)} %reshape.365), calls=%async_computation.1 | async-start | bytes 2228224 | tf_op jit(solution)/shard_map/all_to_all | solution.py:172
  144.5 0.3 compare_reduce_fusion
  144.8 0.6 reshape_select_fusion.1.refs_0_
  145.5 2.9 %slice_bitcast_fusion = (bf16[2,32,64,128]{3,0,2,1:T(2,128)(2,1)S(1)}, bf16[2,32,64,128]{3,0,2,1:T(2,128)(2,1)S(1)}) fusion(bf16[32,2,64,2,128]{4,3,2,1,0:T(2,128)(2,1)} %constant_dynamic-update-slice_fusion.5), kind=kLoop, calls=%fused_computation.13 | loop fusion | bytes 4194304 | tf_op jit(solution)/shard_map/transpose | solution.py:179
  148.4 1.3 copy.144
  149.7 1.3 copy.143
  151.0 8.0 %shard_map.68 = (f32[2,512,128]{2,1,0:T(8,128)}, f32[2,1,8,512]{3,2,1,0:T(8,128)}) custom-call(s32[1,2048]{1,0:T(1,128)} %reshape_select_fusion.1.refs_0_, bf16[2,512,128]{2,1,0:T(8,128)(2,1)} %get-tuple-element.75.refs_1_, bf16[2,2048,128]{2,1,0:T(8,128)(2,1)} %bitcast.107, bf16[2,2048,128]{2,1,0:T(8,128)(2,1)} %bitcast.106), custom_call_target="tpu_custom_call" | custom-call | flops 1073741824 | bytes 2621440 | tf_op jit(solution)/shard_map/pallas_call | solution.py:78
  159.0 0.8 slice_reduce_fusion
  159.9 16.2 %all-to-all-done.1 = bf16[128,2,2112]{2,1,0:T(2,128)(2,1)S(1)} async-done(((bf16[128,2,2112]{2,1,0:T(2,128)(2,1)}), bf16[128,2,2112]{2,1,0:T(2,128)(2,1)S(1)}, u32[]{:S(2)}, u32[]{:S(2)}) %all-to-all-start.1) | async-done | bytes 1081376 | tf_op jit(solution)/shard_map/all_to_all | solution.py:172
  176.1 1.2 reshape.366
  177.3 2.7 %copy.149 = bf16[128,1,4224]{0,2,1:T(8,128)(2,1)S(1)} copy(bf16[128,1,4224]{2,1,0:T(2,128)(2,1)S(1)} %reshape.366) | data formatting | bytes 2162688 | tf_op jit(solution)/shard_map/all_to_all | solution.py:172
  180.1 0.2 convolution_bitcast_fusion
  180.3 0.2 copy.151
  180.5 0.1 reduce_max.9
  180.7 0.5 fusion.5
  181.2 0.3 copy.175
  181.7 0.2 fusion.26
  182.3 0.5 multiply_reduce_fusion
  182.8 0.4 fusion.13
  183.4 10.8 %all_to_all.36 = bf16[4,16,2048]{2,1,0:T(8,128)(2,1)S(1)} all-to-all(bf16[4,16,2048]{2,1,0:T(8,128)(2,1)S(1)} %all_to_all.29), channel_id=1, replica_groups=mesh['seq'=128,'kvh'=4] {'kvh'}, dimensions={0} | all-to-all | bytes 524288 | tf_op jit(solution)/shard_map/all_to_all | solution.py:231
  194.1 0.7 copy.173
  (80 shorter events, 2.9 us)
Async XLA Ops:
  0.0 2.7 %copy-start = (bf16[64,16,128]{2,1,0:T(8,128)(2,1)S(1)}, bf16[64,16,128]{2,1,0:T(8,128)(2,1)}, u32[]{:S(2)}) copy-start(bf16[64,16,128]{2,1,0:T(8,128)(2,1)} %param.6) | copy-start | bytes 786436
  5.9 48.7 %all-to-all-start = ((bf16[128,2,16,128]{3,2,1,0:T(8,128)(2,1)}), bf16[128,2,16,128]{3,2,1,0:T(8,128)(2,1)S(1)}, u32[]{:S(2)}, u32[]{:S(2)}) async-start(bf16[128,2,16,128]{3,2,1,0:T(8,128)(2,1)} %bitcast.93), calls=%async_computation | async-start | bytes 2097152 | tf_op jit(solution)/shard_map/all_to_all | solution.py:126
  23.3 31.3 %copy-start.1 = (bf16[2,64,2,128]{3,2,1,0:T(2,128)(2,1)S(1)}, bf16[2,64,2,128]{3,2,1,0:T(2,128)(2,1)}, u32[]{:S(2)}) copy-start(bf16[2,64,2,128]{3,2,1,0:T(2,128)(2,1)} %param.7) | copy-start | bytes 196612
  54.6 11.0 %collective-permute-start = (bf16[1,2,64,2,128]{4,3,2,1,0:T(2,128)(2,1)S(1)}, bf16[1,2,64,2,128]{4,3,2,1,0:T(2,128)(2,1)S(1)}, u32[]{:S(2)}, u32[]{:S(2)}) collective-permute-start(bf16[1,2,64,2,128]{4,3,2,1,0:T(2,128)(2,1)S(1)} %bitcast.110), channel_id=1, source_target_pairs={{0,32},{4,36},{8,40},{12,44},{16,48},{20,52},{24,56},{28,60},{32,6... | collective-permute-start | bytes 196616 | tf_op jit(solution)/shard_map/ppermute | solution.py:19
  65.8 11.1 %collective-permute-start.1 = (bf16[2,2,64,2,128]{4,3,2,1,0:T(2,128)(2,1)S(1)}, bf16[2,2,64,2,128]{4,3,2,1,0:T(2,128)(2,1)S(1)}, u32[]{:S(2)}, u32[]{:S(2)}) collective-permute-start(bf16[2,2,64,2,128]{4,3,2,1,0:T(2,128)(2,1)S(1)} %pad_maximum_fusion.3), channel_id=1, source_target_pairs={{0,16},{4,20},{8,24},{12,28},{16,32},{20,36},{24,40},{28,44},{32,4... | collective-permute-start | bytes 393224 | tf_op jit(solution)/shard_map/ppermute | solution.py:19
  77.4 10.1 %collective-permute-start.2 = (bf16[4,2,64,2,128]{4,3,2,1,0:T(2,128)(2,1)S(1)}, bf16[4,2,64,2,128]{4,3,2,1,0:T(2,128)(2,1)S(1)}, u32[]{:S(2)}, u32[]{:S(2)}) collective-permute-start(bf16[4,2,64,2,128]{4,3,2,1,0:T(2,128)(2,1)S(1)} %pad_maximum_fusion.2), channel_id=1, source_target_pairs={{0,64},{4,68},{8,72},{12,76},{16,80},{20,84},{24,88},{28,92},{32,9... | collective-permute-start | bytes 786440 | tf_op jit(solution)/shard_map/ppermute | solution.py:19
  88.2 15.0 %collective-permute-start.3 = (bf16[8,2,64,2,128]{4,3,2,1,0:T(2,128)(2,1)S(1)}, bf16[8,2,64,2,128]{4,3,2,1,0:T(2,128)(2,1)S(1)}, u32[]{:S(2)}, u32[]{:S(2)}) collective-permute-start(bf16[8,2,64,2,128]{4,3,2,1,0:T(2,128)(2,1)S(1)} %pad_maximum_fusion.1), channel_id=1, source_target_pairs={{0,8},{4,12},{8,16},{12,20},{16,24},{20,28},{24,32},{28,36},{32,40... | collective-permute-start | bytes 1572872 | tf_op jit(solution)/shard_map/ppermute | solution.py:19
  105.2 18.6 %copy-start.7 = (f32[2,1,8,512]{3,2,1,0:T(8,128)S(1)}, f32[2,1,8,512]{3,2,1,0:T(8,128)}, u32[]{:S(2)}) copy-start(f32[2,1,8,512]{3,2,1,0:T(8,128)} %get-tuple-element.49) | copy-start | bytes 98308
  105.2 18.6 %copy-start.8 = (f32[2,1,8,512]{3,2,1,0:T(8,128)S(1)}, f32[2,1,8,512]{3,2,1,0:T(8,128)}, u32[]{:S(2)}) copy-start(f32[2,1,8,512]{3,2,1,0:T(8,128)} %get-tuple-element.50) | copy-start | bytes 98308
  105.2 18.6 %copy-start.9 = (f32[2,1,8,512]{3,2,1,0:T(8,128)S(1)}, f32[2,1,8,512]{3,2,1,0:T(8,128)}, u32[]{:S(2)}) copy-start(f32[2,1,8,512]{3,2,1,0:T(8,128)} %get-tuple-element.51) | copy-start | bytes 98308
  105.2 18.6 %collective-permute-start.4 = (bf16[16,2,64,2,128]{4,3,2,1,0:T(2,128)(2,1)}, bf16[16,2,64,2,128]{4,3,2,1,0:T(2,128)(2,1)S(1)}, u32[]{:S(2)}, u32[]{:S(2)}) collective-permute-start(bf16[16,2,64,2,128]{4,3,2,1,0:T(2,128)(2,1)} %get-tuple-element.74), channel_id=1, source_target_pairs={{0,4},{4,8},{8,12},{12,16},{16,20},{20,24},{24,28},{28,32},{32,36}... | collective-permute-start | bytes 3145736 | tf_op jit(solution)/shard_map/ppermute | solution.py:19
  114.7 11.8 %copy-start.3 = (bf16[32,2,16,128]{3,2,1,0:T(8,128)(2,1)S(1)}, bf16[32,2,16,128]{3,2,1,0:T(8,128)(2,1)}, u32[]{:S(2)}) copy-start(bf16[32,2,16,128]{3,2,1,0:T(8,128)(2,1)} %get-tuple-element.36) | copy-start | bytes 786436
  114.7 11.8 %copy-start.4 = (bf16[32,2,16,128]{3,2,1,0:T(8,128)(2,1)S(1)}, bf16[32,2,16,128]{3,2,1,0:T(8,128)(2,1)}, u32[]{:S(2)}) copy-start(bf16[32,2,16,128]{3,2,1,0:T(8,128)(2,1)} %get-tuple-element.40) | copy-start | bytes 786436
  114.7 11.8 %copy-start.5 = (bf16[32,2,16,128]{3,2,1,0:T(8,128)(2,1)S(1)}, bf16[32,2,16,128]{3,2,1,0:T(8,128)(2,1)}, u32[]{:S(2)}) copy-start(bf16[32,2,16,128]{3,2,1,0:T(8,128)(2,1)} %get-tuple-element.44) | copy-start | bytes 786436
  114.7 11.8 %copy-start.6 = (bf16[32,2,16,128]{3,2,1,0:T(8,128)(2,1)S(1)}, bf16[32,2,16,128]{3,2,1,0:T(8,128)(2,1)}, u32[]{:S(2)}) copy-start(bf16[32,2,16,128]{3,2,1,0:T(8,128)(2,1)} %get-tuple-element.48) | copy-start | bytes 786436
  131.1 45.0 %all-to-all-start.1 = ((bf16[128,2,2112]{2,1,0:T(2,128)(2,1)}), bf16[128,2,2112]{2,1,0:T(2,128)(2,1)S(1)}, u32[]{:S(2)}, u32[]{:S(2)}) async-start(bf16[128,2,2112]{2,1,0:T(2,128)(2,1)} %reshape.365), calls=%async_computation.1 | async-start | bytes 2228224 | tf_op jit(solution)/shard_map/all_to_all | solution.py:172
  181.6 1.2 copy-start.2

commit v10 on v9

--- a/solution.py
+++ b/solution.py
@@ -158,20 +158,20 @@
     lse_rounded = lax.reduce_precision(served_lse, exponent_bits=8, mantissa_bits=7)
     lse_high = lse_rounded.astype(jnp.bfloat16)
     lse_low = (served_lse - lse_rounded).astype(jnp.bfloat16)
-    payload_width = kv_heads * slab * head_dim
-    lse_width = 2 * kv_heads * slab
-    lse_lanes = -(-lse_width // 128) * 128
-    lse_pack = jnp.concatenate([lse_high, lse_low], axis=2).reshape(seq_count, lse_width)
+    payload_width = slab * head_dim
+    lse_width = 2 * slab
+    lse_lanes = -(-lse_width // 128) * 128 // 2
+    lse_pack = jnp.concatenate([lse_high, lse_low], axis=2)
     payload = jnp.concatenate(
         [
-            served.reshape(seq_count, payload_width),
-            jnp.pad(lse_pack, ((0, 0), (0, lse_lanes - lse_width))),
+            served.reshape(seq_count, kv_heads, payload_width),
+            jnp.pad(lse_pack, ((0, 0), (0, 0), (0, lse_lanes - lse_width))),
         ],
-        axis=1,
+        axis=2,
     )
     returned = lax.all_to_all(payload, "seq", split_axis=0, concat_axis=0, tiled=True)
-    answers = returned[:, :payload_width].reshape(seq_count, kv_heads, capacity, group_size * head_dim)
-    lse_parts = returned[:, payload_width : payload_width + lse_width].reshape(
+    answers = returned[:, :, :payload_width].reshape(seq_count, kv_heads, capacity, group_size * head_dim)
+    lse_parts = returned[:, :, payload_width : payload_width + lse_width].reshape(
         seq_count, kv_heads, 2, capacity, group_size
     )
     lse_parts = jnp.swapaxes(lse_parts, 2, 3).reshape(seq_count, kv_heads, capacity, 2 * group_size)

time: 196 us -> 192 us (0.980)
  local copies, waits for them, and re-layouts: 31.5 us -> 27.1 us
    all_to_all x2 -> x0, local copies, waits for them, and re-layouts: 3.24 us -> none  [per_device(): lax.all_to_all(payload, 'seq', split_axis=0, concat_axis=0, tiled=True)]
    unnamed x31 -> x30, local copies, waits for them, and re-layouts: 9.93 us -> 7.91 us
    concatenate x1 -> x2, other arithmetic: 0.01 us -> 1.98 us  [the longest x1 1.88 us: per_device(): jnp.concatenate([served.reshape(seq_count, kv_heads, payload_width), jnp....]
  transfers between devices with their start and end apart: 7 -> 7, of which waited for: 6 -> 6; matrix products, arithmetic and copies ran while one was open for 9% -> 9% of each run, Pallas kernels for 19% -> 20%
where the time goes in v10:
time: 192 us; the launch traced here: 191 us
  waiting for transfers between devices  60.6 us (32%)
  starting transfers between devices  43.5 us (23%)
  Pallas kernels  38 us (20%)
  local copies, waits for them, and re-layouts  27.1 us (14%)
  blocking collectives  10.8 us (6%)
  other arithmetic  9.24 us (5%)
    pallas_call x5, Pallas kernels, attend(): pl.pallas_call(functools.partial(attend_kernel, thr is not None, scaling,...  38 us
    all_to_all x1, waiting for transfers between devices, per_device(): lax.all_to_all(outgoing, 'seq', split_axis=0, concat_axis=0, tiled=True)  28.6 us
    all_to_all x1, starting transfers between devices, per_device(): lax.all_to_all(outgoing, 'seq', split_axis=0, concat_axis=0, tiled=True)  17.4 us
    all_to_all x1, waiting for transfers between devices, per_device(): lax.all_to_all(payload, 'seq', split_axis=0, concat_axis=0, tiled=True)  16.2 us
    ppermute x5, waiting for transfers between devices, shifted(): lax.ppermute(value, axis, [(source, source + steps) for source in range(i...  15.8 us
    ppermute x5, starting transfers between devices, shifted(): lax.ppermute(value, axis, [(source, source + steps) for source in range(i...  13.9 us
    all_to_all x1, starting transfers between devices, per_device(): lax.all_to_all(payload, 'seq', split_axis=0, concat_axis=0, tiled=True)  12.2 us
    all_to_all x1, blocking collectives, per_device(): lax.all_to_all(heads_out, 'kvh', split_axis=0, concat_axis=1, tiled=True)  10.8 us
  transfers between devices with their start and end apart: 7, of which 6 were waited for; matrix products, arithmetic and copies ran while one was open for 9% of the time, Pallas kernels for 20%

profile of v10, /device:TPU:8, one launch (start us, length us, event | category | flops | bytes accessed | tf_op | source)
XLA Modules:
  0.0 190.9 jit_solution(2521253054841987362)
XLA Ops:
  0.0 0.7 copy.110
  0.7 0.9 select_reduce_fusion
  1.8 0.1 reshape.197
  1.9 0.1 iota_compare_fusion
  2.1 0.2 fusion.9
  2.5 0.2 fusion.13
  2.8 0.8 copy_bitcast_fusion.3
  3.6 0.6 fusion
  4.2 1.7 copy.163
  5.9 17.4 %all-to-all-start = ((bf16[128,2,16,128]{3,2,1,0:T(8,128)(2,1)}), bf16[128,2,16,128]{3,2,1,0:T(8,128)(2,1)S(1)}, u32[]{:S(2)}, u32[]{:S(2)}) async-start(bf16[128,2,16,128]{3,2,1,0:T(8,128)(2,1)} %bitcast.86), calls=%async_computation | async-start | bytes 2097152 | tf_op jit(solution)/shard_map/all_to_all | solution.py:126
  23.3 2.7 %fusion.26 = (bf16[1,1,2048,2,128]{4,3,2,1,0:T(2,128)(2,1)S(1)}, bf16[1,1,2048,2,128]{4,3,2,1,0:T(2,128)(2,1)S(1)}) fusion(bf16[2,1,2048,2,128]{4,3,2,1,0:T(2,128)(2,1)} %param.8), kind=kLoop, calls=%fused_computation.116 | loop fusion | bytes 4194304 | tf_op jit(solution)/shard_map/slice | solution.py:129
  26.0 28.6 %all-to-all-done = bf16[128,2,16,128]{3,2,1,0:T(8,128)(2,1)S(1)} async-done(((bf16[128,2,16,128]{3,2,1,0:T(8,128)(2,1)}), bf16[128,2,16,128]{3,2,1,0:T(8,128)(2,1)S(1)}, u32[]{:S(2)}, u32[]{:S(2)}) %all-to-all-start) | async-done | bytes 1048608 | tf_op jit(solution)/shard_map/all_to_all | solution.py:126
  54.6 3.3 %collective-permute-start = (bf16[1,2,64,2,128]{4,3,2,1,0:T(2,128)(2,1)S(1)}, bf16[1,2,64,2,128]{4,3,2,1,0:T(2,128)(2,1)S(1)}, u32[]{:S(2)}, u32[]{:S(2)}) collective-permute-start(bf16[1,2,64,2,128]{4,3,2,1,0:T(2,128)(2,1)S(1)} %bitcast.97), channel_id=1, source_target_pairs={{0,32},{4,36},{8,40},{12,44},{16,48},{20,52},{24,56},{28,60},{32,6... | collective-permute-start | bytes 196616 | tf_op jit(solution)/shard_map/ppermute | solution.py:19
  57.9 1.6 copy_bitcast_fusion
  59.5 6.1 %collective-permute-done = bf16[1,2,64,2,128]{4,3,2,1,0:T(2,128)(2,1)S(1)} collective-permute-done((bf16[1,2,64,2,128]{4,3,2,1,0:T(2,128)(2,1)S(1)}, bf16[1,2,64,2,128]{4,3,2,1,0:T(2,128)(2,1)S(1)}, u32[]{:S(2)}, u32[]{:S(2)}) %collective-permute-start) | collective-permute-done | bytes 65568 | tf_op jit(solution)/shard_map/ppermute | solution.py:19
  65.7 0.2 pad_maximum_fusion.3
  65.8 2.4 %collective-permute-start.1 = (bf16[2,2,64,2,128]{4,3,2,1,0:T(2,128)(2,1)S(1)}, bf16[2,2,64,2,128]{4,3,2,1,0:T(2,128)(2,1)S(1)}, u32[]{:S(2)}, u32[]{:S(2)}) collective-permute-start(bf16[2,2,64,2,128]{4,3,2,1,0:T(2,128)(2,1)S(1)} %pad_maximum_fusion.3), channel_id=1, source_target_pairs={{0,16},{4,20},{8,24},{12,28},{16,32},{20,36},{24,40},{28,44},{32,4... | collective-permute-start | bytes 393224 | tf_op jit(solution)/shard_map/ppermute | solution.py:19
  68.2 1.1 fusion.27
  69.3 7.5 %shard_map.64 = (bf16[32,2,16,128]{3,2,1,0:T(8,128)(2,1)}, f32[2,1,8,512]{3,2,1,0:T(8,128)}) custom-call(bf16[32,2,16,128]{3,2,1,0:T(8,128)(2,1)} %get-tuple-element.72.refs_0_, bf16[2,2048,128]{2,1,0:T(8,128)(2,1)} %get-tuple-element.88.refs_1_, bf16[2,2048,128]{2,1,0:T(8,128)(2,1)} %get-tuple-element.87.refs_2_), custom_call_target="tpu_custom_call" | custom-call | flops 1073741824 | bytes 2621440 | tf_op jit(solution)/shard_map/pallas_call | solution.py:78
  76.7 0.2 collective-permute-done.1
  77.0 0.4 pad_maximum_fusion.2
  77.4 2.5 %collective-permute-start.2 = (bf16[4,2,64,2,128]{4,3,2,1,0:T(2,128)(2,1)S(1)}, bf16[4,2,64,2,128]{4,3,2,1,0:T(2,128)(2,1)S(1)}, u32[]{:S(2)}, u32[]{:S(2)}) collective-permute-start(bf16[4,2,64,2,128]{4,3,2,1,0:T(2,128)(2,1)S(1)} %pad_maximum_fusion.2), channel_id=1, source_target_pairs={{0,64},{4,68},{8,72},{12,76},{16,80},{20,84},{24,88},{28,92},{32,9... | collective-permute-start | bytes 786440 | tf_op jit(solution)/shard_map/ppermute | solution.py:19
  79.9 7.5 %shard_map.65 = (bf16[32,2,16,128]{3,2,1,0:T(8,128)(2,1)}, f32[2,1,8,512]{3,2,1,0:T(8,128)}) custom-call(bf16[32,2,16,128]{3,2,1,0:T(8,128)(2,1)} %get-tuple-element.71.refs_0_, bf16[2,2048,128]{2,1,0:T(8,128)(2,1)} %get-tuple-element.88.refs_1_, bf16[2,2048,128]{2,1,0:T(8,128)(2,1)} %get-tuple-element.87.refs_2_), custom_call_target="tpu_custom_call" | custom-call | flops 1073741824 | bytes 2621440 | tf_op jit(solution)/shard_map/pallas_call | solution.py:78
  87.4 0.7 pad_maximum_fusion.1
  88.2 3.6 %collective-permute-start.3 = (bf16[8,2,64,2,128]{4,3,2,1,0:T(2,128)(2,1)S(1)}, bf16[8,2,64,2,128]{4,3,2,1,0:T(2,128)(2,1)S(1)}, u32[]{:S(2)}, u32[]{:S(2)}) collective-permute-start(bf16[8,2,64,2,128]{4,3,2,1,0:T(2,128)(2,1)S(1)} %pad_maximum_fusion.1), channel_id=1, source_target_pairs={{0,8},{4,12},{8,16},{12,20},{16,24},{20,28},{24,32},{28,36},{32,40... | collective-permute-start | bytes 1572872 | tf_op jit(solution)/shard_map/ppermute | solution.py:19
  91.8 0.7 constant_dynamic-update-slice_fusion.10
  92.5 7.5 %shard_map.66 = (bf16[32,2,16,128]{3,2,1,0:T(8,128)(2,1)}, f32[2,1,8,512]{3,2,1,0:T(8,128)}) custom-call(bf16[32,2,16,128]{3,2,1,0:T(8,128)(2,1)} %get-tuple-element.70.refs_0_, bf16[2,2048,128]{2,1,0:T(8,128)(2,1)} %get-tuple-element.88.refs_1_, bf16[2,2048,128]{2,1,0:T(8,128)(2,1)} %get-tuple-element.87.refs_2_), custom_call_target="tpu_custom_call" | custom-call | flops 1073741824 | bytes 2621440 | tf_op jit(solution)/shard_map/pallas_call | solution.py:78
  100.0 0.7 constant_dynamic-update-slice_fusion.9
  100.7 0.8 constant_dynamic-update-slice_fusion.8
  101.5 1.2 constant_dynamic-update-slice_fusion.7
  102.7 0.5 collective-permute-done.3
  103.2 2.0 %constant_dynamic-update-slice_fusion.6 = (bf16[32,2,64,2,128]{4,3,2,1,0:T(2,128)(2,1)}, bf16[16,2,64,2,128]{4,3,2,1,0:T(2,128)(2,1)}) fusion(bf16[32,2,64,2,128]{4,3,2,1,0:T(2,128)(2,1)} %get-tuple-element.77, bf16[8,2,64,2,128]{4,3,2,1,0:T(2,128)(2,1)S(1)} %collective-permute-done.3, bf16[16,2,64,2,128]{4,3,2,1,0:T(2,128)(2,1)} %get-tuple-element.78), kind=kLoop, calls=%fused_computation.91 | loop fusion | bytes 1572864
  105.2 2.0 %collective-permute-start.4 = (bf16[16,2,64,2,128]{4,3,2,1,0:T(2,128)(2,1)}, bf16[16,2,64,2,128]{4,3,2,1,0:T(2,128)(2,1)S(1)}, u32[]{:S(2)}, u32[]{:S(2)}) collective-permute-start(bf16[16,2,64,2,128]{4,3,2,1,0:T(2,128)(2,1)} %get-tuple-element.74), channel_id=1, source_target_pairs={{0,4},{4,8},{8,12},{12,16},{16,20},{20,24},{24,28},{28,32},{32,36}... | collective-permute-start | bytes 3145736 | tf_op jit(solution)/shard_map/ppermute | solution.py:19
  107.2 7.5 %shard_map.67 = (bf16[32,2,16,128]{3,2,1,0:T(8,128)(2,1)}, f32[2,1,8,512]{3,2,1,0:T(8,128)}) custom-call(bf16[32,2,16,128]{3,2,1,0:T(8,128)(2,1)} %get-tuple-element.69.refs_0_, bf16[2,2048,128]{2,1,0:T(8,128)(2,1)} %get-tuple-element.88.refs_1_, bf16[2,2048,128]{2,1,0:T(8,128)(2,1)} %get-tuple-element.87.refs_2_), custom_call_target="tpu_custom_call" | custom-call | flops 1073741824 | bytes 2621440 | tf_op jit(solution)/shard_map/pallas_call | solution.py:78
  114.8 9.0 %collective-permute-done.4 = bf16[16,2,64,2,128]{4,3,2,1,0:T(2,128)(2,1)S(1)} collective-permute-done((bf16[16,2,64,2,128]{4,3,2,1,0:T(2,128)(2,1)}, bf16[16,2,64,2,128]{4,3,2,1,0:T(2,128)(2,1)S(1)}, u32[]{:S(2)}, u32[]{:S(2)}) %collective-permute-start.4) | collective-permute-done | bytes 1048608 | tf_op jit(solution)/shard_map/ppermute | solution.py:19
  123.7 0.8 fusion.21
  124.7 1.9 constant_dynamic-update-slice_fusion.5
  126.6 0.1 pad_maximum_fusion
  126.9 0.3 reshape.204
  127.2 1.9 fusion.1
  129.1 12.2 %all-to-all-start.1 = ((bf16[128,2,2112]{2,1,0:T(2,128)(2,1)}), bf16[128,2,2112]{2,1,0:T(2,128)(2,1)S(1)}, u32[]{:S(2)}, u32[]{:S(2)}) async-start(bf16[128,2,2112]{2,1,0:T(2,128)(2,1)} %fusion.1), calls=%async_computation.1 | async-start | bytes 2228224 | tf_op jit(solution)/shard_map/all_to_all | solution.py:172
  142.5 0.3 compare_reduce_fusion
  142.8 0.6 reshape_select_fusion.1.refs_0_
  143.4 2.9 %slice_bitcast_fusion = (bf16[2,32,64,128]{3,0,2,1:T(2,128)(2,1)S(1)}, bf16[2,32,64,128]{3,0,2,1:T(2,128)(2,1)S(1)}) fusion(bf16[32,2,64,2,128]{4,3,2,1,0:T(2,128)(2,1)} %constant_dynamic-update-slice_fusion.5), kind=kLoop, calls=%fused_computation.10 | loop fusion | bytes 4194304 | tf_op jit(solution)/shard_map/transpose | solution.py:179
  146.4 1.3 copy.119
  147.7 1.3 copy.118
  148.9 8.0 %shard_map.68 = (f32[2,512,128]{2,1,0:T(8,128)}, f32[2,1,8,512]{3,2,1,0:T(8,128)}) custom-call(s32[1,2048]{1,0:T(1,128)} %reshape_select_fusion.1.refs_0_, bf16[2,512,128]{2,1,0:T(8,128)(2,1)} %get-tuple-element.75.refs_1_, bf16[2,2048,128]{2,1,0:T(8,128)(2,1)} %bitcast.94, bf16[2,2048,128]{2,1,0:T(8,128)(2,1)} %bitcast.93), custom_call_target="tpu_custom_call" | custom-call | flops 1073741824 | bytes 2621440 | tf_op jit(solution)/shard_map/pallas_call | solution.py:78
  156.9 0.8 slice_reduce_fusion
  157.9 16.2 %all-to-all-done.1 = bf16[128,2,2112]{2,1,0:T(2,128)(2,1)S(1)} async-done(((bf16[128,2,2112]{2,1,0:T(2,128)(2,1)}), bf16[128,2,2112]{2,1,0:T(2,128)(2,1)S(1)}, u32[]{:S(2)}, u32[]{:S(2)}) %all-to-all-start.1) | async-done | bytes 1081376 | tf_op jit(solution)/shard_map/all_to_all | solution.py:172
  174.2 0.7 slice.107
  174.9 1.0 copy.146
  176.0 0.2 convolution_bitcast_fusion
  176.2 0.2 copy.123
  176.4 0.1 reduce_max.9
  176.6 0.1 copy.128
  176.7 0.2 fusion.25
  177.3 0.5 fusion.3
  177.8 0.3 copy.149
  178.2 0.5 multiply_reduce_fusion
  178.7 0.2 copy-done.2
  178.9 0.4 fusion.11
  179.3 0.1 all_to_all.22
  179.4 10.8 %all_to_all.29 = bf16[4,16,2048]{2,1,0:T(8,128)(2,1)S(1)} all-to-all(bf16[4,16,2048]{2,1,0:T(8,128)(2,1)S(1)} %all_to_all.22), channel_id=1, replica_groups=mesh['seq'=128,'kvh'=4] {'kvh'}, dimensions={0} | all-to-all | bytes 524288 | tf_op jit(solution)/shard_map/all_to_all | solution.py:231
  190.2 0.7 copy.148
  (74 shorter events, 2.7 us)
Async XLA Ops:
  0.0 2.7 %copy-start = (bf16[64,16,128]{2,1,0:T(8,128)(2,1)S(1)}, bf16[64,16,128]{2,1,0:T(8,128)(2,1)}, u32[]{:S(2)}) copy-start(bf16[64,16,128]{2,1,0:T(8,128)(2,1)} %param.6) | copy-start | bytes 786436
  5.9 48.7 %all-to-all-start = ((bf16[128,2,16,128]{3,2,1,0:T(8,128)(2,1)}), bf16[128,2,16,128]{3,2,1,0:T(8,128)(2,1)S(1)}, u32[]{:S(2)}, u32[]{:S(2)}) async-start(bf16[128,2,16,128]{3,2,1,0:T(8,128)(2,1)} %bitcast.86), calls=%async_computation | async-start | bytes 2097152 | tf_op jit(solution)/shard_map/all_to_all | solution.py:126
  23.3 31.3 %copy-start.1 = (bf16[2,64,2,128]{3,2,1,0:T(2,128)(2,1)S(1)}, bf16[2,64,2,128]{3,2,1,0:T(2,128)(2,1)}, u32[]{:S(2)}) copy-start(bf16[2,64,2,128]{3,2,1,0:T(2,128)(2,1)} %param.7) | copy-start | bytes 196612
  54.6 11.0 %collective-permute-start = (bf16[1,2,64,2,128]{4,3,2,1,0:T(2,128)(2,1)S(1)}, bf16[1,2,64,2,128]{4,3,2,1,0:T(2,128)(2,1)S(1)}, u32[]{:S(2)}, u32[]{:S(2)}) collective-permute-start(bf16[1,2,64,2,128]{4,3,2,1,0:T(2,128)(2,1)S(1)} %bitcast.97), channel_id=1, source_target_pairs={{0,32},{4,36},{8,40},{12,44},{16,48},{20,52},{24,56},{28,60},{32,6... | collective-permute-start | bytes 196616 | tf_op jit(solution)/shard_map/ppermute | solution.py:19
  65.8 11.1 %collective-permute-start.1 = (bf16[2,2,64,2,128]{4,3,2,1,0:T(2,128)(2,1)S(1)}, bf16[2,2,64,2,128]{4,3,2,1,0:T(2,128)(2,1)S(1)}, u32[]{:S(2)}, u32[]{:S(2)}) collective-permute-start(bf16[2,2,64,2,128]{4,3,2,1,0:T(2,128)(2,1)S(1)} %pad_maximum_fusion.3), channel_id=1, source_target_pairs={{0,16},{4,20},{8,24},{12,28},{16,32},{20,36},{24,40},{28,44},{32,4... | collective-permute-start | bytes 393224 | tf_op jit(solution)/shard_map/ppermute | solution.py:19
  77.4 10.1 %collective-permute-start.2 = (bf16[4,2,64,2,128]{4,3,2,1,0:T(2,128)(2,1)S(1)}, bf16[4,2,64,2,128]{4,3,2,1,0:T(2,128)(2,1)S(1)}, u32[]{:S(2)}, u32[]{:S(2)}) collective-permute-start(bf16[4,2,64,2,128]{4,3,2,1,0:T(2,128)(2,1)S(1)} %pad_maximum_fusion.2), channel_id=1, source_target_pairs={{0,64},{4,68},{8,72},{12,76},{16,80},{20,84},{24,88},{28,92},{32,9... | collective-permute-start | bytes 786440 | tf_op jit(solution)/shard_map/ppermute | solution.py:19
  88.2 15.0 %collective-permute-start.3 = (bf16[8,2,64,2,128]{4,3,2,1,0:T(2,128)(2,1)S(1)}, bf16[8,2,64,2,128]{4,3,2,1,0:T(2,128)(2,1)S(1)}, u32[]{:S(2)}, u32[]{:S(2)}) collective-permute-start(bf16[8,2,64,2,128]{4,3,2,1,0:T(2,128)(2,1)S(1)} %pad_maximum_fusion.1), channel_id=1, source_target_pairs={{0,8},{4,12},{8,16},{12,20},{16,24},{20,28},{24,32},{28,36},{32,40... | collective-permute-start | bytes 1572872 | tf_op jit(solution)/shard_map/ppermute | solution.py:19
  105.2 18.6 %copy-start.7 = (f32[2,1,8,512]{3,2,1,0:T(8,128)S(1)}, f32[2,1,8,512]{3,2,1,0:T(8,128)}, u32[]{:S(2)}) copy-start(f32[2,1,8,512]{3,2,1,0:T(8,128)} %get-tuple-element.49) | copy-start | bytes 98308
  105.2 18.6 %copy-start.8 = (f32[2,1,8,512]{3,2,1,0:T(8,128)S(1)}, f32[2,1,8,512]{3,2,1,0:T(8,128)}, u32[]{:S(2)}) copy-start(f32[2,1,8,512]{3,2,1,0:T(8,128)} %get-tuple-element.50) | copy-start | bytes 98308
  105.2 18.6 %copy-start.9 = (f32[2,1,8,512]{3,2,1,0:T(8,128)S(1)}, f32[2,1,8,512]{3,2,1,0:T(8,128)}, u32[]{:S(2)}) copy-start(f32[2,1,8,512]{3,2,1,0:T(8,128)} %get-tuple-element.51) | copy-start | bytes 98308
  105.2 18.6 %collective-permute-start.4 = (bf16[16,2,64,2,128]{4,3,2,1,0:T(2,128)(2,1)}, bf16[16,2,64,2,128]{4,3,2,1,0:T(2,128)(2,1)S(1)}, u32[]{:S(2)}, u32[]{:S(2)}) collective-permute-start(bf16[16,2,64,2,128]{4,3,2,1,0:T(2,128)(2,1)} %get-tuple-element.74), channel_id=1, source_target_pairs={{0,4},{4,8},{8,12},{12,16},{16,20},{20,24},{24,28},{28,32},{32,36}... | collective-permute-start | bytes 3145736 | tf_op jit(solution)/shard_map/ppermute | solution.py:19
  114.7 11.8 %copy-start.3 = (bf16[32,2,16,128]{3,2,1,0:T(8,128)(2,1)S(1)}, bf16[32,2,16,128]{3,2,1,0:T(8,128)(2,1)}, u32[]{:S(2)}) copy-start(bf16[32,2,16,128]{3,2,1,0:T(8,128)(2,1)} %get-tuple-element.36) | copy-start | bytes 786436
  114.7 11.8 %copy-start.4 = (bf16[32,2,16,128]{3,2,1,0:T(8,128)(2,1)S(1)}, bf16[32,2,16,128]{3,2,1,0:T(8,128)(2,1)}, u32[]{:S(2)}) copy-start(bf16[32,2,16,128]{3,2,1,0:T(8,128)(2,1)} %get-tuple-element.40) | copy-start | bytes 786436
  114.7 11.8 %copy-start.5 = (bf16[32,2,16,128]{3,2,1,0:T(8,128)(2,1)S(1)}, bf16[32,2,16,128]{3,2,1,0:T(8,128)(2,1)}, u32[]{:S(2)}) copy-start(bf16[32,2,16,128]{3,2,1,0:T(8,128)(2,1)} %get-tuple-element.44) | copy-start | bytes 786436
  114.7 11.8 %copy-start.6 = (bf16[32,2,16,128]{3,2,1,0:T(8,128)(2,1)S(1)}, bf16[32,2,16,128]{3,2,1,0:T(8,128)(2,1)}, u32[]{:S(2)}) copy-start(bf16[32,2,16,128]{3,2,1,0:T(8,128)(2,1)} %get-tuple-element.48) | copy-start | bytes 786436
  129.1 45.0 %all-to-all-start.1 = ((bf16[128,2,2112]{2,1,0:T(2,128)(2,1)}), bf16[128,2,2112]{2,1,0:T(2,128)(2,1)S(1)}, u32[]{:S(2)}, u32[]{:S(2)}) async-start(bf16[128,2,2112]{2,1,0:T(2,128)(2,1)} %fusion.1), calls=%async_computation.1 | async-start | bytes 2228224 | tf_op jit(solution)/shard_map/all_to_all | solution.py:172
  177.8 1.0 copy-start.2

commit v11 on v10

--- a/solution.py
+++ b/solution.py
@@ -156,12 +156,17 @@
     served_lse = jnp.swapaxes(served_lse, 0, 1)
     served, served_lse, window = lax.optimization_barrier((served, served_lse, window))
     lse_rounded = lax.reduce_precision(served_lse, exponent_bits=8, mantissa_bits=7)
-    lse_high = lse_rounded.astype(jnp.bfloat16)
-    lse_low = (served_lse - lse_rounded).astype(jnp.bfloat16)
+    lse_rest = served_lse - lse_rounded
+    lse_middle = lax.reduce_precision(lse_rest, exponent_bits=8, mantissa_bits=7)
+    lse_parts_out = [
+        lse_rounded.astype(jnp.bfloat16),
+        lse_middle.astype(jnp.bfloat16),
+        (lse_rest - lse_middle).astype(jnp.bfloat16),
+    ]
     payload_width = slab * head_dim
-    lse_width = 2 * slab
-    lse_lanes = -(-lse_width // 128) * 128 // 2
-    lse_pack = jnp.concatenate([lse_high, lse_low], axis=2)
+    lse_width = len(lse_parts_out) * slab
+    lse_lanes = -(-(2 * slab) // 128) * 128 // 2
+    lse_pack = jnp.concatenate(lse_parts_out, axis=2)
     payload = jnp.concatenate(
         [
             served.reshape(seq_count, kv_heads, payload_width),
@@ -171,10 +176,13 @@
     )
     returned = lax.all_to_all(payload, "seq", split_axis=0, concat_axis=0, tiled=True)
     answers = returned[:, :, :payload_width].reshape(seq_count, kv_heads, capacity, group_size * head_dim)
+    part_count = len(lse_parts_out)
     lse_parts = returned[:, :, payload_width : payload_width + lse_width].reshape(
-        seq_count, kv_heads, 2, capacity, group_size
-    )
-    lse_parts = jnp.swapaxes(lse_parts, 2, 3).reshape(seq_count, kv_heads, capacity, 2 * group_size)
+        seq_count, kv_heads, part_count, capacity, group_size
+    )
+    lse_parts = jnp.swapaxes(lse_parts, 2, 3).reshape(
+        seq_count, kv_heads, capacity, part_count * group_size
+    )
     window_keys = jnp.transpose(window[:, 0], (2, 0, 1, 3)).reshape(kv_heads, blocks * rows_local, head_dim)
     window_values = jnp.transpose(window[:, 1], (2, 0, 1, 3)).reshape(kv_heads, blocks * rows_local, head_dim)
     key_index = jnp.arange(blocks * rows_local, dtype=jnp.int32)
@@ -213,9 +221,11 @@
     picked_parts = jnp.einsum(
         "htcr,thcx->hrx", one_hot, lse_parts, preferred_element_type=jnp.float32
     )
-    picked_lse = (picked_parts[..., :group_size] + picked_parts[..., group_size:]).reshape(
-        kv_heads, rows_local, top_count, group_size
-    )
+    picked_lse = (
+        picked_parts[..., :group_size]
+        + picked_parts[..., group_size : 2 * group_size]
+        + picked_parts[..., 2 * group_size :]
+    ).reshape(kv_heads, rows_local, top_count, group_size)
     ceiling = jnp.maximum(own_lse, jnp.max(picked_lse, axis=2))
     own_weight = jnp.exp(own_lse - ceiling)
     far_weight = jnp.exp(picked_lse - ceiling[:, :, None])

time: 192 us -> 192 us (level)
  no operation moved by 1% of the time
where the time goes in v11:
time: 192 us; the launch traced here: 191 us
  waiting for transfers between devices  60.6 us (32%)
  starting transfers between devices  43.5 us (23%)
  Pallas kernels  38 us (20%)
  local copies, waits for them, and re-layouts  27.1 us (14%)
  blocking collectives  10.8 us (6%)
  other arithmetic  9.28 us (5%)
    pallas_call x5, Pallas kernels, attend(): pl.pallas_call(functools.partial(attend_kernel, thr is not None, scaling,...  38 us
    all_to_all x1, waiting for transfers between devices, per_device(): lax.all_to_all(outgoing, 'seq', split_axis=0, concat_axis=0, tiled=True)  28.6 us
    all_to_all x1, starting transfers between devices, per_device(): lax.all_to_all(outgoing, 'seq', split_axis=0, concat_axis=0, tiled=True)  17.4 us
    all_to_all x1, waiting for transfers between devices, per_device(): lax.all_to_all(payload, 'seq', split_axis=0, concat_axis=0, tiled=True)  16.2 us
    ppermute x5, waiting for transfers between devices, shifted(): lax.ppermute(value, axis, [(source, source + steps) for source in range(i...  15.8 us
    ppermute x5, starting transfers between devices, shifted(): lax.ppermute(value, axis, [(source, source + steps) for source in range(i...  13.9 us
    all_to_all x1, starting transfers between devices, per_device(): lax.all_to_all(payload, 'seq', split_axis=0, concat_axis=0, tiled=True)  12.2 us
    all_to_all x1, blocking collectives, per_device(): lax.all_to_all(heads_out, 'kvh', split_axis=0, concat_axis=1, tiled=True)  10.8 us
  transfers between devices with their start and end apart: 7, of which 6 were waited for; matrix products, arithmetic and copies ran while one was open for 9% of the time, Pallas kernels for 20%

profile of v11, /device:TPU:8, one launch (start us, length us, event | category | flops | bytes accessed | tf_op | source)
XLA Modules:
  0.0 191.0 jit_solution(10468859192660159719)
XLA Ops:
  0.0 0.7 copy.111
  0.7 0.9 select_reduce_fusion
  1.8 0.1 reshape.197
  1.9 0.1 iota_compare_fusion
  2.1 0.2 fusion.9
  2.5 0.2 fusion.13
  2.8 0.8 copy_bitcast_fusion.3
  3.6 0.6 fusion
  4.2 1.7 copy.164
  5.9 17.4 %all-to-all-start = ((bf16[128,2,16,128]{3,2,1,0:T(8,128)(2,1)}), bf16[128,2,16,128]{3,2,1,0:T(8,128)(2,1)S(1)}, u32[]{:S(2)}, u32[]{:S(2)}) async-start(bf16[128,2,16,128]{3,2,1,0:T(8,128)(2,1)} %bitcast.86), calls=%async_computation | async-start | bytes 2097152 | tf_op jit(solution)/shard_map/all_to_all | solution.py:126
  23.3 2.7 %fusion.26 = (bf16[1,1,2048,2,128]{4,3,2,1,0:T(2,128)(2,1)S(1)}, bf16[1,1,2048,2,128]{4,3,2,1,0:T(2,128)(2,1)S(1)}) fusion(bf16[2,1,2048,2,128]{4,3,2,1,0:T(2,128)(2,1)} %param.8), kind=kLoop, calls=%fused_computation.119 | loop fusion | bytes 4194304 | tf_op jit(solution)/shard_map/slice | solution.py:129
  26.0 28.6 %all-to-all-done = bf16[128,2,16,128]{3,2,1,0:T(8,128)(2,1)S(1)} async-done(((bf16[128,2,16,128]{3,2,1,0:T(8,128)(2,1)}), bf16[128,2,16,128]{3,2,1,0:T(8,128)(2,1)S(1)}, u32[]{:S(2)}, u32[]{:S(2)}) %all-to-all-start) | async-done | bytes 1048608 | tf_op jit(solution)/shard_map/all_to_all | solution.py:126
  54.6 3.3 %collective-permute-start = (bf16[1,2,64,2,128]{4,3,2,1,0:T(2,128)(2,1)S(1)}, bf16[1,2,64,2,128]{4,3,2,1,0:T(2,128)(2,1)S(1)}, u32[]{:S(2)}, u32[]{:S(2)}) collective-permute-start(bf16[1,2,64,2,128]{4,3,2,1,0:T(2,128)(2,1)S(1)} %bitcast.97), channel_id=1, source_target_pairs={{0,32},{4,36},{8,40},{12,44},{16,48},{20,52},{24,56},{28,60},{32,6... | collective-permute-start | bytes 196616 | tf_op jit(solution)/shard_map/ppermute | solution.py:19
  57.9 1.6 copy_bitcast_fusion
  59.5 6.1 %collective-permute-done = bf16[1,2,64,2,128]{4,3,2,1,0:T(2,128)(2,1)S(1)} collective-permute-done((bf16[1,2,64,2,128]{4,3,2,1,0:T(2,128)(2,1)S(1)}, bf16[1,2,64,2,128]{4,3,2,1,0:T(2,128)(2,1)S(1)}, u32[]{:S(2)}, u32[]{:S(2)}) %collective-permute-start) | collective-permute-done | bytes 65568 | tf_op jit(solution)/shard_map/ppermute | solution.py:19
  65.7 0.2 pad_maximum_fusion.3
  65.8 2.4 %collective-permute-start.1 = (bf16[2,2,64,2,128]{4,3,2,1,0:T(2,128)(2,1)S(1)}, bf16[2,2,64,2,128]{4,3,2,1,0:T(2,128)(2,1)S(1)}, u32[]{:S(2)}, u32[]{:S(2)}) collective-permute-start(bf16[2,2,64,2,128]{4,3,2,1,0:T(2,128)(2,1)S(1)} %pad_maximum_fusion.3), channel_id=1, source_target_pairs={{0,16},{4,20},{8,24},{12,28},{16,32},{20,36},{24,40},{28,44},{32,4... | collective-permute-start | bytes 393224 | tf_op jit(solution)/shard_map/ppermute | solution.py:19
  68.2 1.1 fusion.27
  69.3 7.5 %shard_map.64 = (bf16[32,2,16,128]{3,2,1,0:T(8,128)(2,1)}, f32[2,1,8,512]{3,2,1,0:T(8,128)}) custom-call(bf16[32,2,16,128]{3,2,1,0:T(8,128)(2,1)} %get-tuple-element.72.refs_0_, bf16[2,2048,128]{2,1,0:T(8,128)(2,1)} %get-tuple-element.89.refs_1_, bf16[2,2048,128]{2,1,0:T(8,128)(2,1)} %get-tuple-element.88.refs_2_), custom_call_target="tpu_custom_call" | custom-call | flops 1073741824 | bytes 2621440 | tf_op jit(solution)/shard_map/pallas_call | solution.py:78
  76.7 0.2 collective-permute-done.1
  77.0 0.4 pad_maximum_fusion.2
  77.4 2.5 %collective-permute-start.2 = (bf16[4,2,64,2,128]{4,3,2,1,0:T(2,128)(2,1)S(1)}, bf16[4,2,64,2,128]{4,3,2,1,0:T(2,128)(2,1)S(1)}, u32[]{:S(2)}, u32[]{:S(2)}) collective-permute-start(bf16[4,2,64,2,128]{4,3,2,1,0:T(2,128)(2,1)S(1)} %pad_maximum_fusion.2), channel_id=1, source_target_pairs={{0,64},{4,68},{8,72},{12,76},{16,80},{20,84},{24,88},{28,92},{32,9... | collective-permute-start | bytes 786440 | tf_op jit(solution)/shard_map/ppermute | solution.py:19
  79.9 7.5 %shard_map.65 = (bf16[32,2,16,128]{3,2,1,0:T(8,128)(2,1)}, f32[2,1,8,512]{3,2,1,0:T(8,128)}) custom-call(bf16[32,2,16,128]{3,2,1,0:T(8,128)(2,1)} %get-tuple-element.71.refs_0_, bf16[2,2048,128]{2,1,0:T(8,128)(2,1)} %get-tuple-element.89.refs_1_, bf16[2,2048,128]{2,1,0:T(8,128)(2,1)} %get-tuple-element.88.refs_2_), custom_call_target="tpu_custom_call" | custom-call | flops 1073741824 | bytes 2621440 | tf_op jit(solution)/shard_map/pallas_call | solution.py:78
  87.4 0.7 pad_maximum_fusion.1
  88.2 3.6 %collective-permute-start.3 = (bf16[8,2,64,2,128]{4,3,2,1,0:T(2,128)(2,1)S(1)}, bf16[8,2,64,2,128]{4,3,2,1,0:T(2,128)(2,1)S(1)}, u32[]{:S(2)}, u32[]{:S(2)}) collective-permute-start(bf16[8,2,64,2,128]{4,3,2,1,0:T(2,128)(2,1)S(1)} %pad_maximum_fusion.1), channel_id=1, source_target_pairs={{0,8},{4,12},{8,16},{12,20},{16,24},{20,28},{24,32},{28,36},{32,40... | collective-permute-start | bytes 1572872 | tf_op jit(solution)/shard_map/ppermute | solution.py:19
  91.8 0.7 constant_dynamic-update-slice_fusion.10
  92.5 7.5 %shard_map.66 = (bf16[32,2,16,128]{3,2,1,0:T(8,128)(2,1)}, f32[2,1,8,512]{3,2,1,0:T(8,128)}) custom-call(bf16[32,2,16,128]{3,2,1,0:T(8,128)(2,1)} %get-tuple-element.70.refs_0_, bf16[2,2048,128]{2,1,0:T(8,128)(2,1)} %get-tuple-element.89.refs_1_, bf16[2,2048,128]{2,1,0:T(8,128)(2,1)} %get-tuple-element.88.refs_2_), custom_call_target="tpu_custom_call" | custom-call | flops 1073741824 | bytes 2621440 | tf_op jit(solution)/shard_map/pallas_call | solution.py:78
  100.0 0.7 constant_dynamic-update-slice_fusion.9
  100.7 0.8 constant_dynamic-update-slice_fusion.8
  101.5 1.2 constant_dynamic-update-slice_fusion.7
  102.7 0.5 collective-permute-done.3
  103.2 2.0 %constant_dynamic-update-slice_fusion.6 = (bf16[32,2,64,2,128]{4,3,2,1,0:T(2,128)(2,1)}, bf16[16,2,64,2,128]{4,3,2,1,0:T(2,128)(2,1)}) fusion(bf16[32,2,64,2,128]{4,3,2,1,0:T(2,128)(2,1)} %get-tuple-element.77, bf16[8,2,64,2,128]{4,3,2,1,0:T(2,128)(2,1)S(1)} %collective-permute-done.3, bf16[16,2,64,2,128]{4,3,2,1,0:T(2,128)(2,1)} %get-tuple-element.78), kind=kLoop, calls=%fused_computation.95 | loop fusion | bytes 1572864
  105.2 2.0 %collective-permute-start.4 = (bf16[16,2,64,2,128]{4,3,2,1,0:T(2,128)(2,1)}, bf16[16,2,64,2,128]{4,3,2,1,0:T(2,128)(2,1)S(1)}, u32[]{:S(2)}, u32[]{:S(2)}) collective-permute-start(bf16[16,2,64,2,128]{4,3,2,1,0:T(2,128)(2,1)} %get-tuple-element.74), channel_id=1, source_target_pairs={{0,4},{4,8},{8,12},{12,16},{16,20},{20,24},{24,28},{28,32},{32,36}... | collective-permute-start | bytes 3145736 | tf_op jit(solution)/shard_map/ppermute | solution.py:19
  107.2 7.5 %shard_map.67 = (bf16[32,2,16,128]{3,2,1,0:T(8,128)(2,1)}, f32[2,1,8,512]{3,2,1,0:T(8,128)}) custom-call(bf16[32,2,16,128]{3,2,1,0:T(8,128)(2,1)} %get-tuple-element.69.refs_0_, bf16[2,2048,128]{2,1,0:T(8,128)(2,1)} %get-tuple-element.89.refs_1_, bf16[2,2048,128]{2,1,0:T(8,128)(2,1)} %get-tuple-element.88.refs_2_), custom_call_target="tpu_custom_call" | custom-call | flops 1073741824 | bytes 2621440 | tf_op jit(solution)/shard_map/pallas_call | solution.py:78
  114.8 9.0 %collective-permute-done.4 = bf16[16,2,64,2,128]{4,3,2,1,0:T(2,128)(2,1)S(1)} collective-permute-done((bf16[16,2,64,2,128]{4,3,2,1,0:T(2,128)(2,1)}, bf16[16,2,64,2,128]{4,3,2,1,0:T(2,128)(2,1)S(1)}, u32[]{:S(2)}, u32[]{:S(2)}) %collective-permute-start.4) | collective-permute-done | bytes 1048608 | tf_op jit(solution)/shard_map/ppermute | solution.py:19
  123.7 0.8 fusion.23
  124.7 1.9 constant_dynamic-update-slice_fusion.5
  126.6 0.1 pad_maximum_fusion
  127.0 0.3 reshape.204
  127.2 1.9 fusion.1
  129.1 12.2 %all-to-all-start.1 = ((bf16[128,2,2112]{2,1,0:T(2,128)(2,1)}), bf16[128,2,2112]{2,1,0:T(2,128)(2,1)S(1)}, u32[]{:S(2)}, u32[]{:S(2)}) async-start(bf16[128,2,2112]{2,1,0:T(2,128)(2,1)} %fusion.1), calls=%async_computation.1 | async-start | bytes 2228224 | tf_op jit(solution)/shard_map/all_to_all | solution.py:177
  142.5 0.3 compare_reduce_fusion
  142.9 0.6 reshape_select_fusion.1.refs_0_
  143.5 2.9 %slice_bitcast_fusion = (bf16[2,32,64,128]{3,0,2,1:T(2,128)(2,1)S(1)}, bf16[2,32,64,128]{3,0,2,1:T(2,128)(2,1)S(1)}) fusion(bf16[32,2,64,2,128]{4,3,2,1,0:T(2,128)(2,1)} %constant_dynamic-update-slice_fusion.5), kind=kLoop, calls=%fused_computation.10 | loop fusion | bytes 4194304 | tf_op jit(solution)/shard_map/transpose | solution.py:187
  146.4 1.3 copy.120
  147.7 1.3 copy.119
  149.0 8.0 %shard_map.68 = (f32[2,512,128]{2,1,0:T(8,128)}, f32[2,1,8,512]{3,2,1,0:T(8,128)}) custom-call(s32[1,2048]{1,0:T(1,128)} %reshape_select_fusion.1.refs_0_, bf16[2,512,128]{2,1,0:T(8,128)(2,1)} %get-tuple-element.75.refs_1_, bf16[2,2048,128]{2,1,0:T(8,128)(2,1)} %bitcast.94, bf16[2,2048,128]{2,1,0:T(8,128)(2,1)} %bitcast.93), custom_call_target="tpu_custom_call" | custom-call | flops 1073741824 | bytes 2621440 | tf_op jit(solution)/shard_map/pallas_call | solution.py:78
  157.0 0.8 slice_reduce_fusion
  157.9 16.2 %all-to-all-done.1 = bf16[128,2,2112]{2,1,0:T(2,128)(2,1)S(1)} async-done(((bf16[128,2,2112]{2,1,0:T(2,128)(2,1)}), bf16[128,2,2112]{2,1,0:T(2,128)(2,1)S(1)}, u32[]{:S(2)}, u32[]{:S(2)}) %all-to-all-start.1) | async-done | bytes 1081376 | tf_op jit(solution)/shard_map/all_to_all | solution.py:177
  174.2 0.7 slice.112
  175.0 1.0 copy.147
  176.0 0.2 convolution_bitcast_fusion
  176.3 0.2 copy.124
  176.4 0.1 reduce_max.9
  176.7 0.1 copy.129
  176.8 0.2 fusion.25
  177.4 0.5 fusion.3
  177.9 0.3 copy.150
  178.2 0.5 multiply_reduce_fusion
  178.7 0.2 copy-done.2
  178.9 0.4 fusion.11
  179.3 0.1 all_to_all.22
  179.5 10.8 %all_to_all.29 = bf16[4,16,2048]{2,1,0:T(8,128)(2,1)S(1)} all-to-all(bf16[4,16,2048]{2,1,0:T(8,128)(2,1)S(1)} %all_to_all.22), channel_id=1, replica_groups=mesh['seq'=128,'kvh'=4] {'kvh'}, dimensions={0} | all-to-all | bytes 524288 | tf_op jit(solution)/shard_map/all_to_all | solution.py:241
  190.2 0.7 copy.149
  (74 shorter events, 2.7 us)
Async XLA Ops:
  0.0 2.7 %copy-start = (bf16[64,16,128]{2,1,0:T(8,128)(2,1)S(1)}, bf16[64,16,128]{2,1,0:T(8,128)(2,1)}, u32[]{:S(2)}) copy-start(bf16[64,16,128]{2,1,0:T(8,128)(2,1)} %param.6) | copy-start | bytes 786436
  5.9 48.7 %all-to-all-start = ((bf16[128,2,16,128]{3,2,1,0:T(8,128)(2,1)}), bf16[128,2,16,128]{3,2,1,0:T(8,128)(2,1)S(1)}, u32[]{:S(2)}, u32[]{:S(2)}) async-start(bf16[128,2,16,128]{3,2,1,0:T(8,128)(2,1)} %bitcast.86), calls=%async_computation | async-start | bytes 2097152 | tf_op jit(solution)/shard_map/all_to_all | solution.py:126
  23.3 31.3 %copy-start.1 = (bf16[2,64,2,128]{3,2,1,0:T(2,128)(2,1)S(1)}, bf16[2,64,2,128]{3,2,1,0:T(2,128)(2,1)}, u32[]{:S(2)}) copy-start(bf16[2,64,2,128]{3,2,1,0:T(2,128)(2,1)} %param.7) | copy-start | bytes 196612
  54.6 11.0 %collective-permute-start = (bf16[1,2,64,2,128]{4,3,2,1,0:T(2,128)(2,1)S(1)}, bf16[1,2,64,2,128]{4,3,2,1,0:T(2,128)(2,1)S(1)}, u32[]{:S(2)}, u32[]{:S(2)}) collective-permute-start(bf16[1,2,64,2,128]{4,3,2,1,0:T(2,128)(2,1)S(1)} %bitcast.97), channel_id=1, source_target_pairs={{0,32},{4,36},{8,40},{12,44},{16,48},{20,52},{24,56},{28,60},{32,6... | collective-permute-start | bytes 196616 | tf_op jit(solution)/shard_map/ppermute | solution.py:19
  65.8 11.1 %collective-permute-start.1 = (bf16[2,2,64,2,128]{4,3,2,1,0:T(2,128)(2,1)S(1)}, bf16[2,2,64,2,128]{4,3,2,1,0:T(2,128)(2,1)S(1)}, u32[]{:S(2)}, u32[]{:S(2)}) collective-permute-start(bf16[2,2,64,2,128]{4,3,2,1,0:T(2,128)(2,1)S(1)} %pad_maximum_fusion.3), channel_id=1, source_target_pairs={{0,16},{4,20},{8,24},{12,28},{16,32},{20,36},{24,40},{28,44},{32,4... | collective-permute-start | bytes 393224 | tf_op jit(solution)/shard_map/ppermute | solution.py:19
  77.4 10.1 %collective-permute-start.2 = (bf16[4,2,64,2,128]{4,3,2,1,0:T(2,128)(2,1)S(1)}, bf16[4,2,64,2,128]{4,3,2,1,0:T(2,128)(2,1)S(1)}, u32[]{:S(2)}, u32[]{:S(2)}) collective-permute-start(bf16[4,2,64,2,128]{4,3,2,1,0:T(2,128)(2,1)S(1)} %pad_maximum_fusion.2), channel_id=1, source_target_pairs={{0,64},{4,68},{8,72},{12,76},{16,80},{20,84},{24,88},{28,92},{32,9... | collective-permute-start | bytes 786440 | tf_op jit(solution)/shard_map/ppermute | solution.py:19
  88.2 15.0 %collective-permute-start.3 = (bf16[8,2,64,2,128]{4,3,2,1,0:T(2,128)(2,1)S(1)}, bf16[8,2,64,2,128]{4,3,2,1,0:T(2,128)(2,1)S(1)}, u32[]{:S(2)}, u32[]{:S(2)}) collective-permute-start(bf16[8,2,64,2,128]{4,3,2,1,0:T(2,128)(2,1)S(1)} %pad_maximum_fusion.1), channel_id=1, source_target_pairs={{0,8},{4,12},{8,16},{12,20},{16,24},{20,28},{24,32},{28,36},{32,40... | collective-permute-start | bytes 1572872 | tf_op jit(solution)/shard_map/ppermute | solution.py:19
  105.2 18.6 %copy-start.7 = (f32[2,1,8,512]{3,2,1,0:T(8,128)S(1)}, f32[2,1,8,512]{3,2,1,0:T(8,128)}, u32[]{:S(2)}) copy-start(f32[2,1,8,512]{3,2,1,0:T(8,128)} %get-tuple-element.49) | copy-start | bytes 98308
  105.2 18.6 %copy-start.8 = (f32[2,1,8,512]{3,2,1,0:T(8,128)S(1)}, f32[2,1,8,512]{3,2,1,0:T(8,128)}, u32[]{:S(2)}) copy-start(f32[2,1,8,512]{3,2,1,0:T(8,128)} %get-tuple-element.50) | copy-start | bytes 98308
  105.2 18.6 %copy-start.9 = (f32[2,1,8,512]{3,2,1,0:T(8,128)S(1)}, f32[2,1,8,512]{3,2,1,0:T(8,128)}, u32[]{:S(2)}) copy-start(f32[2,1,8,512]{3,2,1,0:T(8,128)} %get-tuple-element.51) | copy-start | bytes 98308
  105.2 18.6 %collective-permute-start.4 = (bf16[16,2,64,2,128]{4,3,2,1,0:T(2,128)(2,1)}, bf16[16,2,64,2,128]{4,3,2,1,0:T(2,128)(2,1)S(1)}, u32[]{:S(2)}, u32[]{:S(2)}) collective-permute-start(bf16[16,2,64,2,128]{4,3,2,1,0:T(2,128)(2,1)} %get-tuple-element.74), channel_id=1, source_target_pairs={{0,4},{4,8},{8,12},{12,16},{16,20},{20,24},{24,28},{28,32},{32,36}... | collective-permute-start | bytes 3145736 | tf_op jit(solution)/shard_map/ppermute | solution.py:19
  114.7 11.8 %copy-start.3 = (bf16[32,2,16,128]{3,2,1,0:T(8,128)(2,1)S(1)}, bf16[32,2,16,128]{3,2,1,0:T(8,128)(2,1)}, u32[]{:S(2)}) copy-start(bf16[32,2,16,128]{3,2,1,0:T(8,128)(2,1)} %get-tuple-element.36) | copy-start | bytes 786436
  114.7 11.8 %copy-start.4 = (bf16[32,2,16,128]{3,2,1,0:T(8,128)(2,1)S(1)}, bf16[32,2,16,128]{3,2,1,0:T(8,128)(2,1)}, u32[]{:S(2)}) copy-start(bf16[32,2,16,128]{3,2,1,0:T(8,128)(2,1)} %get-tuple-element.40) | copy-start | bytes 786436
  114.7 11.8 %copy-start.5 = (bf16[32,2,16,128]{3,2,1,0:T(8,128)(2,1)S(1)}, bf16[32,2,16,128]{3,2,1,0:T(8,128)(2,1)}, u32[]{:S(2)}) copy-start(bf16[32,2,16,128]{3,2,1,0:T(8,128)(2,1)} %get-tuple-element.44) | copy-start | bytes 786436
  114.7 11.8 %copy-start.6 = (bf16[32,2,16,128]{3,2,1,0:T(8,128)(2,1)S(1)}, bf16[32,2,16,128]{3,2,1,0:T(8,128)(2,1)}, u32[]{:S(2)}) copy-start(bf16[32,2,16,128]{3,2,1,0:T(8,128)(2,1)} %get-tuple-element.48) | copy-start | bytes 786436
  129.1 45.0 %all-to-all-start.1 = ((bf16[128,2,2112]{2,1,0:T(2,128)(2,1)}), bf16[128,2,2112]{2,1,0:T(2,128)(2,1)S(1)}, u32[]{:S(2)}, u32[]{:S(2)}) async-start(bf16[128,2,2112]{2,1,0:T(2,128)(2,1)} %fusion.1), calls=%async_computation.1 | async-start | bytes 2228224 | tf_op jit(solution)/shard_map/all_to_all | solution.py:177
  177.9 1.0 copy-start.2

commit v12 on v11

--- a/solution.py
+++ b/solution.py
@@ -117,9 +117,16 @@
         .astype(jnp.bfloat16)
         .reshape(kv_heads, seq_count, capacity, requests)
     )
-    requested = jnp.repeat(jnp.swapaxes(grouped, 0, 1), top_count, axis=1)
+    requested = jnp.repeat(jnp.swapaxes(grouped, 0, 1), top_count, axis=1).reshape(
+        kv_heads * requests, group_size, head_dim
+    )
+    head_ids = jnp.arange(kv_heads, dtype=jnp.int32)[:, None]
+    row_of = ((targets * kv_heads + head_ids) * capacity + places).reshape(kv_heads * requests)
+    spread = (
+        jnp.arange(seq_count * kv_heads * capacity, dtype=jnp.int32)[:, None] == row_of[None, :]
+    ).astype(jnp.bfloat16)
     outgoing = jnp.einsum(
-        "htcr,hrgd->thcgd", one_hot, requested, preferred_element_type=jnp.float32
+        "Rk,kgd->Rgd", spread, requested, preferred_element_type=jnp.float32
     ).astype(jnp.bfloat16)
     slab = capacity * group_size
     outgoing = outgoing.reshape(seq_count, kv_heads, slab, head_dim)

time: 192 us -> 193 us (level)
  no operation moved by 1% of the time
where the time goes in v12:
time: 193 us; the launch traced here: 192 us
  waiting for transfers between devices  61 us (32%)
  starting transfers between devices  43.5 us (23%)
  Pallas kernels  38 us (20%)
  local copies, waits for them, and re-layouts  27.6 us (14%)
  blocking collectives  10.8 us (6%)
  other arithmetic  9.07 us (5%)
    pallas_call x5, Pallas kernels, attend(): pl.pallas_call(functools.partial(attend_kernel, thr is not None, scaling,...  38 us
    all_to_all x1, waiting for transfers between devices, per_device(): lax.all_to_all(outgoing, 'seq', split_axis=0, concat_axis=0, tiled=True)  28.6 us
    all_to_all x1, starting transfers between devices, per_device(): lax.all_to_all(outgoing, 'seq', split_axis=0, concat_axis=0, tiled=True)  17.4 us
    all_to_all x1, waiting for transfers between devices, per_device(): lax.all_to_all(payload, 'seq', split_axis=0, concat_axis=0, tiled=True)  16.4 us
    ppermute x5, waiting for transfers between devices, shifted(): lax.ppermute(value, axis, [(source, source + steps) for source in range(i...  16 us
    ppermute x5, starting transfers between devices, shifted(): lax.ppermute(value, axis, [(source, source + steps) for source in range(i...  13.9 us
    all_to_all x1, starting transfers between devices, per_device(): lax.all_to_all(payload, 'seq', split_axis=0, concat_axis=0, tiled=True)  12.2 us
    all_to_all x1, blocking collectives, per_device(): lax.all_to_all(heads_out, 'kvh', split_axis=0, concat_axis=1, tiled=True)  10.8 us
  transfers between devices with their start and end apart: 7, of which 6 were waited for; matrix products, arithmetic and copies ran while one was open for 9% of the time, Pallas kernels for 20%

profile of v12, /device:TPU:8, one launch (start us, length us, event | category | flops | bytes accessed | tf_op | source)
XLA Modules:
  0.0 191.8 jit_solution(5161931887949790569)
XLA Ops:
  0.0 0.7 copy.112
  0.7 0.9 select_reduce_fusion
  1.9 0.1 eq.89
  2.0 0.1 iota_compare_fusion.1
  2.3 0.2 mul.44
  2.5 0.2 fusion.11
  2.9 0.2 fusion.15
  3.2 0.8 copy_bitcast_fusion.2
  4.1 0.7 convolution_convert_fusion
  4.9 1.7 copy.118
  6.5 17.4 %all-to-all-start = ((bf16[128,2,16,128]{3,2,1,0:T(8,128)(2,1)}), bf16[128,2,16,128]{3,2,1,0:T(8,128)(2,1)S(1)}, u32[]{:S(2)}, u32[]{:S(2)}) async-start(bf16[128,2,16,128]{3,2,1,0:T(8,128)(2,1)} %bitcast.10), calls=%async_computation | async-start | bytes 2097152 | tf_op jit(solution)/shard_map/all_to_all | solution.py:133
  23.9 2.7 %fusion.26 = (bf16[1,1,2048,2,128]{4,3,2,1,0:T(2,128)(2,1)S(1)}, bf16[1,1,2048,2,128]{4,3,2,1,0:T(2,128)(2,1)S(1)}) fusion(bf16[2,1,2048,2,128]{4,3,2,1,0:T(2,128)(2,1)} %param.8), kind=kLoop, calls=%fused_computation.119 | loop fusion | bytes 4194304 | tf_op jit(solution)/shard_map/slice | solution.py:136
  26.6 28.6 %all-to-all-done = bf16[128,2,16,128]{3,2,1,0:T(8,128)(2,1)S(1)} async-done(((bf16[128,2,16,128]{3,2,1,0:T(8,128)(2,1)}), bf16[128,2,16,128]{3,2,1,0:T(8,128)(2,1)S(1)}, u32[]{:S(2)}, u32[]{:S(2)}) %all-to-all-start) | async-done | bytes 1048608 | tf_op jit(solution)/shard_map/all_to_all | solution.py:133
  55.2 3.3 %collective-permute-start = (bf16[1,2,64,2,128]{4,3,2,1,0:T(2,128)(2,1)S(1)}, bf16[1,2,64,2,128]{4,3,2,1,0:T(2,128)(2,1)S(1)}, u32[]{:S(2)}, u32[]{:S(2)}) collective-permute-start(bf16[1,2,64,2,128]{4,3,2,1,0:T(2,128)(2,1)S(1)} %bitcast.88), channel_id=1, source_target_pairs={{0,32},{4,36},{8,40},{12,44},{16,48},{20,52},{24,56},{28,60},{32,6... | collective-permute-start | bytes 196616 | tf_op jit(solution)/shard_map/ppermute | solution.py:19
  58.6 1.6 copy_bitcast_fusion
  60.1 6.1 %collective-permute-done = bf16[1,2,64,2,128]{4,3,2,1,0:T(2,128)(2,1)S(1)} collective-permute-done((bf16[1,2,64,2,128]{4,3,2,1,0:T(2,128)(2,1)S(1)}, bf16[1,2,64,2,128]{4,3,2,1,0:T(2,128)(2,1)S(1)}, u32[]{:S(2)}, u32[]{:S(2)}) %collective-permute-start) | collective-permute-done | bytes 65568 | tf_op jit(solution)/shard_map/ppermute | solution.py:19
  66.3 0.2 pad_maximum_fusion.3
  66.4 2.4 %collective-permute-start.1 = (bf16[2,2,64,2,128]{4,3,2,1,0:T(2,128)(2,1)S(1)}, bf16[2,2,64,2,128]{4,3,2,1,0:T(2,128)(2,1)S(1)}, u32[]{:S(2)}, u32[]{:S(2)}) collective-permute-start(bf16[2,2,64,2,128]{4,3,2,1,0:T(2,128)(2,1)S(1)} %pad_maximum_fusion.3), channel_id=1, source_target_pairs={{0,16},{4,20},{8,24},{12,28},{16,32},{20,36},{24,40},{28,44},{32,4... | collective-permute-start | bytes 393224 | tf_op jit(solution)/shard_map/ppermute | solution.py:19
  68.8 1.1 fusion.27
  69.9 7.5 %shard_map.64 = (bf16[32,2,16,128]{3,2,1,0:T(8,128)(2,1)}, f32[2,1,8,512]{3,2,1,0:T(8,128)}) custom-call(bf16[32,2,16,128]{3,2,1,0:T(8,128)(2,1)} %get-tuple-element.72.refs_0_, bf16[2,2048,128]{2,1,0:T(8,128)(2,1)} %get-tuple-element.89.refs_1_, bf16[2,2048,128]{2,1,0:T(8,128)(2,1)} %get-tuple-element.88.refs_2_), custom_call_target="tpu_custom_call" | custom-call | flops 1073741824 | bytes 2621440 | tf_op jit(solution)/shard_map/pallas_call | solution.py:78
  77.4 0.2 collective-permute-done.1
  77.6 0.4 pad_maximum_fusion.2
  78.0 2.7 %collective-permute-start.2 = (bf16[4,2,64,2,128]{4,3,2,1,0:T(2,128)(2,1)S(1)}, bf16[4,2,64,2,128]{4,3,2,1,0:T(2,128)(2,1)S(1)}, u32[]{:S(2)}, u32[]{:S(2)}) collective-permute-start(bf16[4,2,64,2,128]{4,3,2,1,0:T(2,128)(2,1)S(1)} %pad_maximum_fusion.2), channel_id=1, source_target_pairs={{0,64},{4,68},{8,72},{12,76},{16,80},{20,84},{24,88},{28,92},{32,9... | collective-permute-start | bytes 786440 | tf_op jit(solution)/shard_map/ppermute | solution.py:19
  80.7 7.5 %shard_map.65 = (bf16[32,2,16,128]{3,2,1,0:T(8,128)(2,1)}, f32[2,1,8,512]{3,2,1,0:T(8,128)}) custom-call(bf16[32,2,16,128]{3,2,1,0:T(8,128)(2,1)} %get-tuple-element.71.refs_0_, bf16[2,2048,128]{2,1,0:T(8,128)(2,1)} %get-tuple-element.89.refs_1_, bf16[2,2048,128]{2,1,0:T(8,128)(2,1)} %get-tuple-element.88.refs_2_), custom_call_target="tpu_custom_call" | custom-call | flops 1073741824 | bytes 2621440 | tf_op jit(solution)/shard_map/pallas_call | solution.py:78
  88.2 0.7 pad_maximum_fusion.1
  89.0 3.4 %collective-permute-start.3 = (bf16[8,2,64,2,128]{4,3,2,1,0:T(2,128)(2,1)S(1)}, bf16[8,2,64,2,128]{4,3,2,1,0:T(2,128)(2,1)S(1)}, u32[]{:S(2)}, u32[]{:S(2)}) collective-permute-start(bf16[8,2,64,2,128]{4,3,2,1,0:T(2,128)(2,1)S(1)} %pad_maximum_fusion.1), channel_id=1, source_target_pairs={{0,8},{4,12},{8,16},{12,20},{16,24},{20,28},{24,32},{28,36},{32,40... | collective-permute-start | bytes 1572872 | tf_op jit(solution)/shard_map/ppermute | solution.py:19
  92.4 0.7 constant_dynamic-update-slice_fusion.10
  93.1 7.5 %shard_map.66 = (bf16[32,2,16,128]{3,2,1,0:T(8,128)(2,1)}, f32[2,1,8,512]{3,2,1,0:T(8,128)}) custom-call(bf16[32,2,16,128]{3,2,1,0:T(8,128)(2,1)} %get-tuple-element.70.refs_0_, bf16[2,2048,128]{2,1,0:T(8,128)(2,1)} %get-tuple-element.89.refs_1_, bf16[2,2048,128]{2,1,0:T(8,128)(2,1)} %get-tuple-element.88.refs_2_), custom_call_target="tpu_custom_call" | custom-call | flops 1073741824 | bytes 2621440 | tf_op jit(solution)/shard_map/pallas_call | solution.py:78
  100.6 0.7 constant_dynamic-update-slice_fusion.9
  101.3 0.8 constant_dynamic-update-slice_fusion.8
  102.1 1.2 constant_dynamic-update-slice_fusion.7
  103.4 0.7 collective-permute-done.3
  104.0 2.0 %constant_dynamic-update-slice_fusion.6 = (bf16[32,2,64,2,128]{4,3,2,1,0:T(2,128)(2,1)}, bf16[16,2,64,2,128]{4,3,2,1,0:T(2,128)(2,1)}) fusion(bf16[32,2,64,2,128]{4,3,2,1,0:T(2,128)(2,1)} %get-tuple-element.77, bf16[8,2,64,2,128]{4,3,2,1,0:T(2,128)(2,1)S(1)} %collective-permute-done.3, bf16[16,2,64,2,128]{4,3,2,1,0:T(2,128)(2,1)} %get-tuple-element.78), kind=kLoop, calls=%fused_computation.93 | loop fusion | bytes 1572864
  106.0 2.0 %collective-permute-start.4 = (bf16[16,2,64,2,128]{4,3,2,1,0:T(2,128)(2,1)}, bf16[16,2,64,2,128]{4,3,2,1,0:T(2,128)(2,1)S(1)}, u32[]{:S(2)}, u32[]{:S(2)}) collective-permute-start(bf16[16,2,64,2,128]{4,3,2,1,0:T(2,128)(2,1)} %get-tuple-element.74), channel_id=1, source_target_pairs={{0,4},{4,8},{8,12},{12,16},{16,20},{20,24},{24,28},{28,32},{32,36}... | collective-permute-start | bytes 3145736 | tf_op jit(solution)/shard_map/ppermute | solution.py:19
  108.0 7.5 %shard_map.67 = (bf16[32,2,16,128]{3,2,1,0:T(8,128)(2,1)}, f32[2,1,8,512]{3,2,1,0:T(8,128)}) custom-call(bf16[32,2,16,128]{3,2,1,0:T(8,128)(2,1)} %get-tuple-element.69.refs_0_, bf16[2,2048,128]{2,1,0:T(8,128)(2,1)} %get-tuple-element.89.refs_1_, bf16[2,2048,128]{2,1,0:T(8,128)(2,1)} %get-tuple-element.88.refs_2_), custom_call_target="tpu_custom_call" | custom-call | flops 1073741824 | bytes 2621440 | tf_op jit(solution)/shard_map/pallas_call | solution.py:78
  115.5 9.0 %collective-permute-done.4 = bf16[16,2,64,2,128]{4,3,2,1,0:T(2,128)(2,1)S(1)} collective-permute-done((bf16[16,2,64,2,128]{4,3,2,1,0:T(2,128)(2,1)}, bf16[16,2,64,2,128]{4,3,2,1,0:T(2,128)(2,1)S(1)}, u32[]{:S(2)}, u32[]{:S(2)}) %collective-permute-start.4) | collective-permute-done | bytes 1048608 | tf_op jit(solution)/shard_map/ppermute | solution.py:19
  124.5 0.8 fusion.23
  125.4 1.9 constant_dynamic-update-slice_fusion.5
  127.4 0.1 pad_maximum_fusion
  127.6 0.1 pad_maximum_fusion.4
  127.7 0.3 reshape.217
  128.0 1.9 fusion
  129.9 12.2 %all-to-all-start.1 = ((bf16[128,2,2112]{2,1,0:T(2,128)(2,1)}), bf16[128,2,2112]{2,1,0:T(2,128)(2,1)S(1)}, u32[]{:S(2)}, u32[]{:S(2)}) async-start(bf16[128,2,2112]{2,1,0:T(2,128)(2,1)} %fusion), calls=%async_computation.1 | async-start | bytes 2228224 | tf_op jit(solution)/shard_map/all_to_all | solution.py:184
  143.4 0.6 reshape_select_fusion.1.refs_0_
  144.1 2.9 %slice_bitcast_fusion = (bf16[2,32,64,128]{3,0,2,1:T(2,128)(2,1)S(1)}, bf16[2,32,64,128]{3,0,2,1:T(2,128)(2,1)S(1)}) fusion(bf16[32,2,64,2,128]{4,3,2,1,0:T(2,128)(2,1)} %constant_dynamic-update-slice_fusion.5), kind=kLoop, calls=%fused_computation.8 | loop fusion | bytes 4194304 | tf_op jit(solution)/shard_map/transpose | solution.py:194
  147.0 1.3 copy.122
  148.3 1.3 copy.121
  149.6 8.0 %shard_map.68 = (f32[2,512,128]{2,1,0:T(8,128)}, f32[2,1,8,512]{3,2,1,0:T(8,128)}) custom-call(s32[1,2048]{1,0:T(1,128)} %reshape_select_fusion.1.refs_0_, bf16[2,512,128]{2,1,0:T(8,128)(2,1)} %get-tuple-element.75.refs_1_, bf16[2,2048,128]{2,1,0:T(8,128)(2,1)} %bitcast.85, bf16[2,2048,128]{2,1,0:T(8,128)(2,1)} %bitcast.84), custom_call_target="tpu_custom_call" | custom-call | flops 1073741824 | bytes 2621440 | tf_op jit(solution)/shard_map/pallas_call | solution.py:78
  157.6 0.8 slice_reduce_fusion
  158.5 16.4 %all-to-all-done.1 = bf16[128,2,2112]{2,1,0:T(2,128)(2,1)S(1)} async-done(((bf16[128,2,2112]{2,1,0:T(2,128)(2,1)}), bf16[128,2,2112]{2,1,0:T(2,128)(2,1)S(1)}, u32[]{:S(2)}, u32[]{:S(2)}) %all-to-all-start.1) | async-done | bytes 1081376 | tf_op jit(solution)/shard_map/all_to_all | solution.py:184
  175.0 0.7 slice.112
  175.8 1.0 copy.145
  176.8 0.2 convolution_bitcast_fusion
  177.1 0.2 copy.126
  177.2 0.1 reduce_max.9
  177.6 0.2 fusion.25
  178.2 0.5 fusion.7
  178.7 0.3 copy.148
  179.0 0.5 multiply_reduce_fusion
  179.5 0.2 copy-done.2
  179.7 0.4 fusion.13
  180.1 0.1 all_to_all.22
  180.3 10.8 %all_to_all.29 = bf16[4,16,2048]{2,1,0:T(8,128)(2,1)S(1)} all-to-all(bf16[4,16,2048]{2,1,0:T(8,128)(2,1)S(1)} %all_to_all.22), channel_id=1, replica_groups=mesh['seq'=128,'kvh'=4] {'kvh'}, dimensions={0} | all-to-all | bytes 524288 | tf_op jit(solution)/shard_map/all_to_all | solution.py:248
  191.0 0.7 copy.147
  (81 shorter events, 3.0 us)
Async XLA Ops:
  0.0 3.2 %copy-start = (bf16[64,16,128]{2,1,0:T(8,128)(2,1)S(1)}, bf16[64,16,128]{2,1,0:T(8,128)(2,1)}, u32[]{:S(2)}) copy-start(bf16[64,16,128]{2,1,0:T(8,128)(2,1)} %param.6) | copy-start | bytes 786436
  6.5 48.7 %all-to-all-start = ((bf16[128,2,16,128]{3,2,1,0:T(8,128)(2,1)}), bf16[128,2,16,128]{3,2,1,0:T(8,128)(2,1)S(1)}, u32[]{:S(2)}, u32[]{:S(2)}) async-start(bf16[128,2,16,128]{3,2,1,0:T(8,128)(2,1)} %bitcast.10), calls=%async_computation | async-start | bytes 2097152 | tf_op jit(solution)/shard_map/all_to_all | solution.py:133
  23.9 31.3 %copy-start.1 = (bf16[2,64,2,128]{3,2,1,0:T(2,128)(2,1)S(1)}, bf16[2,64,2,128]{3,2,1,0:T(2,128)(2,1)}, u32[]{:S(2)}) copy-start(bf16[2,64,2,128]{3,2,1,0:T(2,128)(2,1)} %param.7) | copy-start | bytes 196612
  55.2 11.0 %collective-permute-start = (bf16[1,2,64,2,128]{4,3,2,1,0:T(2,128)(2,1)S(1)}, bf16[1,2,64,2,128]{4,3,2,1,0:T(2,128)(2,1)S(1)}, u32[]{:S(2)}, u32[]{:S(2)}) collective-permute-start(bf16[1,2,64,2,128]{4,3,2,1,0:T(2,128)(2,1)S(1)} %bitcast.88), channel_id=1, source_target_pairs={{0,32},{4,36},{8,40},{12,44},{16,48},{20,52},{24,56},{28,60},{32,6... | collective-permute-start | bytes 196616 | tf_op jit(solution)/shard_map/ppermute | solution.py:19
  66.4 11.1 %collective-permute-start.1 = (bf16[2,2,64,2,128]{4,3,2,1,0:T(2,128)(2,1)S(1)}, bf16[2,2,64,2,128]{4,3,2,1,0:T(2,128)(2,1)S(1)}, u32[]{:S(2)}, u32[]{:S(2)}) collective-permute-start(bf16[2,2,64,2,128]{4,3,2,1,0:T(2,128)(2,1)S(1)} %pad_maximum_fusion.3), channel_id=1, source_target_pairs={{0,16},{4,20},{8,24},{12,28},{16,32},{20,36},{24,40},{28,44},{32,4... | collective-permute-start | bytes 393224 | tf_op jit(solution)/shard_map/ppermute | solution.py:19
  78.0 10.2 %collective-permute-start.2 = (bf16[4,2,64,2,128]{4,3,2,1,0:T(2,128)(2,1)S(1)}, bf16[4,2,64,2,128]{4,3,2,1,0:T(2,128)(2,1)S(1)}, u32[]{:S(2)}, u32[]{:S(2)}) collective-permute-start(bf16[4,2,64,2,128]{4,3,2,1,0:T(2,128)(2,1)S(1)} %pad_maximum_fusion.2), channel_id=1, source_target_pairs={{0,64},{4,68},{8,72},{12,76},{16,80},{20,84},{24,88},{28,92},{32,9... | collective-permute-start | bytes 786440 | tf_op jit(solution)/shard_map/ppermute | solution.py:19
  89.0 15.0 %collective-permute-start.3 = (bf16[8,2,64,2,128]{4,3,2,1,0:T(2,128)(2,1)S(1)}, bf16[8,2,64,2,128]{4,3,2,1,0:T(2,128)(2,1)S(1)}, u32[]{:S(2)}, u32[]{:S(2)}) collective-permute-start(bf16[8,2,64,2,128]{4,3,2,1,0:T(2,128)(2,1)S(1)} %pad_maximum_fusion.1), channel_id=1, source_target_pairs={{0,8},{4,12},{8,16},{12,20},{16,24},{20,28},{24,32},{28,36},{32,40... | collective-permute-start | bytes 1572872 | tf_op jit(solution)/shard_map/ppermute | solution.py:19
  106.0 18.6 %copy-start.7 = (f32[2,1,8,512]{3,2,1,0:T(8,128)S(1)}, f32[2,1,8,512]{3,2,1,0:T(8,128)}, u32[]{:S(2)}) copy-start(f32[2,1,8,512]{3,2,1,0:T(8,128)} %get-tuple-element.49) | copy-start | bytes 98308
  106.0 18.6 %copy-start.8 = (f32[2,1,8,512]{3,2,1,0:T(8,128)S(1)}, f32[2,1,8,512]{3,2,1,0:T(8,128)}, u32[]{:S(2)}) copy-start(f32[2,1,8,512]{3,2,1,0:T(8,128)} %get-tuple-element.50) | copy-start | bytes 98308
  106.0 18.6 %copy-start.9 = (f32[2,1,8,512]{3,2,1,0:T(8,128)S(1)}, f32[2,1,8,512]{3,2,1,0:T(8,128)}, u32[]{:S(2)}) copy-start(f32[2,1,8,512]{3,2,1,0:T(8,128)} %get-tuple-element.51) | copy-start | bytes 98308
  106.0 18.6 %collective-permute-start.4 = (bf16[16,2,64,2,128]{4,3,2,1,0:T(2,128)(2,1)}, bf16[16,2,64,2,128]{4,3,2,1,0:T(2,128)(2,1)S(1)}, u32[]{:S(2)}, u32[]{:S(2)}) collective-permute-start(bf16[16,2,64,2,128]{4,3,2,1,0:T(2,128)(2,1)} %get-tuple-element.74), channel_id=1, source_target_pairs={{0,4},{4,8},{8,12},{12,16},{16,20},{20,24},{24,28},{28,32},{32,36}... | collective-permute-start | bytes 3145736 | tf_op jit(solution)/shard_map/ppermute | solution.py:19
  115.5 11.8 %copy-start.3 = (bf16[32,2,16,128]{3,2,1,0:T(8,128)(2,1)S(1)}, bf16[32,2,16,128]{3,2,1,0:T(8,128)(2,1)}, u32[]{:S(2)}) copy-start(bf16[32,2,16,128]{3,2,1,0:T(8,128)(2,1)} %get-tuple-element.36) | copy-start | bytes 786436
  115.5 11.8 %copy-start.4 = (bf16[32,2,16,128]{3,2,1,0:T(8,128)(2,1)S(1)}, bf16[32,2,16,128]{3,2,1,0:T(8,128)(2,1)}, u32[]{:S(2)}) copy-start(bf16[32,2,16,128]{3,2,1,0:T(8,128)(2,1)} %get-tuple-element.40) | copy-start | bytes 786436
  115.5 11.8 %copy-start.5 = (bf16[32,2,16,128]{3,2,1,0:T(8,128)(2,1)S(1)}, bf16[32,2,16,128]{3,2,1,0:T(8,128)(2,1)}, u32[]{:S(2)}) copy-start(bf16[32,2,16,128]{3,2,1,0:T(8,128)(2,1)} %get-tuple-element.44) | copy-start | bytes 786436
  115.5 11.8 %copy-start.6 = (bf16[32,2,16,128]{3,2,1,0:T(8,128)(2,1)S(1)}, bf16[32,2,16,128]{3,2,1,0:T(8,128)(2,1)}, u32[]{:S(2)}) copy-start(bf16[32,2,16,128]{3,2,1,0:T(8,128)(2,1)} %get-tuple-element.48) | copy-start | bytes 786436
  129.9 44.9 %all-to-all-start.1 = ((bf16[128,2,2112]{2,1,0:T(2,128)(2,1)}), bf16[128,2,2112]{2,1,0:T(2,128)(2,1)S(1)}, u32[]{:S(2)}, u32[]{:S(2)}) async-start(bf16[128,2,2112]{2,1,0:T(2,128)(2,1)} %fusion), calls=%async_computation.1 | async-start | bytes 2228224 | tf_op jit(solution)/shard_map/all_to_all | solution.py:184
  178.7 1.0 copy-start.2

commit v13 on v11

--- a/solution.py
+++ b/solution.py
@@ -154,7 +154,7 @@
     served_lse = jnp.concatenate([piece[1] for piece in served_pieces], axis=1)[:, :, 0]
     served_lse = served_lse.reshape(kv_heads, seq_count, slab)
     served_lse = jnp.swapaxes(served_lse, 0, 1)
-    served, served_lse, window = lax.optimization_barrier((served, served_lse, window))
+    served, served_lse = lax.optimization_barrier((served, served_lse))
     lse_rounded = lax.reduce_precision(served_lse, exponent_bits=8, mantissa_bits=7)
     lse_rest = served_lse - lse_rounded
     lse_middle = lax.reduce_precision(lse_rest, exponent_bits=8, mantissa_bits=7)

time: 192 us -> 192 us (level)
  other arithmetic: 9.28 us -> 11.3 us
    unnamed x30 -> x36, local copies, waits for them, and re-layouts: 7.92 us -> 7.46 us
  transfers between devices with their start and end apart: 7 -> 7, of which waited for: 6 -> 6; matrix products, arithmetic and copies ran while one was open for 9% -> 10% of each run, Pallas kernels for 20% -> 20%
where the time goes in v13:
time: 192 us; the launch traced here: 191 us
  waiting for transfers between devices  59.6 us (31%)
  starting transfers between devices  43.5 us (23%)
  Pallas kernels  38.1 us (20%)
  local copies, waits for them, and re-layouts  26 us (14%)
  other arithmetic  11.3 us (6%)
  blocking collectives  10.8 us (6%)
    pallas_call x5, Pallas kernels, attend(): pl.pallas_call(functools.partial(attend_kernel, thr is not None, scaling,...  38.1 us
    all_to_all x1, waiting for transfers between devices, per_device(): lax.all_to_all(outgoing, 'seq', split_axis=0, concat_axis=0, tiled=True)  28.6 us
    all_to_all x1, starting transfers between devices, per_device(): lax.all_to_all(outgoing, 'seq', split_axis=0, concat_axis=0, tiled=True)  17.4 us
    ppermute x5, waiting for transfers between devices, shifted(): lax.ppermute(value, axis, [(source, source + steps) for source in range(i...  16.3 us
    all_to_all x1, waiting for transfers between devices, per_device(): lax.all_to_all(payload, 'seq', split_axis=0, concat_axis=0, tiled=True)  14.8 us
    ppermute x5, starting transfers between devices, shifted(): lax.ppermute(value, axis, [(source, source + steps) for source in range(i...  13.8 us
    all_to_all x1, starting transfers between devices, per_device(): lax.all_to_all(payload, 'seq', split_axis=0, concat_axis=0, tiled=True)  12.3 us
    all_to_all x1, blocking collectives, per_device(): lax.all_to_all(heads_out, 'kvh', split_axis=0, concat_axis=1, tiled=True)  10.8 us
  transfers between devices with their start and end apart: 7, of which 6 were waited for; matrix products, arithmetic and copies ran while one was open for 10% of the time, Pallas kernels for 20%

profile of v13, /device:TPU:8, one launch (start us, length us, event | category | flops | bytes accessed | tf_op | source)
XLA Modules:
  0.0 191.1 jit_solution(5866995726114227054)
XLA Ops:
  0.0 0.7 copy.111
  0.7 0.9 select_reduce_fusion
  1.7 0.1 copy.112
  1.8 0.1 reshape.197
  1.9 0.1 iota_compare_fusion
  2.1 0.2 fusion.9
  2.5 0.2 fusion.13
  2.8 0.8 copy_bitcast_fusion.3
  3.7 0.6 fusion
  4.3 1.7 copy.164
  5.9 17.4 %all-to-all-start = ((bf16[128,2,16,128]{3,2,1,0:T(8,128)(2,1)}), bf16[128,2,16,128]{3,2,1,0:T(8,128)(2,1)S(1)}, u32[]{:S(2)}, u32[]{:S(2)}) async-start(bf16[128,2,16,128]{3,2,1,0:T(8,128)(2,1)} %bitcast.86), calls=%async_computation | async-start | bytes 2097152 | tf_op jit(solution)/shard_map/all_to_all | solution.py:126
  23.3 2.7 %fusion.26 = (bf16[1,1,2048,2,128]{4,3,2,1,0:T(2,128)(2,1)S(1)}, bf16[1,1,2048,2,128]{4,3,2,1,0:T(2,128)(2,1)S(1)}) fusion(bf16[2,1,2048,2,128]{4,3,2,1,0:T(2,128)(2,1)} %param.8), kind=kLoop, calls=%fused_computation.119 | loop fusion | bytes 4194304 | tf_op jit(solution)/shard_map/slice | solution.py:129
  26.1 28.6 %all-to-all-done = bf16[128,2,16,128]{3,2,1,0:T(8,128)(2,1)S(1)} async-done(((bf16[128,2,16,128]{3,2,1,0:T(8,128)(2,1)}), bf16[128,2,16,128]{3,2,1,0:T(8,128)(2,1)S(1)}, u32[]{:S(2)}, u32[]{:S(2)}) %all-to-all-start) | async-done | bytes 1048608 | tf_op jit(solution)/shard_map/all_to_all | solution.py:126
  54.6 3.3 %collective-permute-start = (bf16[1,2,64,2,128]{4,3,2,1,0:T(2,128)(2,1)S(1)}, bf16[1,2,64,2,128]{4,3,2,1,0:T(2,128)(2,1)S(1)}, u32[]{:S(2)}, u32[]{:S(2)}) collective-permute-start(bf16[1,2,64,2,128]{4,3,2,1,0:T(2,128)(2,1)S(1)} %bitcast.97), channel_id=1, source_target_pairs={{0,32},{4,36},{8,40},{12,44},{16,48},{20,52},{24,56},{28,60},{32,6... | collective-permute-start | bytes 196616 | tf_op jit(solution)/shard_map/ppermute | solution.py:19
  58.0 1.6 copy_bitcast_fusion
  59.5 6.1 %collective-permute-done = bf16[1,2,64,2,128]{4,3,2,1,0:T(2,128)(2,1)S(1)} collective-permute-done((bf16[1,2,64,2,128]{4,3,2,1,0:T(2,128)(2,1)S(1)}, bf16[1,2,64,2,128]{4,3,2,1,0:T(2,128)(2,1)S(1)}, u32[]{:S(2)}, u32[]{:S(2)}) %collective-permute-start) | collective-permute-done | bytes 65568 | tf_op jit(solution)/shard_map/ppermute | solution.py:19
  65.7 0.2 pad_maximum_fusion.3
  65.9 2.4 %collective-permute-start.1 = (bf16[2,2,64,2,128]{4,3,2,1,0:T(2,128)(2,1)S(1)}, bf16[2,2,64,2,128]{4,3,2,1,0:T(2,128)(2,1)S(1)}, u32[]{:S(2)}, u32[]{:S(2)}) collective-permute-start(bf16[2,2,64,2,128]{4,3,2,1,0:T(2,128)(2,1)S(1)} %pad_maximum_fusion.3), channel_id=1, source_target_pairs={{0,16},{4,20},{8,24},{12,28},{16,32},{20,36},{24,40},{28,44},{32,4... | collective-permute-start | bytes 393224 | tf_op jit(solution)/shard_map/ppermute | solution.py:19
  68.2 1.0 fusion.27
  69.3 7.5 %shard_map.64 = (bf16[32,2,16,128]{3,2,1,0:T(8,128)(2,1)}, f32[2,1,8,512]{3,2,1,0:T(8,128)}) custom-call(bf16[32,2,16,128]{3,2,1,0:T(8,128)(2,1)} %get-tuple-element.70.refs_0_, bf16[2,2048,128]{2,1,0:T(8,128)(2,1)} %get-tuple-element.87.refs_1_, bf16[2,2048,128]{2,1,0:T(8,128)(2,1)} %get-tuple-element.86.refs_2_), custom_call_target="tpu_custom_call" | custom-call | flops 1073741824 | bytes 2621440 | tf_op jit(solution)/shard_map/pallas_call | solution.py:78
  76.7 0.3 collective-permute-done.1
  77.0 0.4 pad_maximum_fusion.2
  77.4 2.5 %collective-permute-start.2 = (bf16[4,2,64,2,128]{4,3,2,1,0:T(2,128)(2,1)S(1)}, bf16[4,2,64,2,128]{4,3,2,1,0:T(2,128)(2,1)S(1)}, u32[]{:S(2)}, u32[]{:S(2)}) collective-permute-start(bf16[4,2,64,2,128]{4,3,2,1,0:T(2,128)(2,1)S(1)} %pad_maximum_fusion.2), channel_id=1, source_target_pairs={{0,64},{4,68},{8,72},{12,76},{16,80},{20,84},{24,88},{28,92},{32,9... | collective-permute-start | bytes 786440 | tf_op jit(solution)/shard_map/ppermute | solution.py:19
  79.9 7.5 %shard_map.65 = (bf16[32,2,16,128]{3,2,1,0:T(8,128)(2,1)}, f32[2,1,8,512]{3,2,1,0:T(8,128)}) custom-call(bf16[32,2,16,128]{3,2,1,0:T(8,128)(2,1)} %get-tuple-element.69.refs_0_, bf16[2,2048,128]{2,1,0:T(8,128)(2,1)} %get-tuple-element.87.refs_1_, bf16[2,2048,128]{2,1,0:T(8,128)(2,1)} %get-tuple-element.86.refs_2_), custom_call_target="tpu_custom_call" | custom-call | flops 1073741824 | bytes 2621440 | tf_op jit(solution)/shard_map/pallas_call | solution.py:78
  87.4 1.5 pad_maximum_fusion.1
  88.9 3.6 %collective-permute-start.3 = (bf16[8,2,64,2,128]{4,3,2,1,0:T(2,128)(2,1)}, bf16[8,2,64,2,128]{4,3,2,1,0:T(2,128)(2,1)S(1)}, u32[]{:S(2)}, u32[]{:S(2)}) collective-permute-start(bf16[8,2,64,2,128]{4,3,2,1,0:T(2,128)(2,1)} %pad_maximum_fusion.1), channel_id=1, source_target_pairs={{0,8},{4,12},{8,16},{12,20},{16,24},{20,28},{24,32},{28,36},{32,40... | collective-permute-start | bytes 1572872 | tf_op jit(solution)/shard_map/ppermute | solution.py:19
  92.5 0.7 constant_dynamic-update-slice_fusion.10
  93.2 7.5 %shard_map.66 = (bf16[32,2,16,128]{3,2,1,0:T(8,128)(2,1)}, f32[2,1,8,512]{3,2,1,0:T(8,128)}) custom-call(bf16[32,2,16,128]{3,2,1,0:T(8,128)(2,1)} %get-tuple-element.68.refs_0_, bf16[2,2048,128]{2,1,0:T(8,128)(2,1)} %get-tuple-element.87.refs_1_, bf16[2,2048,128]{2,1,0:T(8,128)(2,1)} %get-tuple-element.86.refs_2_), custom_call_target="tpu_custom_call" | custom-call | flops 1073741824 | bytes 2621440 | tf_op jit(solution)/shard_map/pallas_call | solution.py:78
  100.7 0.7 constant_dynamic-update-slice_fusion.9
  101.4 0.8 constant_dynamic-update-slice_fusion.8
  102.2 1.1 constant_dynamic-update-slice_fusion.7
  103.3 0.8 collective-permute-done.3
  104.2 1.8 constant_dynamic-update-slice_fusion.6
  106.0 2.1 %collective-permute-start.4 = (bf16[16,2,64,2,128]{4,3,2,1,0:T(2,128)(2,1)}, bf16[16,2,64,2,128]{4,3,2,1,0:T(2,128)(2,1)S(1)}, u32[]{:S(2)}, u32[]{:S(2)}) collective-permute-start(bf16[16,2,64,2,128]{4,3,2,1,0:T(2,128)(2,1)} %get-tuple-element.72), channel_id=1, source_target_pairs={{0,4},{4,8},{8,12},{12,16},{16,20},{20,24},{24,28},{28,32},{32,36}... | collective-permute-start | bytes 3145736 | tf_op jit(solution)/shard_map/ppermute | solution.py:19
  108.1 7.5 %shard_map.67 = (bf16[32,2,16,128]{3,2,1,0:T(8,128)(2,1)}, f32[2,1,8,512]{3,2,1,0:T(8,128)}) custom-call(bf16[32,2,16,128]{3,2,1,0:T(8,128)(2,1)} %get-tuple-element.67.refs_0_, bf16[2,2048,128]{2,1,0:T(8,128)(2,1)} %get-tuple-element.87.refs_1_, bf16[2,2048,128]{2,1,0:T(8,128)(2,1)} %get-tuple-element.86.refs_2_), custom_call_target="tpu_custom_call" | custom-call | flops 1073741824 | bytes 2621440 | tf_op jit(solution)/shard_map/pallas_call | solution.py:78
  115.6 9.0 %collective-permute-done.4 = bf16[16,2,64,2,128]{4,3,2,1,0:T(2,128)(2,1)S(1)} collective-permute-done((bf16[16,2,64,2,128]{4,3,2,1,0:T(2,128)(2,1)}, bf16[16,2,64,2,128]{4,3,2,1,0:T(2,128)(2,1)S(1)}, u32[]{:S(2)}, u32[]{:S(2)}) %collective-permute-start.4) | collective-permute-done | bytes 1048608 | tf_op jit(solution)/shard_map/ppermute | solution.py:19
  124.6 0.9 fusion.23
  125.6 1.3 pad_maximum_fusion
  126.9 0.3 reshape.204
  127.2 0.1 pad_maximum_fusion.4
  127.4 1.9 fusion.1
  129.3 12.3 %all-to-all-start.1 = ((bf16[128,2,2112]{2,1,0:T(2,128)(2,1)}), bf16[128,2,2112]{2,1,0:T(2,128)(2,1)S(1)}, u32[]{:S(2)}, u32[]{:S(2)}) async-start(bf16[128,2,2112]{2,1,0:T(2,128)(2,1)} %fusion.1), calls=%async_computation.1 | async-start | bytes 2228224 | tf_op jit(solution)/shard_map/all_to_all | solution.py:177
  142.8 0.3 compare_reduce_fusion
  143.1 0.6 reshape_select_fusion.1.refs_0_
  143.7 2.5 %constant_dynamic-update-slice_fusion.5 = bf16[32,2,64,2,128]{4,3,2,1,0:T(2,128)(2,1)S(1)} fusion(bf16[32,2,64,2,128]{4,3,2,1,0:T(2,128)(2,1)S(1)} %copy-done.2, bf16[16,2,64,2,128]{4,3,2,1,0:T(2,128)(2,1)} %copy-done.3), kind=kLoop, calls=%fused_computation.94 | loop fusion | bytes 2097152 | tf_op jit(solution)/shard_map/concatenate | solution.py:33
  146.3 1.7 slice_bitcast_fusion
  148.0 1.3 copy.120
  149.3 1.3 copy.119
  150.6 8.1 %shard_map.68 = (f32[2,512,128]{2,1,0:T(8,128)}, f32[2,1,8,512]{3,2,1,0:T(8,128)}) custom-call(s32[1,2048]{1,0:T(1,128)} %reshape_select_fusion.1.refs_0_, bf16[2,512,128]{2,1,0:T(8,128)(2,1)} %get-tuple-element.75.refs_1_, bf16[2,2048,128]{2,1,0:T(8,128)(2,1)} %bitcast.94, bf16[2,2048,128]{2,1,0:T(8,128)(2,1)} %bitcast.93), custom_call_target="tpu_custom_call" | custom-call | flops 1073741824 | bytes 2621440 | tf_op jit(solution)/shard_map/pallas_call | solution.py:78
  158.6 0.8 slice_reduce_fusion
  159.6 14.8 %all-to-all-done.1 = bf16[128,2,2112]{2,1,0:T(2,128)(2,1)S(1)} async-done(((bf16[128,2,2112]{2,1,0:T(2,128)(2,1)}), bf16[128,2,2112]{2,1,0:T(2,128)(2,1)S(1)}, u32[]{:S(2)}, u32[]{:S(2)}) %all-to-all-start.1) | async-done | bytes 1081376 | tf_op jit(solution)/shard_map/all_to_all | solution.py:177
  174.5 0.7 slice.114
  175.2 1.0 copy.147
  176.3 0.2 convolution_bitcast_fusion
  176.6 0.2 copy.124
  176.7 0.1 reduce_max.9
  177.0 0.5 fusion.3
  177.5 0.3 copy.150
  177.9 0.2 fusion.25
  178.5 0.5 multiply_reduce_fusion
  179.1 0.4 fusion.11
  179.5 0.1 all_to_all.22
  179.6 10.8 %all_to_all.29 = bf16[4,16,2048]{2,1,0:T(8,128)(2,1)S(1)} all-to-all(bf16[4,16,2048]{2,1,0:T(8,128)(2,1)S(1)} %all_to_all.22), channel_id=1, replica_groups=mesh['seq'=128,'kvh'=4] {'kvh'}, dimensions={0} | all-to-all | bytes 524288 | tf_op jit(solution)/shard_map/all_to_all | solution.py:241
  190.4 0.7 copy.149
  (80 shorter events, 2.6 us)
Async XLA Ops:
  0.0 2.8 %copy-start = (bf16[64,16,128]{2,1,0:T(8,128)(2,1)S(1)}, bf16[64,16,128]{2,1,0:T(8,128)(2,1)}, u32[]{:S(2)}) copy-start(bf16[64,16,128]{2,1,0:T(8,128)(2,1)} %param.6) | copy-start | bytes 786436
  0.0 4.3 %copy-start.11 = (s32[128,2]{0,1:T(2,128)}, s32[128,2]{0,1:T(2,128)S(1)}, u32[]{:S(2)}) copy-start(s32[128,2]{0,1:T(2,128)S(1)} %multiply_add_fusion.1) | copy-start | bytes 3076
  2.8 3.2 %copy-start.9 = (s32[2,192]{1,0:T(2,128)}, s32[2,192]{1,0:T(2,128)S(1)}, u32[]{:S(2)}) copy-start(s32[2,192]{1,0:T(2,128)S(1)} %multiply_add_fusion) | copy-start | bytes 4612
  5.9 48.7 %all-to-all-start = ((bf16[128,2,16,128]{3,2,1,0:T(8,128)(2,1)}), bf16[128,2,16,128]{3,2,1,0:T(8,128)(2,1)S(1)}, u32[]{:S(2)}, u32[]{:S(2)}) async-start(bf16[128,2,16,128]{3,2,1,0:T(8,128)(2,1)} %bitcast.86), calls=%async_computation | async-start | bytes 2097152 | tf_op jit(solution)/shard_map/all_to_all | solution.py:126
  23.3 31.3 %copy-start.4 = (bf16[2,64,2,128]{3,2,1,0:T(2,128)(2,1)S(1)}, bf16[2,64,2,128]{3,2,1,0:T(2,128)(2,1)}, u32[]{:S(2)}) copy-start(bf16[2,64,2,128]{3,2,1,0:T(2,128)(2,1)} %param.7) | copy-start | bytes 196612
  54.6 11.0 %collective-permute-start = (bf16[1,2,64,2,128]{4,3,2,1,0:T(2,128)(2,1)S(1)}, bf16[1,2,64,2,128]{4,3,2,1,0:T(2,128)(2,1)S(1)}, u32[]{:S(2)}, u32[]{:S(2)}) collective-permute-start(bf16[1,2,64,2,128]{4,3,2,1,0:T(2,128)(2,1)S(1)} %bitcast.97), channel_id=1, source_target_pairs={{0,32},{4,36},{8,40},{12,44},{16,48},{20,52},{24,56},{28,60},{32,6... | collective-permute-start | bytes 196616 | tf_op jit(solution)/shard_map/ppermute | solution.py:19
  65.9 11.1 %collective-permute-start.1 = (bf16[2,2,64,2,128]{4,3,2,1,0:T(2,128)(2,1)S(1)}, bf16[2,2,64,2,128]{4,3,2,1,0:T(2,128)(2,1)S(1)}, u32[]{:S(2)}, u32[]{:S(2)}) collective-permute-start(bf16[2,2,64,2,128]{4,3,2,1,0:T(2,128)(2,1)S(1)} %pad_maximum_fusion.3), channel_id=1, source_target_pairs={{0,16},{4,20},{8,24},{12,28},{16,32},{20,36},{24,40},{28,44},{32,4... | collective-permute-start | bytes 393224 | tf_op jit(solution)/shard_map/ppermute | solution.py:19
  77.4 10.0 %collective-permute-start.2 = (bf16[4,2,64,2,128]{4,3,2,1,0:T(2,128)(2,1)S(1)}, bf16[4,2,64,2,128]{4,3,2,1,0:T(2,128)(2,1)S(1)}, u32[]{:S(2)}, u32[]{:S(2)}) collective-permute-start(bf16[4,2,64,2,128]{4,3,2,1,0:T(2,128)(2,1)S(1)} %pad_maximum_fusion.2), channel_id=1, source_target_pairs={{0,64},{4,68},{8,72},{12,76},{16,80},{20,84},{24,88},{28,92},{32,9... | collective-permute-start | bytes 786440 | tf_op jit(solution)/shard_map/ppermute | solution.py:19
  88.9 15.2 %collective-permute-start.3 = (bf16[8,2,64,2,128]{4,3,2,1,0:T(2,128)(2,1)}, bf16[8,2,64,2,128]{4,3,2,1,0:T(2,128)(2,1)S(1)}, u32[]{:S(2)}, u32[]{:S(2)}) collective-permute-start(bf16[8,2,64,2,128]{4,3,2,1,0:T(2,128)(2,1)} %pad_maximum_fusion.1), channel_id=1, source_target_pairs={{0,8},{4,12},{8,16},{12,20},{16,24},{20,28},{24,32},{28,36},{32,40... | collective-permute-start | bytes 1572872 | tf_op jit(solution)/shard_map/ppermute | solution.py:19
  106.0 19.5 %copy-start.1 = (bf16[32,2,64,2,128]{4,3,2,1,0:T(2,128)(2,1)}, bf16[32,2,64,2,128]{4,3,2,1,0:T(2,128)(2,1)S(1)}, u32[]{:S(2)}) copy-start(bf16[32,2,64,2,128]{4,3,2,1,0:T(2,128)(2,1)S(1)} %get-tuple-element.71) | copy-start | bytes 6291460
  106.0 18.6 %copy-start.6 = (f32[2,1,8,512]{3,2,1,0:T(8,128)S(1)}, f32[2,1,8,512]{3,2,1,0:T(8,128)}, u32[]{:S(2)}) copy-start(f32[2,1,8,512]{3,2,1,0:T(8,128)} %get-tuple-element.50) | copy-start | bytes 98308
  106.0 18.6 %copy-start.7 = (f32[2,1,8,512]{3,2,1,0:T(8,128)S(1)}, f32[2,1,8,512]{3,2,1,0:T(8,128)}, u32[]{:S(2)}) copy-start(f32[2,1,8,512]{3,2,1,0:T(8,128)} %get-tuple-element.51) | copy-start | bytes 98308
  106.0 18.6 %copy-start.8 = (f32[2,1,8,512]{3,2,1,0:T(8,128)S(1)}, f32[2,1,8,512]{3,2,1,0:T(8,128)}, u32[]{:S(2)}) copy-start(f32[2,1,8,512]{3,2,1,0:T(8,128)} %get-tuple-element.52) | copy-start | bytes 98308
  106.0 18.6 %collective-permute-start.4 = (bf16[16,2,64,2,128]{4,3,2,1,0:T(2,128)(2,1)}, bf16[16,2,64,2,128]{4,3,2,1,0:T(2,128)(2,1)S(1)}, u32[]{:S(2)}, u32[]{:S(2)}) collective-permute-start(bf16[16,2,64,2,128]{4,3,2,1,0:T(2,128)(2,1)} %get-tuple-element.72), channel_id=1, source_target_pairs={{0,4},{4,8},{8,12},{12,16},{16,20},{20,24},{24,28},{28,32},{32,36}... | collective-permute-start | bytes 3145736 | tf_op jit(solution)/shard_map/ppermute | solution.py:19
  124.6 2.6 %copy-start.3 = (bf16[16,2,64,2,128]{4,3,2,1,0:T(2,128)(2,1)}, bf16[16,2,64,2,128]{4,3,2,1,0:T(2,128)(2,1)S(1)}, u32[]{:S(2)}) copy-start(bf16[16,2,64,2,128]{4,3,2,1,0:T(2,128)(2,1)S(1)} %collective-permute-done.4) | copy-start | bytes 3145732
  127.4 16.3 %copy-start.2 = (bf16[32,2,64,2,128]{4,3,2,1,0:T(2,128)(2,1)S(1)}, bf16[32,2,64,2,128]{4,3,2,1,0:T(2,128)(2,1)}, u32[]{:S(2)}) copy-start(bf16[32,2,64,2,128]{4,3,2,1,0:T(2,128)(2,1)} %copy-done.1) | copy-start | bytes 6291460
  129.3 45.0 %all-to-all-start.1 = ((bf16[128,2,2112]{2,1,0:T(2,128)(2,1)}), bf16[128,2,2112]{2,1,0:T(2,128)(2,1)S(1)}, u32[]{:S(2)}, u32[]{:S(2)}) async-start(bf16[128,2,2112]{2,1,0:T(2,128)(2,1)} %fusion.1), calls=%async_computation.1 | async-start | bytes 2228224 | tf_op jit(solution)/shard_map/all_to_all | solution.py:177
  174.5 1.8 copy-start.10
  174.5 1.8 copy-start.12
  177.8 1.2 copy-start.5
